TPU v7x, 512 devices: a whole 4x8x8 slice. The times are simulated.
512 devices in a mesh: row: 32 (over z, y_lo), col: 16 (over y_hi, x, core).
Axes of the slice: x: 4, y: 8 (y_hi: 2, y_lo: 4; y = y_hi * 4 + y_lo), z: 8, core: 2. Of those that a mesh axis runs over, the one named last changes fastest.
Arguments:
- group_store: bfloat16 [512, 32, 1600], P('row'), may hold values from -6 to 6
- positions: bfloat16 [320, 1600], replicated, may hold values from -6 to 6
- ln_gain: bfloat16 [1600], replicated, may hold values from 0.099609375 to 1.8984375
- w_query: bfloat16 [1600, 1600], P('row', 'col'), may hold values from -6 to 6
- w_keyval: bfloat16 [1600, 2, 1600], P('row', None, 'col'), may hold values from -6 to 6
- w_out: bfloat16 [1600, 1600], P('col', 'row'), may hold values from -0.3125 to 0.3125
- group_src: int32 [128, 10], replicated, may hold values from 0 to 511, as said below
- lengths: int32 [32, 4], replicated, may hold values from 1 to 10, as said below
- selected: int32 [128, 32], replicated, may hold values from 0 to 319, as said below
Outputs:
- joined_cache: bfloat16 [128, 320, 2, 1600], P('row', None, None, 'col')
- hidden_out: bfloat16 [128, 32, 1600], P('row', None, 'col')
Inputs may be any that keep to these rules, and one draw needn't show every extreme that they name: `group_src`: exactly 32 of the 40 entries of the requests of one row device name a group held by another device, and at most 2 of them name any one other device; some device reaches 2 in every draw. `lengths`: every row device has a request with all 10 groups live. `selected`: each row holds 32 distinct places in increasing order, all below 32 times the request's live groups.
All inputs are finite; a program needn't handle non-finite values.
Results may differ from a plain program's by a relative error of at most 0.015.
Values may be sent and summed in bfloat16 or wider, within the bound.
No kernel may reach another device: no remote copies, remote signals or barrier semaphores. Data moves between devices by JAX's collectives and lax.ppermute only.
A program may use at most 64 MiB of HBM per device.

v0:
```python
import jax
import jax.numpy as jnp
from jax import lax
from jax.sharding import PartitionSpec as P

HEADS = 25
HEAD_DIM = 64
REM_DEV = 32
TOKEN_SPLIT = 4
HIGH = lax.Precision.HIGHEST


def layer_norm(shifted, ln_gain):
    center = shifted - jnp.mean(shifted, axis=-1, keepdims=True)
    spread = jnp.mean(center * center, axis=-1, keepdims=True)
    return center * lax.rsqrt(spread + 1e-05) * ln_gain.astype(jnp.float32)


def split_weights(allw, w_query, w_keyval, w_out, row_count):
    q_rows, q_cols = w_query.shape
    o_rows, o_cols = w_out.shape
    q_size = w_query.size
    kv_size = w_keyval.size
    query_rows = allw[:, :q_size].reshape(row_count * q_rows, q_cols)
    keyval_rows = allw[:, q_size:q_size + kv_size].reshape(row_count * q_rows, 2, q_cols)
    out_cols = (
        allw[:, q_size + kv_size:]
        .reshape(row_count, o_rows, o_cols)
        .transpose(1, 0, 2)
        .reshape(o_rows, row_count * o_cols)
    )
    return query_rows, keyval_rows, out_cols


def fetch_groups(group_store, group_src, row_count, row_index, col_count, col_index, req_here, extra):
    slot_count, group_len, full_width = group_store.shape
    group_count = group_src.shape[1]
    ref_count = req_here * group_count
    local_count = ref_count - REM_DEV
    capacity = max(2, (REM_DEV + row_count - 2) // (row_count - 1))
    owner_src = group_src.reshape(row_count, ref_count)
    holder_all = owner_src // slot_count
    slot_all = owner_src % slot_count
    owner_ids = jnp.arange(row_count, dtype=jnp.int32)
    remote_all = holder_all != owner_ids[:, None]
    outgoing = remote_all & (holder_all == row_index)
    out_rank = jnp.cumsum(outgoing.astype(jnp.int32), axis=1) - 1
    slot_ids = jnp.arange(capacity, dtype=jnp.int32)
    chosen = outgoing[:, None, :] & (out_rank[:, None, :] == slot_ids[None, :, None])
    send_slot = jnp.sum(jnp.where(chosen, slot_all[:, None, :], 0), axis=2)
    send_live = jnp.any(chosen, axis=2)
    my_holder = lax.dynamic_index_in_dim(holder_all, row_index, 0, keepdims=False)
    my_slot = lax.dynamic_index_in_dim(slot_all, row_index, 0, keepdims=False)
    my_remote = lax.dynamic_index_in_dim(remote_all, row_index, 0, keepdims=False)
    incoming = (my_holder[None, :] == owner_ids[:, None]) & my_remote[None, :]
    in_rank = jnp.cumsum(incoming.astype(jnp.int32), axis=1) - 1
    my_rank = jnp.sum(jnp.where(incoming, in_rank, 0), axis=0)
    flat_index = my_holder * capacity + my_rank
    ordinal = jnp.cumsum(my_remote.astype(jnp.int32)) - 1
    compact_ids = jnp.arange(REM_DEV, dtype=jnp.int32)
    compact_pick = my_remote[None, :] & (ordinal[None, :] == compact_ids[:, None])
    compact_index = jnp.sum(jnp.where(compact_pick, flat_index[None, :], 0), axis=1)
    compact_ref = jnp.sum(jnp.where(compact_pick, jnp.arange(ref_count)[None, :], 0), axis=1)
    local_ordinal = jnp.cumsum((~my_remote).astype(jnp.int32)) - 1
    local_ids = jnp.arange(local_count, dtype=jnp.int32)
    local_pick = (~my_remote)[None, :] & (local_ordinal[None, :] == local_ids[:, None])
    local_ref = jnp.sum(jnp.where(local_pick, jnp.arange(ref_count)[None, :], 0), axis=1)
    local_slot = jnp.sum(jnp.where(local_pick, my_slot[None, :], 0), axis=1)

    split = TOKEN_SPLIT
    if col_count % split or group_len % split:
        split = 1
    part = group_len // split
    own_part = col_index % split
    store_rows = group_store.reshape(slot_count * group_len, full_width)
    tok_ids = jnp.arange(part, dtype=jnp.int32)
    send_rows = send_slot[:, :, None] * group_len + own_part * part + tok_ids
    payload = store_rows[send_rows.reshape(-1)].reshape(row_count, capacity * part, full_width)
    live_rows = jnp.repeat(send_live, part, axis=1)
    extra_rows = -(-extra.shape[0] // full_width)
    extra_pad = jnp.pad(extra, (0, extra_rows * full_width - extra.shape[0])).reshape(extra_rows, full_width)
    sent = jnp.concatenate(
        [
            jnp.where(live_rows[:, :, None], payload, jnp.zeros_like(payload)),
            jnp.broadcast_to(extra_pad[None], (row_count, extra_rows, full_width)),
        ],
        axis=1,
    )
    received = lax.all_to_all(sent, "row", split_axis=0, concat_axis=0, tiled=True)
    extra_all = received[:, capacity * part:].reshape(row_count, -1)[:, : extra.shape[0]]
    flat = received[:, : capacity * part].reshape(row_count * capacity * part, full_width)
    compact = flat[(compact_index[:, None] * part + tok_ids).reshape(-1)]
    pieces = [compact] + [
        lax.ppermute(compact, "col", [(c, c ^ m) for c in range(col_count)]) for m in range(1, split)
    ]
    near_rows = (local_slot[:, None] * group_len + jnp.arange(group_len, dtype=jnp.int32)).reshape(-1)
    near = store_rows[near_rows]
    blocks = [near]
    refs = [jnp.repeat(local_ref, group_len)]
    toks = [jnp.tile(jnp.arange(group_len, dtype=jnp.int32), local_count)]
    for m in range(split):
        blocks.append(pieces[m])
        refs.append(jnp.repeat(compact_ref, part))
        toks.append(jnp.tile((own_part ^ m) * part + tok_ids, REM_DEV))
    tok_all = jnp.arange(group_len, dtype=jnp.int32)[None, :]
    remote_row = local_count * group_len + (
        ((tok_all // part) ^ own_part) * REM_DEV * part + ordinal[:, None] * part + tok_all % part
    )
    near_row = local_ordinal[:, None] * group_len + tok_all
    row_of = jnp.where(my_remote[:, None], remote_row, near_row)
    return blocks, refs, toks, row_of.reshape(-1), extra_all


def per_device(
    group_store, positions, ln_gain, w_query, w_keyval, w_out, group_src, lengths, selected
):
    row_count = lax.axis_size("row")
    col_count = lax.axis_size("col")
    row_index = lax.axis_index("row")
    col_index = lax.axis_index("col")
    slot_count, group_len, full_width = group_store.shape
    narrow = full_width // col_count
    req_here = lengths.shape[1]
    group_count = group_src.shape[1]
    token_span = group_count * group_len
    sel_count = selected.shape[1]
    query_count = req_here * sel_count
    first_feature = col_index * narrow

    pack = jnp.concatenate([w_query.reshape(-1), w_keyval.reshape(-1), w_out.reshape(-1)])
    blocks, refs, toks, row_of, allw = fetch_groups(
        group_store, group_src, row_count, row_index, col_count, col_index, req_here, pack
    )
    query_rows, keyval_rows, out_cols = split_weights(allw, w_query, w_keyval, w_out, row_count)
    w_cat = jnp.concatenate([keyval_rows.reshape(full_width, 2 * narrow), query_rows], axis=1)

    pos_f = positions.astype(jnp.float32)
    out_kv, out_q, out_sh = [], [], []
    for block, ref, tok in zip(blocks, refs, toks):
        place = (ref % group_count) * group_len + tok
        shifted = block.astype(jnp.float32) + pos_f[place] - pos_f[tok]
        normed = layer_norm(shifted, ln_gain).astype(jnp.bfloat16)
        both = jnp.dot(normed, w_cat, preferred_element_type=jnp.float32).astype(jnp.bfloat16)
        out_kv.append(both[:, : 2 * narrow])
        out_q.append(both[:, 2 * narrow:])
        out_sh.append(lax.dynamic_slice_in_dim(shifted, first_feature, narrow, 1))
    kv_rows = jnp.concatenate(out_kv)
    q_rows = jnp.concatenate(out_q)
    sh_rows = jnp.concatenate(out_sh)

    my_lengths = lax.dynamic_index_in_dim(lengths, row_index, 0, keepdims=False)
    my_picked = lax.dynamic_slice_in_dim(selected, row_index * req_here, req_here, 0)
    token_place = jnp.arange(token_span, dtype=jnp.int32)
    keyval = kv_rows[row_of].reshape(req_here, token_span, 2, narrow)
    alive = token_place[None, :] < (my_lengths * group_len)[:, None]
    joined_cache = jnp.where(alive[:, :, None, None], keyval, jnp.zeros_like(keyval))

    req_ids = jnp.arange(req_here, dtype=jnp.int32)[:, None]
    picked_row = row_of.reshape(req_here, token_span)[req_ids, my_picked]
    queries = q_rows[picked_row]
    picked_shift = sh_rows[picked_row]

    feature_head = (first_feature + jnp.arange(narrow, dtype=jnp.int32)) // HEAD_DIM
    first_head = first_feature // HEAD_DIM
    last_piece = (first_feature + narrow - 1) // HEAD_DIM - first_head
    piece_count = (narrow + 2 * HEAD_DIM - 2) // HEAD_DIM
    query_f = queries.astype(jnp.float32)
    key_f = joined_cache[:, :, 0].astype(jnp.float32)
    value_f = joined_cache[:, :, 1].astype(jnp.float32)
    masks = [feature_head == first_head + p for p in range(piece_count)]
    partial = [
        jnp.einsum(
            "bie,bte->bit", jnp.where(m[None, None, :], query_f, 0.0), key_f, precision=HIGH
        )
        for m in masks
    ]
    right_piece = partial[0]
    for p in range(1, piece_count):
        right_piece = jnp.where(last_piece == p, partial[p], right_piece)
    from_left = lax.ppermute(right_piece, "col", [(i, i + 1) for i in range(col_count - 1)])
    from_right = lax.ppermute(partial[0], "col", [(i + 1, i) for i in range(col_count - 1)])
    allowed = token_place[None, None, :] <= my_picked[:, :, None]
    attended = jnp.zeros((req_here, sel_count, narrow), jnp.float32)
    for p in range(piece_count):
        full = partial[p]
        if p == 0:
            full = full + from_left
        full = full + jnp.where(last_piece == p, from_right, 0.0)
        scores = jnp.where(allowed, full * 0.125, -1e30)
        highest = jnp.max(scores, axis=-1, keepdims=True)
        weights = jnp.where(allowed, jnp.exp(scores - highest), 0.0)
        totals = jnp.sum(weights, axis=-1)
        summed = jnp.einsum("bit,bte->bie", weights, value_f, precision=HIGH)
        attended = jnp.where(masks[p][None, None, :], summed / totals[:, :, None], attended)
    attended = attended.astype(jnp.bfloat16).reshape(query_count, narrow)

    projected = jnp.dot(attended, out_cols, preferred_element_type=jnp.float32)
    projected = projected.reshape(query_count, col_count, narrow).transpose(1, 0, 2)
    own_out = jnp.sum(lax.all_to_all(projected, "col", 0, 0, tiled=True), axis=0)
    hidden_out = (picked_shift.reshape(query_count, narrow) + own_out).astype(jnp.bfloat16)
    return (joined_cache, hidden_out.reshape(req_here, sel_count, narrow))


def solution(mesh):
    return jax.shard_map(
        per_device,
        mesh=mesh,
        in_specs=(
            P("row", None, None),
            P(),
            P(),
            P("row", "col"),
            P("row", None, "col"),
            P("col", "row"),
            P(),
            P(),
            P(),
        ),
        out_specs=(P("row", None, None, "col"), P("row", None, "col")),
        check_vma=False,
    )
```

profile of v0, /device:TPU:328, one launch (start us, length us, event | category | flops | bytes accessed | tf_op | source)
XLA Modules:
  0.0 242.0 jit_solution(12367845848709379092)
XLA Ops:
  5.5 2.3 gather_fusion.3
  10.4 9.6 %all-to-all-start = ((bf16[32,29,1600]{2,1,0:T(8,128)(2,1)}), bf16[32,29,1600]{2,1,0:T(8,128)(2,1)}, u32[]{:S(2)}, u32[]{:S(2)}) async-start(bf16[32,29,1600]{2,1,0:T(8,128)(2,1)} %pad_maximum_fusion), calls=%async_computation | async-start | bytes 6815744 | tf_op jit(solution)/shard_map/all_to_all | solution.py:89
  27.5 2.3 gather_fusion
  30.1 2.6 %gather_fusion.12 = f32[256,1600]{1,0:T(8,128)} fusion(f32[320,1600]{1,0:T(8,128)S(1)} %convert_element_type.108, s32[1024]{0:T(1024)S(1)} %pad_clamp_fusion.2), kind=kCustom, calls=%fused_computation.12 | custom fusion | bytes 3277824 | tf_op jit(solution)/shard_map/gather | solution.py:141
  32.6 2.6 %gather_fusion.11 = f32[256,1600]{1,0:T(8,128)} fusion(f32[320,1600]{1,0:T(8,128)S(1)} %convert_element_type.108, s32[1024]{0:T(1024)S(1)} %pad_clamp_fusion.3), kind=kCustom, calls=%fused_computation.11 | custom fusion | bytes 3277824 | tf_op jit(solution)/shard_map/gather | solution.py:141
  35.2 2.6 %gather_fusion.10 = f32[256,1600]{1,0:T(8,128)} fusion(f32[320,1600]{1,0:T(8,128)S(1)} %convert_element_type.108, s32[1024]{0:T(1024)S(1)} %pad_clamp_fusion.4), kind=kCustom, calls=%fused_computation.10 | custom fusion | bytes 3277824 | tf_op jit(solution)/shard_map/gather | solution.py:141
  37.9 2.6 %gather_fusion.9 = f32[256,1600]{1,0:T(8,128)} fusion(f32[320,1600]{1,0:T(8,128)S(1)} %convert_element_type.108, s32[1024]{0:T(1024)S(1)} %pad_clamp_fusion.5), kind=kCustom, calls=%fused_computation.9 | custom fusion | bytes 3277824 | tf_op jit(solution)/shard_map/gather | solution.py:141
  40.5 2.6 %gather_fusion.8 = f32[256,1600]{1,0:T(8,128)} fusion(f32[320,1600]{1,0:T(8,128)S(1)} %convert_element_type.108, s32[1024]{0:T(1024)S(1)} %pad_clamp_fusion.6), kind=kCustom, calls=%fused_computation.8 | custom fusion | bytes 3277824 | tf_op jit(solution)/shard_map/gather | solution.py:141
  43.1 2.6 %gather_fusion.7 = f32[256,1600]{1,0:T(8,128)} fusion(f32[320,1600]{1,0:T(8,128)S(1)} %convert_element_type.108, s32[1024]{0:T(1024)S(1)} %pad_clamp_fusion.7), kind=kCustom, calls=%fused_computation.7 | custom fusion | bytes 3277824 | tf_op jit(solution)/shard_map/gather | solution.py:141
  45.7 2.6 %gather_fusion.6 = f32[256,1600]{1,0:T(8,128)} fusion(f32[320,1600]{1,0:T(8,128)S(1)} %convert_element_type.108, s32[1024]{0:T(1024)S(1)} %get-tuple-element.76), kind=kCustom, calls=%fused_computation.6 | custom fusion | bytes 3277824 | tf_op jit(solution)/shard_map/gather | solution.py:141
  48.3 2.7 %gather_fusion.5 = f32[256,1600]{1,0:T(8,128)} fusion(f32[320,1600]{1,0:T(8,128)S(1)} %convert_element_type.108, s32[1024]{0:T(1024)S(1)} %get-tuple-element.77), kind=kCustom, calls=%fused_computation.5 | custom fusion | bytes 3277824 | tf_op jit(solution)/shard_map/gather | solution.py:141
  51.0 2.6 %gather_fusion.2 = f32[256,1600]{1,0:T(8,128)} fusion(f32[320,1600]{1,0:T(8,128)S(1)} %convert_element_type.108, s32[1024]{0:T(1024)S(1)} %pad_clamp_fusion.12), kind=kCustom, calls=%fused_computation.2 | custom fusion | bytes 3277824 | tf_op jit(solution)/shard_map/gather | solution.py:141
  53.6 2.6 %gather_fusion.1 = f32[256,1600]{1,0:T(8,128)} fusion(f32[320,1600]{1,0:T(8,128)S(1)} %convert_element_type.108, s32[1024]{0:T(1024)S(1)} %pad_clamp_fusion.13), kind=kCustom, calls=%fused_computation.1 | custom fusion | bytes 3277824 | tf_op jit(solution)/shard_map/gather | solution.py:141
  59.4 45.2 %all-to-all-done = bf16[32,29,1600]{2,1,0:T(8,128)(2,1)} async-done(((bf16[32,29,1600]{2,1,0:T(8,128)(2,1)}), bf16[32,29,1600]{2,1,0:T(8,128)(2,1)}, u32[]{:S(2)}, u32[]{:S(2)}) %all-to-all-start) | async-done | bytes 2969632 | tf_op jit(solution)/shard_map/all_to_all | solution.py:89
  114.5 3.7 %collective-permute-start.2 = (bf16[256,1600]{0,1:T(8,128)(2,1)}, bf16[256,1600]{0,1:T(8,128)(2,1)}, u32[]{:S(2)}, u32[]{:S(2)}) collective-permute-start(bf16[256,1600]{0,1:T(8,128)(2,1)} %copy.65), channel_id=1, source_target_pairs={{0,3},{1,2},{2,1},{3,0},{4,7},{5,6},{6,5},{7,4},{8,11},{9,10},{10,... | collective-permute-start | bytes 2457608 | tf_op jit(solution)/shard_map/ppermute | solution.py:94
  118.2 3.3 %collective-permute-start.1 = (bf16[256,1600]{0,1:T(8,128)(2,1)}, bf16[256,1600]{0,1:T(8,128)(2,1)}, u32[]{:S(2)}, u32[]{:S(2)}) collective-permute-start(bf16[256,1600]{0,1:T(8,128)(2,1)} %copy.65), channel_id=1, source_target_pairs={{0,2},{1,3},{2,0},{3,1},{4,6},{5,7},{6,4},{7,5},{8,10},{9,11},{10,... | collective-permute-start | bytes 2457608 | tf_op jit(solution)/shard_map/ppermute | solution.py:94
  133.7 3.9 %fusion.75 = (f32[256]{0:T(256)S(1)}, f32[256,1600]{1,0:T(8,128)S(1)}, f32[256]{0:T(256)S(1)}, f32[256,1600]{1,0:T(8,128)S(1)}) fusion(f32[256,1600]{1,0:T(8,128)} %gather_fusion.8, f32[256,1600]{1,0:T(8,128)} %gather_fusion.7, bf16[256,1600]{1,0:T(8,128)(2,1)} %copy.66, f32[256,1600]{1,0:T(8,128)} %gather_fusion.2, f32[256,1600]{1,0:T(8,128)} %gather_fusion.1, ...), kind=kLoop, calls=%fused_computation.253 | loop fusion | flops 3276288 | bytes 11470848 | tf_op jit(solution)/shard_map/reduce_sum | solution.py:14
  138.0 2.7 %copy.70 = bf16[256,1600]{1,0:T(8,128)(2,1)} copy(bf16[256,1600]{0,1:T(8,128)(2,1)} %collective-permute-done.2) | data formatting | bytes 1638400 | tf_op jit(solution)/shard_map/ppermute | solution.py:94
  144.3 10.6 %collective-permute-done.1 = bf16[256,1600]{0,1:T(8,128)(2,1)} collective-permute-done((bf16[256,1600]{0,1:T(8,128)(2,1)}, bf16[256,1600]{0,1:T(8,128)(2,1)}, u32[]{:S(2)}, u32[]{:S(2)}) %collective-permute-start.1) | collective-permute-done | bytes 819232 | tf_op jit(solution)/shard_map/ppermute | solution.py:94
  157.1 3.9 %fusion.72 = (f32[256]{0:T(256)S(1)}, f32[256,1600]{1,0:T(8,128)S(1)}, f32[256]{0:T(256)S(1)}, f32[256,1600]{1,0:T(8,128)S(1)}) fusion(f32[256,1600]{1,0:T(8,128)} %gather_fusion.12, f32[256,1600]{1,0:T(8,128)} %gather_fusion.11, bf16[256,1600]{1,0:T(8,128)(2,1)} %copy.70, f32[256,1600]{1,0:T(8,128)} %gather_fusion.10, f32[256,1600]{1,0:T(8,128)} %gather_fusion.9, ...), kind=kLoop, calls=%fused_computation.251 | loop fusion | flops 3276288 | bytes 11470848 | tf_op jit(solution)/shard_map/reduce_sum | solution.py:14
  167.6 4.1 %gather_fusion.13 = bf16[1280,200]{1,0:T(8,128)(2,1)S(1)} fusion(bf16[1280,200]{1,0:T(8,128)(2,1)S(1)} %copy.71, s32[2048]{0:T(1024)S(1)} %pad_clamp_fusion), kind=kCustom, calls=%fused_computation.13 | custom fusion | bytes 1029120 | tf_op jit(solution)/shard_map/gather | solution.py:154
  175.9 3.3 %collective-permute-start.4 = (f32[4,32,320]{2,1,0:T(8,128)S(1)}, f32[4,32,320]{2,1,0:T(8,128)S(1)}, u32[]{:S(2)}, u32[]{:S(2)}) collective-permute-start(f32[4,32,320]{2,1,0:T(8,128)S(1)} %get-tuple-element.66), channel_id=1, source_target_pairs={{0,1},{1,2},{2,3},{3,4},{4,5},{5,6},{6,7},{7,8},{8,9},{9,10},{10,1... | collective-permute-start | bytes 491528 | tf_op jit(solution)/shard_map/ppermute | solution.py:180
  184.2 38.7 %all-to-all-start.1 = ((f32[16,128,100]{1,2,0:T(8,128)}), f32[16,128,100]{1,2,0:T(8,128)S(1)}, u32[]{:S(2)}, u32[]{:S(2)}) async-start(f32[16,128,100]{1,2,0:T(8,128)} %convolution_bitcast_fusion), calls=%async_computation.1 | async-start | bytes 1703936 | tf_op jit(solution)/shard_map/all_to_all | solution.py:199
  234.5 6.7 %all-to-all-done.1 = f32[16,128,100]{1,2,0:T(8,128)S(1)} async-done(((f32[16,128,100]{1,2,0:T(8,128)}), f32[16,128,100]{1,2,0:T(8,128)S(1)}, u32[]{:S(2)}, u32[]{:S(2)}) %all-to-all-start.1) | async-done | bytes 819232 | tf_op jit(solution)/shard_map/all_to_all | solution.py:199
  (253 shorter events, 73.8 us)
Async XLA Ops:
  0.6 4.9 %copy-start = (bf16[16,32,1600]{2,1,0:T(8,128)(2,1)S(1)}, bf16[16,32,1600]{2,1,0:T(8,128)(2,1)}, u32[]{:S(2)}) copy-start(bf16[16,32,1600]{2,1,0:T(8,128)(2,1)} %param.9) | copy-start | bytes 4915204
  10.4 9.7 %copy-start.19 = (s32[128,32]{0,1:T(8,128)S(1)}, s32[128,32]{0,1:T(8,128)}, u32[]{:S(2)}) copy-start(s32[128,32]{0,1:T(8,128)} %param.17) | copy-start | bytes 49156
  10.4 11.5 %copy-start.22 = (bf16[1600]{0:T(1024)(128)(2,1)S(1)}, bf16[1600]{0:T(1024)(128)(2,1)}, u32[]{:S(2)}) copy-start(bf16[1600]{0:T(1024)(128)(2,1)} %param.11) | copy-start | bytes 9604
  10.4 94.3 %all-to-all-start = ((bf16[32,29,1600]{2,1,0:T(8,128)(2,1)}), bf16[32,29,1600]{2,1,0:T(8,128)(2,1)}, u32[]{:S(2)}, u32[]{:S(2)}) async-start(bf16[32,29,1600]{2,1,0:T(8,128)(2,1)} %pad_maximum_fusion), calls=%async_computation | async-start | bytes 6815744 | tf_op jit(solution)/shard_map/all_to_all | solution.py:89
  27.5 2.4 copy-start.10
  53.6 2.6 %copy-start.25 = (s32[32,4]{0,1:T(4,128)S(1)}, s32[32,4]{0,1:T(4,128)}, u32[]{:S(2)}) copy-start(s32[32,4]{0,1:T(4,128)} %param.16) | copy-start | bytes 1540
  111.5 12.0 %copy-start.8 = (bf16[32,10000]{1,0:T(8,128)(2,1)S(1)}, bf16[32,10000]{1,0:T(8,128)(2,1)}, u32[]{:S(2)}) copy-start(bf16[32,10000]{1,0:T(8,128)(2,1)} %slice.107) | copy-start | bytes 1920004
  113.2 12.9 %copy-start.7 = (f32[256,1600]{1,0:T(8,128)S(1)}, f32[256,1600]{1,0:T(8,128)}, u32[]{:S(2)}) copy-start(f32[256,1600]{1,0:T(8,128)} %gather_fusion.6) | copy-start | bytes 4915204
  114.5 23.5 %collective-permute-start.2 = (bf16[256,1600]{0,1:T(8,128)(2,1)}, bf16[256,1600]{0,1:T(8,128)(2,1)}, u32[]{:S(2)}, u32[]{:S(2)}) collective-permute-start(bf16[256,1600]{0,1:T(8,128)(2,1)} %copy.65), channel_id=1, source_target_pairs={{0,3},{1,2},{2,1},{3,0},{4,7},{5,6},{6,5},{7,4},{8,11},{9,10},{10,... | collective-permute-start | bytes 2457608 | tf_op jit(solution)/shard_map/ppermute | solution.py:94
  118.2 36.7 %collective-permute-start.1 = (bf16[256,1600]{0,1:T(8,128)(2,1)}, bf16[256,1600]{0,1:T(8,128)(2,1)}, u32[]{:S(2)}, u32[]{:S(2)}) collective-permute-start(bf16[256,1600]{0,1:T(8,128)(2,1)} %copy.65), channel_id=1, source_target_pairs={{0,2},{1,3},{2,0},{3,1},{4,6},{5,7},{6,4},{7,5},{8,10},{9,11},{10,... | collective-permute-start | bytes 2457608 | tf_op jit(solution)/shard_map/ppermute | solution.py:94
  121.5 10.0 %collective-permute-start = (bf16[256,1600]{0,1:T(8,128)(2,1)}, bf16[256,1600]{0,1:T(8,128)(2,1)}, u32[]{:S(2)}, u32[]{:S(2)}) collective-permute-start(bf16[256,1600]{0,1:T(8,128)(2,1)} %copy.65), channel_id=1, source_target_pairs={{0,1},{1,0},{2,3},{3,2},{4,5},{5,4},{6,7},{7,6},{8,9},{9,8},{10,11... | collective-permute-start | bytes 2457608 | tf_op jit(solution)/shard_map/ppermute | solution.py:94
  126.0 2.3 copy-start.14
  128.0 3.5 %copy-start.6 = (f32[256,1600]{1,0:T(8,128)}, f32[256,1600]{1,0:T(8,128)S(1)}, u32[]{:S(2)}) copy-start(f32[256,1600]{1,0:T(8,128)S(1)} %get-tuple-element.40) | copy-start | bytes 4915204
  137.6 23.4 %copy-start.3 = (f32[256,1600]{1,0:T(8,128)}, f32[256,1600]{1,0:T(8,128)S(1)}, u32[]{:S(2)}) copy-start(f32[256,1600]{1,0:T(8,128)S(1)} %get-tuple-element.71) | copy-start | bytes 4915204
  137.6 28.2 %copy-start.2 = (f32[256,1600]{1,0:T(8,128)}, f32[256,1600]{1,0:T(8,128)S(1)}, u32[]{:S(2)}) copy-start(f32[256,1600]{1,0:T(8,128)S(1)} %get-tuple-element.38) | copy-start | bytes 4915204
  161.0 3.3 %copy-start.5 = (f32[256,1600]{1,0:T(8,128)}, f32[256,1600]{1,0:T(8,128)S(1)}, u32[]{:S(2)}) copy-start(f32[256,1600]{1,0:T(8,128)S(1)} %get-tuple-element.69) | copy-start | bytes 4915204
  161.0 4.5 %copy-start.4 = (f32[256,1600]{1,0:T(8,128)}, f32[256,1600]{1,0:T(8,128)S(1)}, u32[]{:S(2)}) copy-start(f32[256,1600]{1,0:T(8,128)S(1)} %get-tuple-element.32) | copy-start | bytes 4915204
  161.1 2.1 copy-start.15
  172.0 3.6 %copy-start.23 = (pred[100]{0:T(512)(128)(4,1)S(1)}, pred[100]{0:T(512)(128)(4,1)}, u32[]{:S(2)}) copy-start(pred[100]{0:T(512)(128)(4,1)} %get-tuple-element.75) | copy-start | bytes 304
  173.6 5.7 %copy-start.9 = (bf16[32,5000]{1,0:T(8,128)(2,1)S(1)}, bf16[32,5000]{1,0:T(8,128)(2,1)}, u32[]{:S(2)}) copy-start(bf16[32,5000]{1,0:T(8,128)(2,1)} %get-tuple-element.47) | copy-start | bytes 960004
  174.3 6.5 %collective-permute-start.3 = (f32[4,32,320]{2,1,0:T(8,128)S(1)}, f32[4,32,320]{2,1,0:T(8,128)S(1)}, u32[]{:S(2)}, u32[]{:S(2)}) collective-permute-start(f32[4,32,320]{2,1,0:T(8,128)S(1)} %fusion.20), channel_id=1, source_target_pairs={{1,0},{2,1},{3,2},{4,3},{5,4},{6,5},{7,6},{8,7},{9,8},{10,9},{11,1... | collective-permute-start | bytes 491528 | tf_op jit(solution)/shard_map/ppermute | solution.py:181
  175.9 4.9 %collective-permute-start.4 = (f32[4,32,320]{2,1,0:T(8,128)S(1)}, f32[4,32,320]{2,1,0:T(8,128)S(1)}, u32[]{:S(2)}, u32[]{:S(2)}) collective-permute-start(f32[4,32,320]{2,1,0:T(8,128)S(1)} %get-tuple-element.66), channel_id=1, source_target_pairs={{0,1},{1,2},{2,3},{3,4},{4,5},{5,6},{6,7},{7,8},{8,9},{9,10},{10,1... | collective-permute-start | bytes 491528 | tf_op jit(solution)/shard_map/ppermute | solution.py:180
  184.2 57.0 %all-to-all-start.1 = ((f32[16,128,100]{1,2,0:T(8,128)}), f32[16,128,100]{1,2,0:T(8,128)S(1)}, u32[]{:S(2)}, u32[]{:S(2)}) async-start(f32[16,128,100]{1,2,0:T(8,128)} %convolution_bitcast_fusion), calls=%async_computation.1 | async-start | bytes 1703936 | tf_op jit(solution)/shard_map/all_to_all | solution.py:199
  222.9 19.1 %copy-start.1 = (bf16[16,32,1600]{2,1,0:T(8,128)(2,1)S(1)}, bf16[16,32,1600]{2,1,0:T(8,128)(2,1)}, u32[]{:S(2)}) copy-start(bf16[16,32,1600]{2,1,0:T(8,128)(2,1)} %param.9) | copy-start | bytes 4915204
  (10 other events, 15.7 us)
where the time goes:
time: 243 us; the launch traced here: 242 us
  local copies, waits for them, and re-layouts  83.9 us (35%)
  waiting for transfers between devices  62.5 us (26%)
  starting transfers between devices  61.9 us (25%)
  other arithmetic  20.9 us (9%)
  matrix products  11.1 us (5%)
    all_to_all x1, waiting for transfers between devices, fetch_groups(): lax.all_to_all(sent, 'row', split_axis=0, concat_axis=0, tiled=True)  45.2 us
    all_to_all x1, starting transfers between devices, per_device(): lax.all_to_all(projected, 'col', 0, 0, tiled=True)  38.7 us
    gather x10, local copies, waits for them, and re-layouts, per_device(): shifted = block.astype(jnp.float32) + pos_f[place] - pos_f[tok]  26.1 us
    unnamed x69, local copies, waits for them, and re-layouts  14.1 us
    ppermute x3, waiting for transfers between devices, fetch_groups(): lax.ppermute(compact, 'col', [(c, c ^ m) for c in range(col_count)])  10.6 us
    reduce_sum x3, other arithmetic, layer_norm(): center = shifted - jnp.mean(shifted, axis=-1, keepdims=True)  9.81 us
    all_to_all x1, starting transfers between devices, fetch_groups(): lax.all_to_all(sent, 'row', split_axis=0, concat_axis=0, tiled=True)  9.61 us
    ppermute x3, starting transfers between devices, fetch_groups(): lax.ppermute(compact, 'col', [(c, c ^ m) for c in range(col_count)])  9.02 us
  transfers between devices with their start and end apart: 7, of which 3 were waited for; matrix products, arithmetic and copies ran while one was open for 30% of the time, Pallas kernels for 0%

commit v1 on v0

--- a/solution.py
+++ b/solution.py
@@ -77,18 +77,13 @@
     send_rows = send_slot[:, :, None] * group_len + own_part * part + tok_ids
     payload = store_rows[send_rows.reshape(-1)].reshape(row_count, capacity * part, full_width)
     live_rows = jnp.repeat(send_live, part, axis=1)
-    extra_rows = -(-extra.shape[0] // full_width)
-    extra_pad = jnp.pad(extra, (0, extra_rows * full_width - extra.shape[0])).reshape(extra_rows, full_width)
-    sent = jnp.concatenate(
-        [
-            jnp.where(live_rows[:, :, None], payload, jnp.zeros_like(payload)),
-            jnp.broadcast_to(extra_pad[None], (row_count, extra_rows, full_width)),
-        ],
-        axis=1,
-    )
+    sent = jnp.where(live_rows[:, :, None], payload, jnp.zeros_like(payload))
     received = lax.all_to_all(sent, "row", split_axis=0, concat_axis=0, tiled=True)
-    extra_all = received[:, capacity * part:].reshape(row_count, -1)[:, : extra.shape[0]]
-    flat = received[:, : capacity * part].reshape(row_count * capacity * part, full_width)
+    extra, received = lax.optimization_barrier((extra, received))
+    extra_all = lax.all_to_all(
+        jnp.broadcast_to(extra[None], (row_count,) + extra.shape), "row", 0, 0, tiled=True
+    )
+    flat = received.reshape(row_count * capacity * part, full_width)
     compact = flat[(compact_index[:, None] * part + tok_ids).reshape(-1)]
     pieces = [compact] + [
         lax.ppermute(compact, "col", [(c, c ^ m) for c in range(col_count)]) for m in range(1, split)

time: 243 us -> 221 us (0.909)
  the two profiles are of different devices: /device:TPU:328 before, /device:TPU:9 now
where the time goes in v1:
time: 221 us; the launch traced here: 217 us
  local copies, waits for them, and re-layouts  91.9 us (42%)
  starting transfers between devices  55.2 us (25%)
  waiting for transfers between devices  29.8 us (13%)
  other arithmetic  27.3 us (12%)
  matrix products  10.6 us (5%)
    unnamed x62, local copies, waits for them, and re-layouts  26.5 us
    gather x10, local copies, waits for them, and re-layouts, per_device(): shifted = block.astype(jnp.float32) + pos_f[place] - pos_f[tok]  26 us
    all_to_all x1, starting transfers between devices, per_device(): lax.all_to_all(projected, 'col', 0, 0, tiled=True)  17.3 us
    all_to_all x1, waiting for transfers between devices, per_device(): lax.all_to_all(projected, 'col', 0, 0, tiled=True)  15.4 us
    all_to_all x1, starting transfers between devices, fetch_groups(): lax.all_to_all(sent, 'row', split_axis=0, concat_axis=0, tiled=True)  13.6 us
    broadcast_in_dim x1, other arithmetic, fetch_groups(): jnp.broadcast_to(extra[None], (row_count,) + extra.shape)  9.81 us
    reduce_sum x4, other arithmetic, layer_norm(): center = shifted - jnp.mean(shifted, axis=-1, keepdims=True)  9.51 us
    all_to_all x1, waiting for transfers between devices, fetch_groups(): lax.all_to_all(jnp.broadcast_to(extra[None], (row_count,) + extra.shape),...  9.09 us
  transfers between devices with their start and end apart: 8, of which 5 were waited for; matrix products, arithmetic and copies ran while one was open for 38% of the time, Pallas kernels for 0%

profile of v1, /device:TPU:9, one launch (start us, length us, event | category | flops | bytes accessed | tf_op | source)
XLA Modules:
  0.0 216.7 jit_solution(18092641242301321048)
XLA Ops:
  6.4 13.6 %all-to-all-start = ((bf16[32,16,1600]{2,1,0:T(8,128)(2,1)}), bf16[32,16,1600]{2,1,0:T(8,128)(2,1)}, u32[]{:S(2)}, u32[]{:S(2)}) async-start(bf16[32,16,1600]{2,1,0:T(8,128)(2,1)} %broadcast_select_fusion), calls=%async_computation | async-start | bytes 3407872 | tf_op jit(solution)/shard_map/all_to_all | solution.py:81
  30.7 2.6 %gather_fusion.12 = f32[256,1600]{1,0:T(8,128)} fusion(f32[320,1600]{1,0:T(8,128)S(1)} %convert_element_type.106, s32[1024]{0:T(1024)S(1)} %pad_clamp_fusion.2), kind=kCustom, calls=%fused_computation.12 | custom fusion | bytes 3277824 | tf_op jit(solution)/shard_map/gather | solution.py:136
  33.3 2.6 %gather_fusion.11 = f32[256,1600]{1,0:T(8,128)} fusion(f32[320,1600]{1,0:T(8,128)S(1)} %convert_element_type.106, s32[1024]{0:T(1024)S(1)} %pad_clamp_fusion.3), kind=kCustom, calls=%fused_computation.11 | custom fusion | bytes 3277824 | tf_op jit(solution)/shard_map/gather | solution.py:136
  35.9 2.6 %gather_fusion.10 = f32[256,1600]{1,0:T(8,128)} fusion(f32[320,1600]{1,0:T(8,128)S(1)} %convert_element_type.106, s32[1024]{0:T(1024)S(1)} %pad_clamp_fusion.4), kind=kCustom, calls=%fused_computation.10 | custom fusion | bytes 3277824 | tf_op jit(solution)/shard_map/gather | solution.py:136
  38.6 2.6 %gather_fusion.9 = f32[256,1600]{1,0:T(8,128)} fusion(f32[320,1600]{1,0:T(8,128)S(1)} %convert_element_type.106, s32[1024]{0:T(1024)S(1)} %pad_clamp_fusion.5), kind=kCustom, calls=%fused_computation.9 | custom fusion | bytes 3277824 | tf_op jit(solution)/shard_map/gather | solution.py:136
  43.7 2.6 %gather_fusion.7 = f32[256,1600]{1,0:T(8,128)} fusion(f32[320,1600]{1,0:T(8,128)S(1)} %convert_element_type.106, s32[1024]{0:T(1024)S(1)} %get-tuple-element.81), kind=kCustom, calls=%fused_computation.7 | custom fusion | bytes 3277824 | tf_op jit(solution)/shard_map/gather | solution.py:136
  46.3 2.7 %gather_fusion.6 = f32[256,1600]{1,0:T(8,128)} fusion(f32[320,1600]{1,0:T(8,128)S(1)} %convert_element_type.106, s32[1024]{0:T(1024)S(1)} %get-tuple-element.82), kind=kCustom, calls=%fused_computation.6 | custom fusion | bytes 3277824 | tf_op jit(solution)/shard_map/gather | solution.py:136
  51.6 2.6 %gather_fusion.2 = f32[256,1600]{1,0:T(8,128)} fusion(f32[320,1600]{1,0:T(8,128)S(1)} %convert_element_type.106, s32[1024]{0:T(1024)S(1)} %pad_clamp_fusion.12), kind=kCustom, calls=%fused_computation.2 | custom fusion | bytes 3277824 | tf_op jit(solution)/shard_map/gather | solution.py:136
  54.2 2.6 %gather_fusion.1 = f32[256,1600]{1,0:T(8,128)} fusion(f32[320,1600]{1,0:T(8,128)S(1)} %convert_element_type.106, s32[1024]{0:T(1024)S(1)} %pad_clamp_fusion.13), kind=kCustom, calls=%fused_computation.1 | custom fusion | bytes 3277824 | tf_op jit(solution)/shard_map/gather | solution.py:136
  62.1 3.8 %gather_fusion.4 = bf16[256,1600]{1,0:T(8,128)(2,1)S(1)} fusion(bf16[512,1600]{1,0:T(8,128)(2,1)} %bitcast.10, s32[1024]{0:T(1024)S(1)} %pad_clamp_fusion.10), kind=kCustom, calls=%fused_computation.4 | custom fusion | bytes 1639424 | tf_op jit(solution)/shard_map/gather | solution.py:87
  67.2 4.7 %collective-permute-start.2 = (bf16[256,1600]{0,1:T(8,128)(2,1)}, bf16[256,1600]{0,1:T(8,128)(2,1)}, u32[]{:S(2)}, u32[]{:S(2)}) collective-permute-start(bf16[256,1600]{0,1:T(8,128)(2,1)} %copy.65), channel_id=1, source_target_pairs={{0,3},{1,2},{2,1},{3,0},{4,7},{5,6},{6,5},{7,4},{8,11},{9,10},{10,... | collective-permute-start | bytes 2457608 | tf_op jit(solution)/shard_map/ppermute | solution.py:89
  78.0 9.8 %reduce.17 = bf16[32,20000]{1,0:T(8,128)(2,1)} reduce(bf16[32,1,20000]{2,1,0:T(2,128)(2,1)S(1)} %broadcast_in_dim.257, bf16[]{:T(256)} %broadcast.1089), dimensions={1}, to_apply=%broadcast_in_dim.257.reduce_sub_computation | reduce | bytes 2560002 | tf_op jit(solution)/shard_map/broadcast_in_dim | solution.py:84
  87.8 2.9 %reshape.1110 = bf16[32,2,10000]{2,1,0:T(2,128)(2,1)} reshape(bf16[32,20000]{1,0:T(8,128)(2,1)} %reduce.17) | data formatting | bytes 2560000
  90.7 8.8 %all-to-all-start.1 = ((bf16[32,2,10000]{2,1,0:T(2,128)(2,1)}), bf16[32,2,10000]{2,1,0:T(2,128)(2,1)}, u32[]{:S(2)}, u32[]{:S(2)}) async-start(bf16[32,2,10000]{2,1,0:T(2,128)(2,1)} %reshape.1110), calls=%async_computation.1 | async-start | bytes 2588672 | tf_op jit(solution)/shard_map/all_to_all | solution.py:83
  105.1 3.6 %collective-permute-done.1 = bf16[256,1600]{0,1:T(8,128)(2,1)} collective-permute-done((bf16[256,1600]{0,1:T(8,128)(2,1)}, bf16[256,1600]{0,1:T(8,128)(2,1)}, u32[]{:S(2)}, u32[]{:S(2)}) %collective-permute-start.1) | collective-permute-done | bytes 819232 | tf_op jit(solution)/shard_map/ppermute | solution.py:89
  110.9 3.9 %fusion.72 = (f32[256]{0:T(256)S(1)}, f32[256,1600]{1,0:T(8,128)S(1)}, f32[256]{0:T(256)S(1)}, f32[256,1600]{1,0:T(8,128)S(1)}) fusion(f32[256,1600]{1,0:T(8,128)} %gather_fusion.12, f32[256,1600]{1,0:T(8,128)} %gather_fusion.11, bf16[256,1600]{1,0:T(8,128)(2,1)} %copy.70, f32[256,1600]{1,0:T(8,128)} %gather_fusion.10, f32[256,1600]{1,0:T(8,128)} %gather_fusion.9, ...), kind=kLoop, calls=%fused_computation.251 | loop fusion | flops 3276288 | bytes 11470848 | tf_op jit(solution)/shard_map/reduce_sum | solution.py:14
  114.9 2.7 %copy.66 = bf16[256,1600]{1,0:T(8,128)(2,1)} copy(bf16[256,1600]{0,1:T(8,128)(2,1)} %collective-permute-done) | data formatting | bytes 1638400 | tf_op jit(solution)/shard_map/ppermute | solution.py:89
  122.7 9.1 %all-to-all-done.1 = bf16[32,2,10000]{2,1,0:T(2,128)(2,1)} async-done(((bf16[32,2,10000]{2,1,0:T(2,128)(2,1)}), bf16[32,2,10000]{2,1,0:T(2,128)(2,1)}, u32[]{:S(2)}, u32[]{:S(2)}) %all-to-all-start.1) | async-done | bytes 1280032 | tf_op jit(solution)/shard_map/all_to_all | solution.py:83
  131.7 8.2 %reshape.1111 = bf16[32,1,20000]{2,1,0:T(2,128)(2,1)S(1)} reshape(bf16[32,2,10000]{2,1,0:T(2,128)(2,1)} %all-to-all-done.1) | data formatting | bytes 2560000
  151.5 4.3 %gather_fusion.13 = bf16[1280,200]{1,0:T(8,128)(2,1)S(1)} fusion(bf16[1280,200]{1,0:T(8,128)(2,1)S(1)} %copy.71, s32[2048]{0:T(1024)S(1)} %pad_clamp_fusion), kind=kCustom, calls=%fused_computation.13 | custom fusion | bytes 1029120 | tf_op jit(solution)/shard_map/gather | solution.py:149
  158.4 3.7 %collective-permute-start.3 = (f32[4,32,320]{2,1,0:T(8,128)S(1)}, f32[4,32,320]{2,1,0:T(8,128)S(1)}, u32[]{:S(2)}, u32[]{:S(2)}) collective-permute-start(f32[4,32,320]{2,1,0:T(8,128)S(1)} %fusion.20), channel_id=1, source_target_pairs={{1,0},{2,1},{3,2},{4,3},{5,4},{6,5},{7,6},{8,7},{9,8},{10,9},{11,1... | collective-permute-start | bytes 491528 | tf_op jit(solution)/shard_map/ppermute | solution.py:176
  162.4 2.9 %collective-permute-start.4 = (f32[4,32,320]{2,1,0:T(8,128)S(1)}, f32[4,32,320]{2,1,0:T(8,128)S(1)}, u32[]{:S(2)}, u32[]{:S(2)}) collective-permute-start(f32[4,32,320]{2,1,0:T(8,128)S(1)} %get-tuple-element.70), channel_id=1, source_target_pairs={{0,1},{1,2},{2,3},{3,4},{4,5},{5,6},{6,7},{7,8},{8,9},{9,10},{10,1... | collective-permute-start | bytes 491528 | tf_op jit(solution)/shard_map/ppermute | solution.py:175
  171.3 17.3 %all-to-all-start.2 = ((f32[16,128,100]{1,2,0:T(8,128)}), f32[16,128,100]{1,2,0:T(8,128)S(1)}, u32[]{:S(2)}, u32[]{:S(2)}) async-start(f32[16,128,100]{1,2,0:T(8,128)} %convolution_bitcast_fusion), calls=%async_computation.2 | async-start | bytes 1703936 | tf_op jit(solution)/shard_map/all_to_all | solution.py:194
  200.3 15.4 %all-to-all-done.2 = f32[16,128,100]{1,2,0:T(8,128)S(1)} async-done(((f32[16,128,100]{1,2,0:T(8,128)}), f32[16,128,100]{1,2,0:T(8,128)S(1)}, u32[]{:S(2)}, u32[]{:S(2)}) %all-to-all-start.2) | async-done | bytes 819232 | tf_op jit(solution)/shard_map/all_to_all | solution.py:194
  (243 shorter events, 79.2 us)
Async XLA Ops:
  0.6 2.0 copy-start
  6.4 14.1 %copy-start.17 = (s32[128,32]{0,1:T(8,128)S(1)}, s32[128,32]{0,1:T(8,128)}, u32[]{:S(2)}) copy-start(s32[128,32]{0,1:T(8,128)} %param.17) | copy-start | bytes 49156
  6.4 55.7 %all-to-all-start = ((bf16[32,16,1600]{2,1,0:T(8,128)(2,1)}), bf16[32,16,1600]{2,1,0:T(8,128)(2,1)}, u32[]{:S(2)}, u32[]{:S(2)}) async-start(bf16[32,16,1600]{2,1,0:T(8,128)(2,1)} %broadcast_select_fusion), calls=%async_computation | async-start | bytes 3407872 | tf_op jit(solution)/shard_map/all_to_all | solution.py:81
  20.0 6.8 %copy-start.20 = (bf16[1600]{0:T(1024)(128)(2,1)S(1)}, bf16[1600]{0:T(1024)(128)(2,1)}, u32[]{:S(2)}) copy-start(bf16[1600]{0:T(1024)(128)(2,1)} %param.11) | copy-start | bytes 9604
  20.0 6.8 %copy-start.19 = (bf16[50,100]{1,0:T(8,128)(2,1)S(1)}, bf16[50,100]{1,0:T(8,128)(2,1)}, u32[]{:S(2)}) copy-start(bf16[50,100]{1,0:T(8,128)(2,1)} %param.12) | copy-start | bytes 30004
  20.0 7.2 %copy-start.16 = (bf16[50,2,100]{2,1,0:T(2,128)(2,1)S(1)}, bf16[50,2,100]{2,1,0:T(2,128)(2,1)}, u32[]{:S(2)}) copy-start(bf16[50,2,100]{2,1,0:T(2,128)(2,1)} %param.13) | copy-start | bytes 60004
  20.0 7.3 %copy-start.18 = (bf16[100,50]{0,1:T(8,128)(2,1)S(1)}, bf16[100,50]{0,1:T(8,128)(2,1)}, u32[]{:S(2)}) copy-start(bf16[100,50]{0,1:T(8,128)(2,1)} %param.14) | copy-start | bytes 30004
  54.2 2.9 %copy-start.21 = (s32[32,4]{0,1:T(4,128)S(1)}, s32[32,4]{0,1:T(4,128)}, u32[]{:S(2)}) copy-start(s32[32,4]{0,1:T(4,128)} %param.16) | copy-start | bytes 1540
  67.2 35.7 %collective-permute-start.2 = (bf16[256,1600]{0,1:T(8,128)(2,1)}, bf16[256,1600]{0,1:T(8,128)(2,1)}, u32[]{:S(2)}, u32[]{:S(2)}) collective-permute-start(bf16[256,1600]{0,1:T(8,128)(2,1)} %copy.65), channel_id=1, source_target_pairs={{0,3},{1,2},{2,1},{3,0},{4,7},{5,6},{6,5},{7,4},{8,11},{9,10},{10,... | collective-permute-start | bytes 2457608 | tf_op jit(solution)/shard_map/ppermute | solution.py:89
  71.9 36.8 %collective-permute-start.1 = (bf16[256,1600]{0,1:T(8,128)(2,1)}, bf16[256,1600]{0,1:T(8,128)(2,1)}, u32[]{:S(2)}, u32[]{:S(2)}) collective-permute-start(bf16[256,1600]{0,1:T(8,128)(2,1)} %copy.65), channel_id=1, source_target_pairs={{0,2},{1,3},{2,0},{3,1},{4,6},{5,7},{6,4},{7,5},{8,10},{9,11},{10,... | collective-permute-start | bytes 2457608 | tf_op jit(solution)/shard_map/ppermute | solution.py:89
  74.0 40.8 %collective-permute-start = (bf16[256,1600]{0,1:T(8,128)(2,1)}, bf16[256,1600]{0,1:T(8,128)(2,1)}, u32[]{:S(2)}, u32[]{:S(2)}) collective-permute-start(bf16[256,1600]{0,1:T(8,128)(2,1)} %copy.65), channel_id=1, source_target_pairs={{0,1},{1,0},{2,3},{3,2},{4,5},{5,4},{6,7},{7,6},{8,9},{9,8},{10,11... | collective-permute-start | bytes 2457608 | tf_op jit(solution)/shard_map/ppermute | solution.py:89
  90.7 8.8 %copy-start.14 = (f32[256,1600]{1,0:T(8,128)S(1)}, f32[256,1600]{1,0:T(8,128)}, u32[]{:S(2)}) copy-start(f32[256,1600]{1,0:T(8,128)} %gather_fusion.6) | copy-start | bytes 4915204
  90.7 41.0 %all-to-all-start.1 = ((bf16[32,2,10000]{2,1,0:T(2,128)(2,1)}), bf16[32,2,10000]{2,1,0:T(2,128)(2,1)}, u32[]{:S(2)}, u32[]{:S(2)}) async-start(bf16[32,2,10000]{2,1,0:T(2,128)(2,1)} %reshape.1110), calls=%async_computation.1 | async-start | bytes 2588672 | tf_op jit(solution)/shard_map/all_to_all | solution.py:83
  114.9 6.2 %copy-start.2 = (f32[256,1600]{1,0:T(8,128)}, f32[256,1600]{1,0:T(8,128)S(1)}, u32[]{:S(2)}) copy-start(f32[256,1600]{1,0:T(8,128)S(1)} %get-tuple-element.36) | copy-start | bytes 4915204
  114.9 6.2 %copy-start.4 = (f32[256,1600]{1,0:T(8,128)}, f32[256,1600]{1,0:T(8,128)S(1)}, u32[]{:S(2)}) copy-start(f32[256,1600]{1,0:T(8,128)S(1)} %get-tuple-element.73) | copy-start | bytes 4915204
  117.6 2.0 copy-start.13
  140.3 2.7 %copy-start.7 = (f32[256,1600]{1,0:T(8,128)S(1)}, f32[256,1600]{1,0:T(8,128)}, u32[]{:S(2)}) copy-start(f32[256,1600]{1,0:T(8,128)} %copy-done.6) | copy-start | bytes 4915204
  143.0 2.4 %copy-start.9 = (f32[256,1600]{1,0:T(8,128)S(1)}, f32[256,1600]{1,0:T(8,128)}, u32[]{:S(2)}) copy-start(f32[256,1600]{1,0:T(8,128)} %copy-done.8) | copy-start | bytes 4915204
  143.0 2.4 %copy-start.15 = (bf16[1600,200]{1,0:T(8,128)(2,1)S(1)}, bf16[1600,200]{1,0:T(8,128)(2,1)}, u32[]{:S(2)}) copy-start(bf16[1600,200]{1,0:T(8,128)(2,1)} %reshape_reshape.4) | copy-start | bytes 1920004
  145.4 1.5 copy-start.11
  158.4 8.6 %collective-permute-start.3 = (f32[4,32,320]{2,1,0:T(8,128)S(1)}, f32[4,32,320]{2,1,0:T(8,128)S(1)}, u32[]{:S(2)}, u32[]{:S(2)}) collective-permute-start(f32[4,32,320]{2,1,0:T(8,128)S(1)} %fusion.20), channel_id=1, source_target_pairs={{1,0},{2,1},{3,2},{4,3},{5,4},{6,5},{7,6},{8,7},{9,8},{10,9},{11,1... | collective-permute-start | bytes 491528 | tf_op jit(solution)/shard_map/ppermute | solution.py:176
  162.4 5.5 %collective-permute-start.4 = (f32[4,32,320]{2,1,0:T(8,128)S(1)}, f32[4,32,320]{2,1,0:T(8,128)S(1)}, u32[]{:S(2)}, u32[]{:S(2)}) collective-permute-start(f32[4,32,320]{2,1,0:T(8,128)S(1)} %get-tuple-element.70), channel_id=1, source_target_pairs={{0,1},{1,2},{2,3},{3,4},{4,5},{5,6},{6,7},{7,8},{8,9},{9,10},{10,1... | collective-permute-start | bytes 491528 | tf_op jit(solution)/shard_map/ppermute | solution.py:175
  171.3 44.3 %all-to-all-start.2 = ((f32[16,128,100]{1,2,0:T(8,128)}), f32[16,128,100]{1,2,0:T(8,128)S(1)}, u32[]{:S(2)}, u32[]{:S(2)}) async-start(f32[16,128,100]{1,2,0:T(8,128)} %convolution_bitcast_fusion), calls=%async_computation.2 | async-start | bytes 1703936 | tf_op jit(solution)/shard_map/all_to_all | solution.py:194
  193.7 22.7 %copy-start.1 = (bf16[16,32,1600]{2,1,0:T(8,128)(2,1)S(1)}, bf16[16,32,1600]{2,1,0:T(8,128)(2,1)}, u32[]{:S(2)}) copy-start(bf16[16,32,1600]{2,1,0:T(8,128)(2,1)} %param.9) | copy-start | bytes 4915204
  (6 other events, 8.0 us)

commit v2 on v1

--- a/solution.py
+++ b/solution.py
@@ -14,22 +14,6 @@
     center = shifted - jnp.mean(shifted, axis=-1, keepdims=True)
     spread = jnp.mean(center * center, axis=-1, keepdims=True)
     return center * lax.rsqrt(spread + 1e-05) * ln_gain.astype(jnp.float32)
-
-
-def split_weights(allw, w_query, w_keyval, w_out, row_count):
-    q_rows, q_cols = w_query.shape
-    o_rows, o_cols = w_out.shape
-    q_size = w_query.size
-    kv_size = w_keyval.size
-    query_rows = allw[:, :q_size].reshape(row_count * q_rows, q_cols)
-    keyval_rows = allw[:, q_size:q_size + kv_size].reshape(row_count * q_rows, 2, q_cols)
-    out_cols = (
-        allw[:, q_size + kv_size:]
-        .reshape(row_count, o_rows, o_cols)
-        .transpose(1, 0, 2)
-        .reshape(o_rows, row_count * o_cols)
-    )
-    return query_rows, keyval_rows, out_cols
 
 
 def fetch_groups(group_store, group_src, row_count, row_index, col_count, col_index, req_here, extra):
@@ -122,12 +106,15 @@
     query_count = req_here * sel_count
     first_feature = col_index * narrow
 
-    pack = jnp.concatenate([w_query.reshape(-1), w_keyval.reshape(-1), w_out.reshape(-1)])
+    pack = jnp.concatenate(
+        [w_keyval.reshape(w_keyval.shape[0], 2 * narrow), w_query, w_out.T], axis=1
+    )
     blocks, refs, toks, row_of, allw = fetch_groups(
         group_store, group_src, row_count, row_index, col_count, col_index, req_here, pack
     )
-    query_rows, keyval_rows, out_cols = split_weights(allw, w_query, w_keyval, w_out, row_count)
-    w_cat = jnp.concatenate([keyval_rows.reshape(full_width, 2 * narrow), query_rows], axis=1)
+    allw = allw.reshape(full_width, 4 * narrow)
+    w_cat = allw[:, : 3 * narrow]
+    out_rows = allw[:, 3 * narrow:]
 
     pos_f = positions.astype(jnp.float32)
     out_kv, out_q, out_sh = [], [], []
@@ -189,7 +176,9 @@
         attended = jnp.where(masks[p][None, None, :], summed / totals[:, :, None], attended)
     attended = attended.astype(jnp.bfloat16).reshape(query_count, narrow)
 
-    projected = jnp.dot(attended, out_cols, preferred_element_type=jnp.float32)
+    projected = lax.dot_general(
+        attended, out_rows, (((1,), (1,)), ((), ())), preferred_element_type=jnp.float32
+    )
     projected = projected.reshape(query_count, col_count, narrow).transpose(1, 0, 2)
     own_out = jnp.sum(lax.all_to_all(projected, "col", 0, 0, tiled=True), axis=0)
     hidden_out = (picked_shift.reshape(query_count, narrow) + own_out).astype(jnp.bfloat16)

time: 221 us -> 261 us (1.18)
  local copies, waits for them, and re-layouts: 91.9 us -> 119 us
  waiting for transfers between devices: 29.8 us -> 38.2 us
  other arithmetic: 27.3 us -> 32.2 us
    gather x10, local copies, waits for them, and re-layouts: 26 us -> 49 us  [per_device(): shifted = block.astype(jnp.float32) + pos_f[place] - pos_f[tok]]
    ppermute x3, waiting for transfers between devices: 3.59 us -> 15.1 us  [fetch_groups(): lax.ppermute(compact, 'col', [(c, c ^ m) for c in range(col_count)])]
    broadcast_in_dim x1 -> x0, other arithmetic: 9.81 us -> none  [fetch_groups(): jnp.broadcast_to(extra[None], (row_count,) + extra.shape)]
    unnamed x62 -> x92, local copies, waits for them, and re-layouts: 26.5 us -> 22.7 us
  transfers between devices with their start and end apart: 8 -> 8, of which waited for: 5 -> 3; matrix products, arithmetic and copies ran while one was open for 38% -> 43% of each run, Pallas kernels for 0% -> 0%
where the time goes in v2:
time: 261 us; the launch traced here: 256 us
  local copies, waits for them, and re-layouts  119 us (46%)
  starting transfers between devices  55.5 us (21%)
  waiting for transfers between devices  38.2 us (15%)
  other arithmetic  32.2 us (12%)
  matrix products  9.94 us (4%)
    gather x10, local copies, waits for them, and re-layouts, per_device(): shifted = block.astype(jnp.float32) + pos_f[place] - pos_f[tok]  49 us
    unnamed x92, local copies, waits for them, and re-layouts  22.7 us
    all_to_all x1, starting transfers between devices, per_device(): lax.all_to_all(projected, 'col', 0, 0, tiled=True)  17.2 us
    ppermute x3, waiting for transfers between devices, fetch_groups(): lax.ppermute(compact, 'col', [(c, c ^ m) for c in range(col_count)])  15.1 us
    all_to_all x1, waiting for transfers between devices, per_device(): lax.all_to_all(projected, 'col', 0, 0, tiled=True)  14.6 us
    all_to_all x1, starting transfers between devices, fetch_groups(): lax.all_to_all(sent, 'row', split_axis=0, concat_axis=0, tiled=True)  13.5 us
    reduce_sum x4, other arithmetic, layer_norm(): center = shifted - jnp.mean(shifted, axis=-1, keepdims=True)  11.4 us
    all_to_all x1, starting transfers between devices, fetch_groups(): lax.all_to_all(jnp.broadcast_to(extra[None], (row_count,) + extra.shape),...  10.1 us
  transfers between devices with their start and end apart: 8, of which 3 were waited for; matrix products, arithmetic and copies ran while one was open for 43% of the time, Pallas kernels for 0%

profile of v2, /device:TPU:9, one launch (start us, length us, event | category | flops | bytes accessed | tf_op | source)
XLA Modules:
  0.0 256.2 jit_solution(3811020949040908543)
XLA Ops:
  6.4 13.5 %all-to-all-start = ((bf16[32,16,1600]{2,1,0:T(8,128)(2,1)}), bf16[32,16,1600]{2,1,0:T(8,128)(2,1)S(1)}, u32[]{:S(2)}, u32[]{:S(2)}) async-start(bf16[32,16,1600]{2,1,0:T(8,128)(2,1)} %broadcast_select_fusion), calls=%async_computation | async-start | bytes 3407872 | tf_op jit(solution)/shard_map/all_to_all | solution.py:65
  39.7 2.7 %convert_element_type.106 = f32[320,1600]{1,0:T(8,128)} convert(bf16[320,1600]{1,0:T(8,128)(2,1)} %param.10) | non-fusion elementwise | flops 512000 | bytes 3072000 | tf_op jit(solution)/shard_map/convert_element_type | solution.py:119
  42.4 5.0 %gather_fusion.12 = f32[256,1600]{1,0:T(8,128)} fusion(f32[320,1600]{1,0:T(8,128)} %convert_element_type.106, s32[1024]{0:T(1024)} %pad_clamp_fusion.2), kind=kCustom, calls=%fused_computation.12 | custom fusion | bytes 3277824 | tf_op jit(solution)/shard_map/gather | solution.py:123
  47.4 5.0 %gather_fusion.11 = f32[256,1600]{1,0:T(8,128)} fusion(f32[320,1600]{1,0:T(8,128)} %convert_element_type.106, s32[1024]{0:T(1024)} %pad_clamp_fusion.3), kind=kCustom, calls=%fused_computation.11 | custom fusion | bytes 3277824 | tf_op jit(solution)/shard_map/gather | solution.py:123
  52.5 4.8 %gather_fusion.10 = f32[256,1600]{1,0:T(8,128)} fusion(f32[320,1600]{1,0:T(8,128)} %convert_element_type.106, s32[1024]{0:T(1024)S(1)} %pad_clamp_fusion.4), kind=kCustom, calls=%fused_computation.10 | custom fusion | bytes 3277824 | tf_op jit(solution)/shard_map/gather | solution.py:123
  57.3 4.8 %gather_fusion.9 = f32[256,1600]{1,0:T(8,128)} fusion(f32[320,1600]{1,0:T(8,128)} %convert_element_type.106, s32[1024]{0:T(1024)S(1)} %pad_clamp_fusion.5), kind=kCustom, calls=%fused_computation.9 | custom fusion | bytes 3277824 | tf_op jit(solution)/shard_map/gather | solution.py:123
  62.1 4.9 %gather_fusion.8 = f32[256,1600]{1,0:T(8,128)} fusion(f32[320,1600]{1,0:T(8,128)} %convert_element_type.106, s32[1024]{0:T(1024)S(1)} %get-tuple-element.78), kind=kCustom, calls=%fused_computation.8 | custom fusion | bytes 3277824 | tf_op jit(solution)/shard_map/gather | solution.py:123
  67.0 4.8 %gather_fusion.7 = f32[256,1600]{1,0:T(8,128)} fusion(f32[320,1600]{1,0:T(8,128)} %convert_element_type.106, s32[1024]{0:T(1024)S(1)} %get-tuple-element.79), kind=kCustom, calls=%fused_computation.7 | custom fusion | bytes 3277824 | tf_op jit(solution)/shard_map/gather | solution.py:123
  71.8 5.0 %gather_fusion.6 = f32[256,1600]{1,0:T(8,128)} fusion(f32[320,1600]{1,0:T(8,128)} %convert_element_type.106, s32[1024]{0:T(1024)S(1)} %get-tuple-element.80), kind=kCustom, calls=%fused_computation.6 | custom fusion | bytes 3277824 | tf_op jit(solution)/shard_map/gather | solution.py:123
  76.9 4.8 %gather_fusion.5 = f32[256,1600]{1,0:T(8,128)} fusion(f32[320,1600]{1,0:T(8,128)} %convert_element_type.106, s32[1024]{0:T(1024)S(1)} %get-tuple-element.81), kind=kCustom, calls=%fused_computation.5 | custom fusion | bytes 3277824 | tf_op jit(solution)/shard_map/gather | solution.py:123
  81.7 4.8 %gather_fusion.2 = f32[256,1600]{1,0:T(8,128)} fusion(f32[320,1600]{1,0:T(8,128)} %convert_element_type.106, s32[1024]{0:T(1024)S(1)} %pad_clamp_fusion.12), kind=kCustom, calls=%fused_computation.2 | custom fusion | bytes 3277824 | tf_op jit(solution)/shard_map/gather | solution.py:123
  86.6 4.9 %gather_fusion.1 = f32[256,1600]{1,0:T(8,128)} fusion(f32[320,1600]{1,0:T(8,128)} %convert_element_type.106, s32[1024]{0:T(1024)S(1)} %pad_clamp_fusion.13), kind=kCustom, calls=%fused_computation.1 | custom fusion | bytes 3277824 | tf_op jit(solution)/shard_map/gather | solution.py:123
  101.9 4.2 %collective-permute-start.2 = (bf16[256,1600]{0,1:T(8,128)(2,1)}, bf16[256,1600]{0,1:T(8,128)(2,1)}, u32[]{:S(2)}, u32[]{:S(2)}) collective-permute-start(bf16[256,1600]{0,1:T(8,128)(2,1)} %copy.60), channel_id=1, source_target_pairs={{0,3},{1,2},{2,1},{3,0},{4,7},{5,6},{6,5},{7,4},{8,11},{9,10},{10,... | collective-permute-start | bytes 2457608 | tf_op jit(solution)/shard_map/ppermute | solution.py:73
  111.7 10.1 %all-to-all-start.1 = ((bf16[32,50,400]{2,1,0:T(8,128)(2,1)}), bf16[32,50,400]{2,1,0:T(8,128)(2,1)}, u32[]{:S(2)}, u32[]{:S(2)}) async-start(bf16[32,50,400]{2,1,0:T(8,128)(2,1)} %broadcast_in_dim.257), calls=%async_computation.1 | async-start | bytes 3670016 | tf_op jit(solution)/shard_map/all_to_all | solution.py:67
  127.9 15.1 %collective-permute-done.1 = bf16[256,1600]{0,1:T(8,128)(2,1)S(1)} collective-permute-done((bf16[256,1600]{0,1:T(8,128)(2,1)}, bf16[256,1600]{0,1:T(8,128)(2,1)S(1)}, u32[]{:S(2)}, u32[]{:S(2)}) %collective-permute-start.1) | collective-permute-done | bytes 819232 | tf_op jit(solution)/shard_map/ppermute | solution.py:73
  144.3 5.1 %fusion.77 = (f32[256]{0:T(256)S(1)}, f32[256,1600]{1,0:T(8,128)S(1)}, f32[256]{0:T(256)S(1)}, f32[256,1600]{1,0:T(8,128)}) fusion(f32[256,1600]{1,0:T(8,128)} %gather_fusion.12, f32[256,1600]{1,0:T(8,128)} %gather_fusion.11, bf16[256,1600]{1,0:T(8,128)(2,1)} %copy.65, f32[256,1600]{1,0:T(8,128)} %gather_fusion.10, f32[256,1600]{1,0:T(8,128)} %gather_fusion.9, ...), kind=kLoop, calls=%fused_computation.255 | loop fusion | flops 3276288 | bytes 11470848 | tf_op jit(solution)/shard_map/reduce_sum | solution.py:14
  149.4 2.7 %copy.61 = bf16[256,1600]{1,0:T(8,128)(2,1)} copy(bf16[256,1600]{0,1:T(8,128)(2,1)} %collective-permute-done) | data formatting | bytes 1638400 | tf_op jit(solution)/shard_map/ppermute | solution.py:73
  157.7 8.5 %all-to-all-done.1 = bf16[32,50,400]{2,1,0:T(8,128)(2,1)} async-done(((bf16[32,50,400]{2,1,0:T(8,128)(2,1)}), bf16[32,50,400]{2,1,0:T(8,128)(2,1)}, u32[]{:S(2)}, u32[]{:S(2)}) %all-to-all-start.1) | async-done | bytes 1280032 | tf_op jit(solution)/shard_map/all_to_all | solution.py:67
  166.2 3.7 %reshape.920 = bf16[1600,400]{1,0:T(8,128)(2,1)} reshape(bf16[32,50,400]{2,1,0:T(8,128)(2,1)} %all-to-all-done.1) | data formatting | bytes 2560000 | tf_op jit(solution)/shard_map/reshape | solution.py:115
  190.3 4.1 %gather_fusion.13 = bf16[1280,200]{1,0:T(8,128)(2,1)S(1)} fusion(bf16[1280,200]{1,0:T(8,128)(2,1)S(1)} %copy.66, s32[2048]{0:T(1024)S(1)} %pad_clamp_fusion), kind=kCustom, calls=%fused_computation.13 | custom fusion | bytes 1029120 | tf_op jit(solution)/shard_map/gather | solution.py:136
  197.0 3.3 %collective-permute-start.3 = (f32[4,32,320]{2,1,0:T(8,128)S(1)}, f32[4,32,320]{2,1,0:T(8,128)}, u32[]{:S(2)}, u32[]{:S(2)}) collective-permute-start(f32[4,32,320]{2,1,0:T(8,128)S(1)} %fusion.25), channel_id=1, source_target_pairs={{1,0},{2,1},{3,2},{4,3},{5,4},{6,5},{7,6},{8,7},{9,8},{10,9},{11,1... | collective-permute-start | bytes 491528 | tf_op jit(solution)/shard_map/ppermute | solution.py:163
  201.3 2.9 %collective-permute-start.4 = (f32[4,32,320]{2,1,0:T(8,128)}, f32[4,32,320]{2,1,0:T(8,128)}, u32[]{:S(2)}, u32[]{:S(2)}) collective-permute-start(f32[4,32,320]{2,1,0:T(8,128)} %get-tuple-element.68), channel_id=1, source_target_pairs={{0,1},{1,2},{2,3},{3,4},{4,5},{5,6},{6,7},{7,8},{8,9},{9,10},{10,1... | collective-permute-start | bytes 491528 | tf_op jit(solution)/shard_map/ppermute | solution.py:162
  211.9 17.2 %all-to-all-start.2 = ((f32[16,128,100]{1,2,0:T(8,128)}), f32[16,128,100]{1,2,0:T(8,128)S(1)}, u32[]{:S(2)}, u32[]{:S(2)}) async-start(f32[16,128,100]{1,2,0:T(8,128)} %convolution_bitcast_fusion), calls=%async_computation.2 | async-start | bytes 1703936 | tf_op jit(solution)/shard_map/all_to_all | solution.py:183
  240.6 14.6 %all-to-all-done.2 = f32[16,128,100]{1,2,0:T(8,128)S(1)} async-done(((f32[16,128,100]{1,2,0:T(8,128)}), f32[16,128,100]{1,2,0:T(8,128)S(1)}, u32[]{:S(2)}, u32[]{:S(2)}) %all-to-all-start.2) | async-done | bytes 819232 | tf_op jit(solution)/shard_map/all_to_all | solution.py:183
  (264 shorter events, 97.9 us)
Async XLA Ops:
  6.4 15.7 %copy-start.17 = (s32[128,32]{0,1:T(8,128)S(1)}, s32[128,32]{0,1:T(8,128)}, u32[]{:S(2)}) copy-start(s32[128,32]{0,1:T(8,128)} %param.17) | copy-start | bytes 49156
  6.4 90.8 %all-to-all-start = ((bf16[32,16,1600]{2,1,0:T(8,128)(2,1)}), bf16[32,16,1600]{2,1,0:T(8,128)(2,1)S(1)}, u32[]{:S(2)}, u32[]{:S(2)}) async-start(bf16[32,16,1600]{2,1,0:T(8,128)(2,1)} %broadcast_select_fusion), calls=%async_computation | async-start | bytes 3407872 | tf_op jit(solution)/shard_map/all_to_all | solution.py:65
  20.0 15.0 %copy-start.21 = (bf16[1600]{0:T(1024)(128)(2,1)S(1)}, bf16[1600]{0:T(1024)(128)(2,1)}, u32[]{:S(2)}) copy-start(bf16[1600]{0:T(1024)(128)(2,1)} %param.11) | copy-start | bytes 9604
  20.0 16.4 %copy-start.16 = (bf16[50,2,100]{2,1,0:T(2,128)(2,1)S(1)}, bf16[50,2,100]{2,1,0:T(2,128)(2,1)}, u32[]{:S(2)}) copy-start(bf16[50,2,100]{2,1,0:T(2,128)(2,1)} %param.13) | copy-start | bytes 60004
  47.4 5.0 %copy-start.22 = (s32[256,1]{0,1:T(1,128)S(1)}, s32[256,1]{0,1:T(1,128)}, u32[]{:S(2)}) copy-start(s32[256,1]{0,1:T(1,128)} %get-tuple-element.38) | copy-start | bytes 3076
  47.4 5.0 %copy-start.23 = (s32[256,1]{0,1:T(1,128)S(1)}, s32[256,1]{0,1:T(1,128)}, u32[]{:S(2)}) copy-start(s32[256,1]{0,1:T(1,128)} %tile.19) | copy-start | bytes 3076
  76.9 4.8 %copy-start.26 = (s32[256,1]{0,1:T(1,128)S(1)}, s32[256,1]{0,1:T(1,128)}, u32[]{:S(2)}) copy-start(s32[256,1]{0,1:T(1,128)} %get-tuple-element.63) | copy-start | bytes 3076
  81.7 4.8 %copy-start.25 = (s32[256,1]{0,1:T(1,128)S(1)}, s32[256,1]{0,1:T(1,128)}, u32[]{:S(2)}) copy-start(s32[256,1]{0,1:T(1,128)} %get-tuple-element.64) | copy-start | bytes 3076
  86.6 4.9 %copy-start.33 = (s32[32,4]{0,1:T(4,128)S(1)}, s32[32,4]{0,1:T(4,128)}, u32[]{:S(2)}) copy-start(s32[32,4]{0,1:T(4,128)} %param.16) | copy-start | bytes 1540
  86.6 6.2 %copy-start.24 = (s32[256,1]{0,1:T(1,128)S(1)}, s32[256,1]{0,1:T(1,128)}, u32[]{:S(2)}) copy-start(s32[256,1]{0,1:T(1,128)} %add.736) | copy-start | bytes 3076
  86.6 6.9 %copy-start.18 = (bf16[100,50]{0,1:T(8,128)(2,1)S(1)}, bf16[100,50]{0,1:T(8,128)(2,1)}, u32[]{:S(2)}) copy-start(bf16[100,50]{0,1:T(8,128)(2,1)} %param.14) | copy-start | bytes 30004
  86.6 6.9 %copy-start.19 = (bf16[50,100]{1,0:T(8,128)(2,1)S(1)}, bf16[50,100]{1,0:T(8,128)(2,1)}, u32[]{:S(2)}) copy-start(bf16[50,100]{1,0:T(8,128)(2,1)} %param.12) | copy-start | bytes 30004
  101.9 23.8 %collective-permute-start.2 = (bf16[256,1600]{0,1:T(8,128)(2,1)}, bf16[256,1600]{0,1:T(8,128)(2,1)}, u32[]{:S(2)}, u32[]{:S(2)}) collective-permute-start(bf16[256,1600]{0,1:T(8,128)(2,1)} %copy.60), channel_id=1, source_target_pairs={{0,3},{1,2},{2,1},{3,0},{4,7},{5,6},{6,5},{7,4},{8,11},{9,10},{10,... | collective-permute-start | bytes 2457608 | tf_op jit(solution)/shard_map/ppermute | solution.py:73
  106.1 36.8 %collective-permute-start.1 = (bf16[256,1600]{0,1:T(8,128)(2,1)}, bf16[256,1600]{0,1:T(8,128)(2,1)S(1)}, u32[]{:S(2)}, u32[]{:S(2)}) collective-permute-start(bf16[256,1600]{0,1:T(8,128)(2,1)} %copy.60), channel_id=1, source_target_pairs={{0,2},{1,3},{2,0},{3,1},{4,6},{5,7},{6,4},{7,5},{8,10},{9,11},{10,... | collective-permute-start | bytes 2457608 | tf_op jit(solution)/shard_map/ppermute | solution.py:73
  108.3 41.2 %collective-permute-start = (bf16[256,1600]{0,1:T(8,128)(2,1)}, bf16[256,1600]{0,1:T(8,128)(2,1)}, u32[]{:S(2)}, u32[]{:S(2)}) collective-permute-start(bf16[256,1600]{0,1:T(8,128)(2,1)} %copy.60), channel_id=1, source_target_pairs={{0,1},{1,0},{2,3},{3,2},{4,5},{5,4},{6,7},{7,6},{8,9},{9,8},{10,11... | collective-permute-start | bytes 2457608 | tf_op jit(solution)/shard_map/ppermute | solution.py:73
  111.7 10.1 %copy-start.1 = (bf16[256,1600]{1,0:T(8,128)(2,1)S(1)}, bf16[256,1600]{1,0:T(8,128)(2,1)}, u32[]{:S(2)}) copy-start(bf16[256,1600]{1,0:T(8,128)(2,1)} %gather_fusion.4) | copy-start | bytes 2457604
  111.7 54.5 %all-to-all-start.1 = ((bf16[32,50,400]{2,1,0:T(8,128)(2,1)}), bf16[32,50,400]{2,1,0:T(8,128)(2,1)}, u32[]{:S(2)}, u32[]{:S(2)}) async-start(bf16[32,50,400]{2,1,0:T(8,128)(2,1)} %broadcast_in_dim.257), calls=%async_computation.1 | async-start | bytes 3670016 | tf_op jit(solution)/shard_map/all_to_all | solution.py:67
  149.4 24.4 %copy-start.2 = (f32[256,1600]{1,0:T(8,128)}, f32[256,1600]{1,0:T(8,128)S(1)}, u32[]{:S(2)}) copy-start(f32[256,1600]{1,0:T(8,128)S(1)} %get-tuple-element.36) | copy-start | bytes 4915204
  157.7 12.2 %copy-start.20 = (f32[1600]{0:T(1024)S(1)}, f32[1600]{0:T(1024)}, u32[]{:S(2)}) copy-start(f32[1600]{0:T(1024)} %convert_element_type.107) | copy-start | bytes 19204
  175.3 5.8 %copy-start.12 = (bf16[256,300]{0,1:T(8,128)(2,1)}, bf16[256,300]{0,1:T(8,128)(2,1)S(1)}, u32[]{:S(2)}) copy-start(bf16[256,300]{0,1:T(8,128)(2,1)S(1)} %convolution_convert_fusion) | copy-start | bytes 460804
  194.8 5.6 %copy-start.27 = (pred[100]{0:T(512)(128)(4,1)S(1)}, pred[100]{0:T(512)(128)(4,1)}, u32[]{:S(2)}) copy-start(pred[100]{0:T(512)(128)(4,1)} %get-tuple-element.75) | copy-start | bytes 304
  197.0 10.5 %collective-permute-start.3 = (f32[4,32,320]{2,1,0:T(8,128)S(1)}, f32[4,32,320]{2,1,0:T(8,128)}, u32[]{:S(2)}, u32[]{:S(2)}) collective-permute-start(f32[4,32,320]{2,1,0:T(8,128)S(1)} %fusion.25), channel_id=1, source_target_pairs={{1,0},{2,1},{3,2},{4,3},{5,4},{6,5},{7,6},{8,7},{9,8},{10,9},{11,1... | collective-permute-start | bytes 491528 | tf_op jit(solution)/shard_map/ppermute | solution.py:163
  201.3 6.2 %collective-permute-start.4 = (f32[4,32,320]{2,1,0:T(8,128)}, f32[4,32,320]{2,1,0:T(8,128)}, u32[]{:S(2)}, u32[]{:S(2)}) collective-permute-start(f32[4,32,320]{2,1,0:T(8,128)} %get-tuple-element.68), channel_id=1, source_target_pairs={{0,1},{1,2},{2,3},{3,4},{4,5},{5,6},{6,7},{7,8},{8,9},{9,10},{10,1... | collective-permute-start | bytes 491528 | tf_op jit(solution)/shard_map/ppermute | solution.py:162
  211.9 43.3 %all-to-all-start.2 = ((f32[16,128,100]{1,2,0:T(8,128)}), f32[16,128,100]{1,2,0:T(8,128)S(1)}, u32[]{:S(2)}, u32[]{:S(2)}) async-start(f32[16,128,100]{1,2,0:T(8,128)} %convolution_bitcast_fusion), calls=%async_computation.2 | async-start | bytes 1703936 | tf_op jit(solution)/shard_map/all_to_all | solution.py:183
  (23 other events, 48.0 us)

commit v3 on v2

--- a/solution.py
+++ b/solution.py
@@ -76,11 +76,11 @@
     near = store_rows[near_rows]
     blocks = [near]
     refs = [jnp.repeat(local_ref, group_len)]
-    toks = [jnp.tile(jnp.arange(group_len, dtype=jnp.int32), local_count)]
+    toks = [(0, group_len)]
     for m in range(split):
         blocks.append(pieces[m])
         refs.append(jnp.repeat(compact_ref, part))
-        toks.append(jnp.tile((own_part ^ m) * part + tok_ids, REM_DEV))
+        toks.append(((own_part ^ m) * part, part))
     tok_all = jnp.arange(group_len, dtype=jnp.int32)[None, :]
     remote_row = local_count * group_len + (
         ((tok_all // part) ^ own_part) * REM_DEV * part + ordinal[:, None] * part + tok_all % part
@@ -116,11 +116,15 @@
     w_cat = allw[:, : 3 * narrow]
     out_rows = allw[:, 3 * narrow:]
 
-    pos_f = positions.astype(jnp.float32)
     out_kv, out_q, out_sh = [], [], []
-    for block, ref, tok in zip(blocks, refs, toks):
+    for block, ref, (tok_start, tok_len) in zip(blocks, refs, toks):
+        groups_in = block.shape[0] // tok_len
+        tok = tok_start + jnp.tile(jnp.arange(tok_len, dtype=jnp.int32), groups_in)
         place = (ref % group_count) * group_len + tok
-        shifted = block.astype(jnp.float32) + pos_f[place] - pos_f[tok]
+        pos_place = positions[place].astype(jnp.float32)
+        pos_tok = lax.dynamic_slice_in_dim(positions, tok_start, tok_len, 0).astype(jnp.float32)
+        pos_tok = jnp.broadcast_to(pos_tok[None], (groups_in, tok_len, full_width)).reshape(block.shape)
+        shifted = block.astype(jnp.float32) + pos_place - pos_tok
         normed = layer_norm(shifted, ln_gain).astype(jnp.bfloat16)
         both = jnp.dot(normed, w_cat, preferred_element_type=jnp.float32).astype(jnp.bfloat16)
         out_kv.append(both[:, : 2 * narrow])

time: 261 us -> 214 us (0.82); the launches traced: 256 us -> 213 us
  local copies, waits for them, and re-layouts: 119 us -> 71.4 us
  waiting for transfers between devices: 38.2 us -> 61.2 us
  other arithmetic: 32.2 us -> 16.8 us
  starting transfers between devices: 55.5 us -> 52 us
    gather x10 -> x5, local copies, waits for them, and re-layouts: 49 us -> 11.3 us  [per_device(): pos_place = positions[place].astype(jnp.float32)]
    all_to_all x1, waiting for transfers between devices: 0.01 us -> 16.1 us  [fetch_groups(): lax.all_to_all(sent, 'row', split_axis=0, concat_axis=0, tiled=True)]
    reduce_sum x4, other arithmetic: 11.4 us -> 5.4 us  [layer_norm(): center = shifted - jnp.mean(shifted, axis=-1, keepdims=True)]
    ppermute x3, waiting for transfers between devices: 15.1 us -> 19.9 us  [fetch_groups(): lax.ppermute(compact, 'col', [(c, c ^ m) for c in range(col_count)])]
    unnamed x92 -> x86, local copies, waits for them, and re-layouts: 22.7 us -> 18.9 us
    all_to_all x1, starting transfers between devices: 10.1 us -> 6.58 us  [fetch_groups(): lax.all_to_all(jnp.broadcast_to(extra[None], (row_count,) + extra.shape),...]
  transfers between devices with their start and end apart: 8 -> 8, of which waited for: 3 -> 5; matrix products, arithmetic and copies ran while one was open for 43% -> 25% of each run, Pallas kernels for 0% -> 0%
where the time goes in v3:
time: 214 us; the launch traced here: 213 us
  local copies, waits for them, and re-layouts  71.4 us (33%)
  waiting for transfers between devices  61.2 us (29%)
  starting transfers between devices  52 us (24%)
  other arithmetic  16.8 us (8%)
  matrix products  10 us (5%)
    ppermute x3, waiting for transfers between devices, fetch_groups(): lax.ppermute(compact, 'col', [(c, c ^ m) for c in range(col_count)])  19.9 us
    unnamed x86, local copies, waits for them, and re-layouts  18.9 us
    all_to_all x1, starting transfers between devices, per_device(): lax.all_to_all(projected, 'col', 0, 0, tiled=True)  16.5 us
    all_to_all x1, waiting for transfers between devices, fetch_groups(): lax.all_to_all(sent, 'row', split_axis=0, concat_axis=0, tiled=True)  16.1 us
    all_to_all x1, waiting for transfers between devices, per_device(): lax.all_to_all(projected, 'col', 0, 0, tiled=True)  14.5 us
    all_to_all x1, starting transfers between devices, fetch_groups(): lax.all_to_all(sent, 'row', split_axis=0, concat_axis=0, tiled=True)  13.6 us
    gather x5, local copies, waits for them, and re-layouts, per_device(): pos_place = positions[place].astype(jnp.float32)  11.3 us
    all_to_all x1, waiting for transfers between devices, fetch_groups(): lax.all_to_all(jnp.broadcast_to(extra[None], (row_count,) + extra.shape),...  10.7 us
  transfers between devices with their start and end apart: 8, of which 5 were waited for; matrix products, arithmetic and copies ran while one was open for 25% of the time, Pallas kernels for 0%

profile of v3, /device:TPU:9, one launch (start us, length us, event | category | flops | bytes accessed | tf_op | source)
XLA Modules:
  0.0 213.0 jit_solution(10926901126824193982)
XLA Ops:
  2.6 2.3 %gather_fusion.2 = bf16[512,1600]{1,0:T(8,128)(2,1)S(1)} fusion(bf16[512,1600]{1,0:T(8,128)(2,1)S(1)} %bitcast.75, s32[1024]{0:T(1024)S(1)} %pad_clamp_fusion.7), kind=kCustom, calls=%fused_computation.2 | custom fusion | bytes 3278848 | tf_op jit(solution)/shard_map/gather | solution.py:62
  6.4 13.6 %all-to-all-start = ((bf16[32,16,1600]{2,1,0:T(8,128)(2,1)}), bf16[32,16,1600]{2,1,0:T(8,128)(2,1)}, u32[]{:S(2)}, u32[]{:S(2)}) async-start(bf16[32,16,1600]{2,1,0:T(8,128)(2,1)} %broadcast_select_fusion), calls=%async_computation | async-start | bytes 3407872 | tf_op jit(solution)/shard_map/all_to_all | solution.py:65
  27.4 2.3 %gather_fusion = bf16[256,1600]{1,0:T(8,128)(2,1)} fusion(bf16[512,1600]{1,0:T(8,128)(2,1)S(1)} %bitcast.74, s32[1024]{0:T(1024)S(1)} %pad_clamp_fusion.9), kind=kCustom, calls=%fused_computation | custom fusion | bytes 1639424 | tf_op jit(solution)/shard_map/gather | solution.py:76
  29.8 2.2 %gather_fusion.1 = bf16[256,1600]{1,0:T(8,128)(2,1)} fusion(bf16[320,1600]{1,0:T(8,128)(2,1)S(1)} %copy-done.1, s32[1024]{0:T(1024)S(1)} %pad_clamp_fusion.8), kind=kCustom, calls=%fused_computation.1 | custom fusion | bytes 1639424 | tf_op jit(solution)/shard_map/gather | solution.py:124
  32.0 2.3 %gather_fusion.4 = bf16[256,1600]{1,0:T(8,128)(2,1)} fusion(bf16[320,1600]{1,0:T(8,128)(2,1)S(1)} %copy-done.1, s32[1024]{0:T(1024)S(1)} %pad_clamp_fusion.5), kind=kCustom, calls=%fused_computation.4 | custom fusion | bytes 1639424 | tf_op jit(solution)/shard_map/gather | solution.py:124
  34.3 2.2 %gather_fusion.7 = bf16[256,1600]{1,0:T(8,128)(2,1)} fusion(bf16[320,1600]{1,0:T(8,128)(2,1)S(1)} %copy-done.1, s32[1024]{0:T(1024)S(1)} %pad_clamp_fusion.2), kind=kCustom, calls=%fused_computation.7 | custom fusion | bytes 1639424 | tf_op jit(solution)/shard_map/gather | solution.py:124
  36.6 2.3 %gather_fusion.6 = bf16[256,1600]{1,0:T(8,128)(2,1)} fusion(bf16[320,1600]{1,0:T(8,128)(2,1)S(1)} %copy-done.1, s32[1024]{0:T(1024)S(1)} %pad_clamp_fusion.3), kind=kCustom, calls=%fused_computation.6 | custom fusion | bytes 1639424 | tf_op jit(solution)/shard_map/gather | solution.py:124
  38.9 2.2 %gather_fusion.5 = bf16[256,1600]{1,0:T(8,128)(2,1)} fusion(bf16[320,1600]{1,0:T(8,128)(2,1)S(1)} %copy-done.1, s32[1024]{0:T(1024)S(1)} %pad_clamp_fusion.4), kind=kCustom, calls=%fused_computation.5 | custom fusion | bytes 1639424 | tf_op jit(solution)/shard_map/gather | solution.py:124
  45.9 16.1 %all-to-all-done = bf16[32,16,1600]{2,1,0:T(8,128)(2,1)} async-done(((bf16[32,16,1600]{2,1,0:T(8,128)(2,1)}), bf16[32,16,1600]{2,1,0:T(8,128)(2,1)}, u32[]{:S(2)}, u32[]{:S(2)}) %all-to-all-start) | async-done | bytes 1638432 | tf_op jit(solution)/shard_map/all_to_all | solution.py:65
  62.0 3.8 %gather_fusion.3 = bf16[256,1600]{1,0:T(8,128)(2,1)S(1)} fusion(bf16[512,1600]{1,0:T(8,128)(2,1)} %bitcast.11, s32[1024]{0:T(1024)S(1)} %pad_clamp_fusion.6), kind=kCustom, calls=%fused_computation.3 | custom fusion | bytes 1639424 | tf_op jit(solution)/shard_map/gather | solution.py:71
  67.2 4.7 %collective-permute-start.2 = (bf16[256,1600]{0,1:T(8,128)(2,1)}, bf16[256,1600]{0,1:T(8,128)(2,1)}, u32[]{:S(2)}, u32[]{:S(2)}) collective-permute-start(bf16[256,1600]{0,1:T(8,128)(2,1)} %copy.60), channel_id=1, source_target_pairs={{0,3},{1,2},{2,1},{3,0},{4,7},{5,6},{6,5},{7,4},{8,11},{9,10},{10,... | collective-permute-start | bytes 2457608 | tf_op jit(solution)/shard_map/ppermute | solution.py:73
  71.9 2.2 %collective-permute-start.1 = (bf16[256,1600]{0,1:T(8,128)(2,1)}, bf16[256,1600]{0,1:T(8,128)(2,1)}, u32[]{:S(2)}, u32[]{:S(2)}) collective-permute-start(bf16[256,1600]{0,1:T(8,128)(2,1)} %copy.60), channel_id=1, source_target_pairs={{0,2},{1,3},{2,0},{3,1},{4,6},{5,7},{6,4},{7,5},{8,10},{9,11},{10,... | collective-permute-start | bytes 2457608 | tf_op jit(solution)/shard_map/ppermute | solution.py:73
  77.5 6.6 %all-to-all-start.1 = ((bf16[32,50,400]{2,1,0:T(8,128)(2,1)}), bf16[32,50,400]{2,1,0:T(8,128)(2,1)}, u32[]{:S(2)}, u32[]{:S(2)}) async-start(bf16[32,50,400]{2,1,0:T(8,128)(2,1)} %broadcast_in_dim.283), calls=%async_computation.1 | async-start | bytes 3670016 | tf_op jit(solution)/shard_map/all_to_all | solution.py:67
  87.3 3.9 %collective-permute-done.2 = bf16[256,1600]{0,1:T(8,128)(2,1)} collective-permute-done((bf16[256,1600]{0,1:T(8,128)(2,1)}, bf16[256,1600]{0,1:T(8,128)(2,1)}, u32[]{:S(2)}, u32[]{:S(2)}) %collective-permute-start.2) | collective-permute-done | bytes 819232 | tf_op jit(solution)/shard_map/ppermute | solution.py:73
  92.8 15.9 %collective-permute-done.1 = bf16[256,1600]{0,1:T(8,128)(2,1)} collective-permute-done((bf16[256,1600]{0,1:T(8,128)(2,1)}, bf16[256,1600]{0,1:T(8,128)(2,1)}, u32[]{:S(2)}, u32[]{:S(2)}) %collective-permute-start.1) | collective-permute-done | bytes 819232 | tf_op jit(solution)/shard_map/ppermute | solution.py:73
  110.2 2.2 %copy.61 = bf16[256,1600]{1,0:T(8,128)(2,1)} copy(bf16[256,1600]{0,1:T(8,128)(2,1)} %collective-permute-done) | data formatting | bytes 1638400 | tf_op jit(solution)/shard_map/ppermute | solution.py:73
  117.9 10.7 %all-to-all-done.1 = bf16[32,50,400]{2,1,0:T(8,128)(2,1)} async-done(((bf16[32,50,400]{2,1,0:T(8,128)(2,1)}), bf16[32,50,400]{2,1,0:T(8,128)(2,1)}, u32[]{:S(2)}, u32[]{:S(2)}) %all-to-all-start.1) | async-done | bytes 1280032 | tf_op jit(solution)/shard_map/all_to_all | solution.py:67
  128.6 3.7 %reshape.893 = bf16[1600,400]{1,0:T(8,128)(2,1)} reshape(bf16[32,50,400]{2,1,0:T(8,128)(2,1)} %all-to-all-done.1) | data formatting | bytes 2560000 | tf_op jit(solution)/shard_map/reshape | solution.py:115
  132.3 2.7 %convolution_convert_fusion.4 = bf16[256,300]{0,1:T(8,128)(2,1)S(1)} fusion(f32[256,1600]{1,0:T(8,128)} %copy-done.5, f32[1600]{0:T(1024)S(1)} %convert_element_type.167, f32[256]{0:T(256)S(1)} %copy-done.32, f32[256]{0:T(256)S(1)} %broadcast_multiply_fusion.4, bf16[1600,400]{1,0:T(8,128)(2,1)} %reshape.893), kind=kOutput, calls=%fused_computation.33 | convolution fusion | flops 247475200 | bytes 3094784 | tf_op jit(solution)/shard_map/dot_general | solution.py:129
  146.6 4.1 %gather_fusion.8 = bf16[1280,200]{1,0:T(8,128)(2,1)S(1)} fusion(bf16[1280,200]{1,0:T(8,128)(2,1)S(1)} %copy.66, s32[2048]{0:T(1024)S(1)} %pad_clamp_fusion), kind=kCustom, calls=%fused_computation.8 | custom fusion | bytes 1029120 | tf_op jit(solution)/shard_map/gather | solution.py:140
  153.3 3.5 %collective-permute-start.3 = (f32[4,32,320]{2,1,0:T(8,128)S(1)}, f32[4,32,320]{2,1,0:T(8,128)}, u32[]{:S(2)}, u32[]{:S(2)}) collective-permute-start(f32[4,32,320]{2,1,0:T(8,128)S(1)} %fusion.25), channel_id=1, source_target_pairs={{1,0},{2,1},{3,2},{4,3},{5,4},{6,5},{7,6},{8,7},{9,8},{10,9},{11,1... | collective-permute-start | bytes 491528 | tf_op jit(solution)/shard_map/ppermute | solution.py:167
  157.8 2.9 %collective-permute-start.4 = (f32[4,32,320]{2,1,0:T(8,128)}, f32[4,32,320]{2,1,0:T(8,128)S(1)}, u32[]{:S(2)}, u32[]{:S(2)}) collective-permute-start(f32[4,32,320]{2,1,0:T(8,128)} %get-tuple-element.67), channel_id=1, source_target_pairs={{0,1},{1,2},{2,3},{3,4},{4,5},{5,6},{6,7},{7,8},{8,9},{9,10},{10,1... | collective-permute-start | bytes 491528 | tf_op jit(solution)/shard_map/ppermute | solution.py:166
  169.6 16.5 %all-to-all-start.2 = ((f32[16,128,100]{1,2,0:T(8,128)}), f32[16,128,100]{1,2,0:T(8,128)S(1)}, u32[]{:S(2)}, u32[]{:S(2)}) async-start(f32[16,128,100]{1,2,0:T(8,128)} %convolution_bitcast_fusion), calls=%async_computation.2 | async-start | bytes 1703936 | tf_op jit(solution)/shard_map/all_to_all | solution.py:187
  197.7 14.5 %all-to-all-done.2 = f32[16,128,100]{1,2,0:T(8,128)S(1)} async-done(((f32[16,128,100]{1,2,0:T(8,128)}), f32[16,128,100]{1,2,0:T(8,128)S(1)}, u32[]{:S(2)}, u32[]{:S(2)}) %all-to-all-start.2) | async-done | bytes 819232 | tf_op jit(solution)/shard_map/all_to_all | solution.py:187
  (247 shorter events, 67.8 us)
Async XLA Ops:
  6.4 13.8 %copy-start.26 = (bf16[1600]{0:T(1024)(128)(2,1)S(1)}, bf16[1600]{0:T(1024)(128)(2,1)}, u32[]{:S(2)}) copy-start(bf16[1600]{0:T(1024)(128)(2,1)} %param.11) | copy-start | bytes 9604
  6.4 14.4 %copy-start.19 = (bf16[50,2,100]{2,1,0:T(2,128)(2,1)S(1)}, bf16[50,2,100]{2,1,0:T(2,128)(2,1)}, u32[]{:S(2)}) copy-start(bf16[50,2,100]{2,1,0:T(2,128)(2,1)} %param.13) | copy-start | bytes 60004
  6.4 14.5 %copy-start.23 = (s32[128,32]{0,1:T(8,128)S(1)}, s32[128,32]{0,1:T(8,128)}, u32[]{:S(2)}) copy-start(s32[128,32]{0,1:T(8,128)} %param.17) | copy-start | bytes 49156
  6.4 55.7 %all-to-all-start = ((bf16[32,16,1600]{2,1,0:T(8,128)(2,1)}), bf16[32,16,1600]{2,1,0:T(8,128)(2,1)}, u32[]{:S(2)}, u32[]{:S(2)}) async-start(bf16[32,16,1600]{2,1,0:T(8,128)(2,1)} %broadcast_select_fusion), calls=%async_computation | async-start | bytes 3407872 | tf_op jit(solution)/shard_map/all_to_all | solution.py:65
  44.0 109.0 %copy-start.29 = (pred[100]{0:T(512)(128)(4,1)}, pred[100]{0:T(512)(128)(4,1)S(1)}, u32[]{:S(2)}) copy-start(pred[100]{0:T(512)(128)(4,1)S(1)} %get-tuple-element.73) | copy-start | bytes 304
  44.0 112.7 %copy-start.27 = (pred[100]{0:T(512)(128)(4,1)}, pred[100]{0:T(512)(128)(4,1)S(1)}, u32[]{:S(2)}) copy-start(pred[100]{0:T(512)(128)(4,1)S(1)} %get-tuple-element.74) | copy-start | bytes 304
  44.1 107.8 %copy-start.21 = (s32[1024]{0:T(1024)}, s32[1024]{0:T(1024)S(1)}, u32[]{:S(2)}) copy-start(s32[1024]{0:T(1024)S(1)} %pad_clamp_fusion.1) | copy-start | bytes 12292
  67.2 24.1 %collective-permute-start.2 = (bf16[256,1600]{0,1:T(8,128)(2,1)}, bf16[256,1600]{0,1:T(8,128)(2,1)}, u32[]{:S(2)}, u32[]{:S(2)}) collective-permute-start(bf16[256,1600]{0,1:T(8,128)(2,1)} %copy.60), channel_id=1, source_target_pairs={{0,3},{1,2},{2,1},{3,0},{4,7},{5,6},{6,5},{7,4},{8,11},{9,10},{10,... | collective-permute-start | bytes 2457608 | tf_op jit(solution)/shard_map/ppermute | solution.py:73
  71.9 36.8 %collective-permute-start.1 = (bf16[256,1600]{0,1:T(8,128)(2,1)}, bf16[256,1600]{0,1:T(8,128)(2,1)}, u32[]{:S(2)}, u32[]{:S(2)}) collective-permute-start(bf16[256,1600]{0,1:T(8,128)(2,1)} %copy.60), channel_id=1, source_target_pairs={{0,2},{1,3},{2,0},{3,1},{4,6},{5,7},{6,4},{7,5},{8,10},{9,11},{10,... | collective-permute-start | bytes 2457608 | tf_op jit(solution)/shard_map/ppermute | solution.py:73
  74.0 36.2 %collective-permute-start = (bf16[256,1600]{0,1:T(8,128)(2,1)}, bf16[256,1600]{0,1:T(8,128)(2,1)}, u32[]{:S(2)}, u32[]{:S(2)}) collective-permute-start(bf16[256,1600]{0,1:T(8,128)(2,1)} %copy.60), channel_id=1, source_target_pairs={{0,1},{1,0},{2,3},{3,2},{4,5},{5,4},{6,7},{7,6},{8,9},{9,8},{10,11... | collective-permute-start | bytes 2457608 | tf_op jit(solution)/shard_map/ppermute | solution.py:73
  77.5 6.6 %copy-start.12 = (bf16[256,1600]{1,0:T(8,128)(2,1)S(1)}, bf16[256,1600]{1,0:T(8,128)(2,1)}, u32[]{:S(2)}) copy-start(bf16[256,1600]{1,0:T(8,128)(2,1)} %gather_fusion.4) | copy-start | bytes 2457604
  77.5 51.1 %all-to-all-start.1 = ((bf16[32,50,400]{2,1,0:T(8,128)(2,1)}), bf16[32,50,400]{2,1,0:T(8,128)(2,1)}, u32[]{:S(2)}, u32[]{:S(2)}) async-start(bf16[32,50,400]{2,1,0:T(8,128)(2,1)} %broadcast_in_dim.283), calls=%async_computation.1 | async-start | bytes 3670016 | tf_op jit(solution)/shard_map/all_to_all | solution.py:67
  117.5 19.4 %copy-start.4 = (f32[256,1600]{1,0:T(8,128)}, f32[256,1600]{1,0:T(8,128)S(1)}, u32[]{:S(2)}) copy-start(f32[256,1600]{1,0:T(8,128)S(1)} %get-tuple-element.42) | copy-start | bytes 4915204
  117.9 14.4 %copy-start.32 = (f32[256]{0:T(256)S(1)}, f32[256]{0:T(256)}, u32[]{:S(2)}) copy-start(f32[256]{0:T(256)} %add_rsqrt_fusion.4) | copy-start | bytes 3076
  132.2 4.0 %copy-start.3 = (f32[256,1600]{1,0:T(8,128)S(1)}, f32[256,1600]{1,0:T(8,128)}, u32[]{:S(2)}) copy-start(f32[256,1600]{1,0:T(8,128)} %copy-done.2) | copy-start | bytes 4915204
  132.2 4.0 %copy-start.13 = (bf16[1600,400]{1,0:T(8,128)(2,1)S(1)}, bf16[1600,400]{1,0:T(8,128)(2,1)}, u32[]{:S(2)}) copy-start(bf16[1600,400]{1,0:T(8,128)(2,1)} %reshape.893) | copy-start | bytes 3840004
  132.2 3.9 %copy-start.33 = (f32[256]{0:T(256)S(1)}, f32[256]{0:T(256)}, u32[]{:S(2)}) copy-start(f32[256]{0:T(256)} %add_rsqrt_fusion.3) | copy-start | bytes 3076
  137.0 3.8 %copy-start.16 = (bf16[256,300]{0,1:T(8,128)(2,1)}, bf16[256,300]{0,1:T(8,128)(2,1)S(1)}, u32[]{:S(2)}) copy-start(bf16[256,300]{0,1:T(8,128)(2,1)S(1)} %convolution_convert_fusion.3) | copy-start | bytes 460804
  140.0 4.5 %copy-start.14 = (bf16[1280,200]{0,1:T(8,128)(2,1)S(1)}, bf16[1280,200]{0,1:T(8,128)(2,1)}, u32[]{:S(2)}) copy-start(bf16[1280,200]{0,1:T(8,128)(2,1)} %slice_dynamic-update-slice_fusion.4) | copy-start | bytes 1536004
  152.6 8.1 %copy-start.18 = (s32[4,32]{0,1:T(8,128)S(1)}, s32[4,32]{0,1:T(8,128)}, u32[]{:S(2)}) copy-start(s32[4,32]{0,1:T(8,128)} %get-tuple-element.32) | copy-start | bytes 1540
  153.3 11.3 %collective-permute-start.3 = (f32[4,32,320]{2,1,0:T(8,128)S(1)}, f32[4,32,320]{2,1,0:T(8,128)}, u32[]{:S(2)}, u32[]{:S(2)}) collective-permute-start(f32[4,32,320]{2,1,0:T(8,128)S(1)} %fusion.25), channel_id=1, source_target_pairs={{1,0},{2,1},{3,2},{4,3},{5,4},{6,5},{7,6},{8,7},{9,8},{10,9},{11,1... | collective-permute-start | bytes 491528 | tf_op jit(solution)/shard_map/ppermute | solution.py:167
  157.8 6.8 %collective-permute-start.4 = (f32[4,32,320]{2,1,0:T(8,128)}, f32[4,32,320]{2,1,0:T(8,128)S(1)}, u32[]{:S(2)}, u32[]{:S(2)}) collective-permute-start(f32[4,32,320]{2,1,0:T(8,128)} %get-tuple-element.67), channel_id=1, source_target_pairs={{0,1},{1,2},{2,3},{3,4},{4,5},{5,6},{6,7},{7,8},{8,9},{9,10},{10,1... | collective-permute-start | bytes 491528 | tf_op jit(solution)/shard_map/ppermute | solution.py:166
  169.6 25.0 %copy-start.22 = (s32[1024]{0:T(1024)S(1)}, s32[1024]{0:T(1024)}, u32[]{:S(2)}) copy-start(s32[1024]{0:T(1024)} %copy-done.21) | copy-start | bytes 12292
  169.6 42.6 %all-to-all-start.2 = ((f32[16,128,100]{1,2,0:T(8,128)}), f32[16,128,100]{1,2,0:T(8,128)S(1)}, u32[]{:S(2)}, u32[]{:S(2)}) async-start(f32[16,128,100]{1,2,0:T(8,128)} %convolution_bitcast_fusion), calls=%async_computation.2 | async-start | bytes 1703936 | tf_op jit(solution)/shard_map/all_to_all | solution.py:187
  (20 other events, 42.6 us)

commit v4 on v3

--- a/solution.py
+++ b/solution.py
@@ -64,9 +64,10 @@
     sent = jnp.where(live_rows[:, :, None], payload, jnp.zeros_like(payload))
     received = lax.all_to_all(sent, "row", split_axis=0, concat_axis=0, tiled=True)
     extra, received = lax.optimization_barrier((extra, received))
+    extra_tiles = extra.reshape(16, -1)
     extra_all = lax.all_to_all(
-        jnp.broadcast_to(extra[None], (row_count,) + extra.shape), "row", 0, 0, tiled=True
-    )
+        jnp.broadcast_to(extra_tiles[None], (row_count,) + extra_tiles.shape), "row", 0, 0, tiled=True
+    ).reshape((row_count,) + extra.shape)
     flat = received.reshape(row_count * capacity * part, full_width)
     compact = flat[(compact_index[:, None] * part + tok_ids).reshape(-1)]
     pieces = [compact] + [

time: 214 us -> 204 us (0.953)
  waiting for transfers between devices: 61.2 us -> 48 us
  other arithmetic: 16.8 us -> 19.1 us
    all_to_all x1, waiting for transfers between devices: 10.7 us -> 0.01 us  [fetch_groups(): lax.all_to_all(jnp.broadcast_to(extra_tiles[None], (row_count,) + extra_t...]
    another operation x0 -> x1, local copies, waits for them, and re-layouts: none -> 4.53 us  [per_device(): allw = allw.reshape(full_width, 4 * narrow)]
    reshape x1 -> x0, local copies, waits for them, and re-layouts: 3.69 us -> none  [per_device(): allw = allw.reshape(full_width, 4 * narrow)]
    all_to_all x1, waiting for transfers between devices: 16.1 us -> 13.4 us  [fetch_groups(): lax.all_to_all(sent, 'row', split_axis=0, concat_axis=0, tiled=True)]
    unnamed x86 -> x94, local copies, waits for them, and re-layouts: 18.9 us -> 18.8 us
  transfers between devices with their start and end apart: 8 -> 8, of which waited for: 5 -> 4; matrix products, arithmetic and copies ran while one was open for 25% -> 28% of each run, Pallas kernels for 0% -> 0%
where the time goes in v4:
time: 204 us; the launch traced here: 202 us
  local copies, waits for them, and re-layouts  72 us (35%)
  starting transfers between devices  51.4 us (25%)
  waiting for transfers between devices  48 us (24%)
  other arithmetic  19.1 us (9%)
  matrix products  10.1 us (5%)
    ppermute x3, waiting for transfers between devices, fetch_groups(): lax.ppermute(compact, 'col', [(c, c ^ m) for c in range(col_count)])  20.5 us
    unnamed x94, local copies, waits for them, and re-layouts  18.8 us
    all_to_all x1, starting transfers between devices, per_device(): lax.all_to_all(projected, 'col', 0, 0, tiled=True)  16.6 us
    all_to_all x1, waiting for transfers between devices, per_device(): lax.all_to_all(projected, 'col', 0, 0, tiled=True)  14.1 us
    all_to_all x1, starting transfers between devices, fetch_groups(): lax.all_to_all(sent, 'row', split_axis=0, concat_axis=0, tiled=True)  13.6 us
    all_to_all x1, waiting for transfers between devices, fetch_groups(): lax.all_to_all(sent, 'row', split_axis=0, concat_axis=0, tiled=True)  13.4 us
    gather x5, local copies, waits for them, and re-layouts, per_device(): pos_place = positions[place].astype(jnp.float32)  11.3 us
    ppermute x3, starting transfers between devices, fetch_groups(): lax.ppermute(compact, 'col', [(c, c ^ m) for c in range(col_count)])  8.95 us
  transfers between devices with their start and end apart: 8, of which 4 were waited for; matrix products, arithmetic and copies ran while one was open for 28% of the time, Pallas kernels for 0%

profile of v4, /device:TPU:9, one launch (start us, length us, event | category | flops | bytes accessed | tf_op | source)
XLA Modules:
  0.0 202.3 jit_solution(12996779242285401183)
XLA Ops:
  2.6 2.3 %gather_fusion.2 = bf16[512,1600]{1,0:T(8,128)(2,1)S(1)} fusion(bf16[512,1600]{1,0:T(8,128)(2,1)S(1)} %bitcast.75, s32[1024]{0:T(1024)S(1)} %pad_clamp_fusion.7), kind=kCustom, calls=%fused_computation.2 | custom fusion | bytes 3278848 | tf_op jit(solution)/shard_map/gather | solution.py:62
  6.4 13.6 %all-to-all-start = ((bf16[32,16,1600]{2,1,0:T(8,128)(2,1)}), bf16[32,16,1600]{2,1,0:T(8,128)(2,1)}, u32[]{:S(2)}, u32[]{:S(2)}) async-start(bf16[32,16,1600]{2,1,0:T(8,128)(2,1)} %broadcast_select_fusion), calls=%async_computation | async-start | bytes 3407872 | tf_op jit(solution)/shard_map/all_to_all | solution.py:65
  28.1 2.3 %gather_fusion = bf16[256,1600]{1,0:T(8,128)(2,1)} fusion(bf16[512,1600]{1,0:T(8,128)(2,1)S(1)} %bitcast.74, s32[1024]{0:T(1024)S(1)} %pad_clamp_fusion.9), kind=kCustom, calls=%fused_computation | custom fusion | bytes 1639424 | tf_op jit(solution)/shard_map/gather | solution.py:77
  30.3 2.2 %gather_fusion.1 = bf16[256,1600]{1,0:T(8,128)(2,1)} fusion(bf16[320,1600]{1,0:T(8,128)(2,1)S(1)} %copy-done.1, s32[1024]{0:T(1024)S(1)} %pad_clamp_fusion.8), kind=kCustom, calls=%fused_computation.1 | custom fusion | bytes 1639424 | tf_op jit(solution)/shard_map/gather | solution.py:125
  32.6 2.3 %gather_fusion.4 = bf16[256,1600]{1,0:T(8,128)(2,1)} fusion(bf16[320,1600]{1,0:T(8,128)(2,1)S(1)} %copy-done.1, s32[1024]{0:T(1024)S(1)} %pad_clamp_fusion.5), kind=kCustom, calls=%fused_computation.4 | custom fusion | bytes 1639424 | tf_op jit(solution)/shard_map/gather | solution.py:125
  34.9 2.3 %gather_fusion.7 = bf16[256,1600]{1,0:T(8,128)(2,1)} fusion(bf16[320,1600]{1,0:T(8,128)(2,1)S(1)} %copy-done.1, s32[1024]{0:T(1024)S(1)} %pad_clamp_fusion.2), kind=kCustom, calls=%fused_computation.7 | custom fusion | bytes 1639424 | tf_op jit(solution)/shard_map/gather | solution.py:125
  37.2 2.3 %gather_fusion.6 = bf16[256,1600]{1,0:T(8,128)(2,1)} fusion(bf16[320,1600]{1,0:T(8,128)(2,1)S(1)} %copy-done.1, s32[1024]{0:T(1024)S(1)} %pad_clamp_fusion.3), kind=kCustom, calls=%fused_computation.6 | custom fusion | bytes 1639424 | tf_op jit(solution)/shard_map/gather | solution.py:125
  39.4 2.2 %gather_fusion.5 = bf16[256,1600]{1,0:T(8,128)(2,1)} fusion(bf16[320,1600]{1,0:T(8,128)(2,1)S(1)} %copy-done.1, s32[1024]{0:T(1024)S(1)} %pad_clamp_fusion.4), kind=kCustom, calls=%fused_computation.5 | custom fusion | bytes 1639424 | tf_op jit(solution)/shard_map/gather | solution.py:125
  48.6 13.4 %all-to-all-done = bf16[32,16,1600]{2,1,0:T(8,128)(2,1)} async-done(((bf16[32,16,1600]{2,1,0:T(8,128)(2,1)}), bf16[32,16,1600]{2,1,0:T(8,128)(2,1)}, u32[]{:S(2)}, u32[]{:S(2)}) %all-to-all-start) | async-done | bytes 1638432 | tf_op jit(solution)/shard_map/all_to_all | solution.py:65
  62.1 3.8 %gather_fusion.3 = bf16[256,1600]{1,0:T(8,128)(2,1)S(1)} fusion(bf16[512,1600]{1,0:T(8,128)(2,1)} %bitcast.11, s32[1024]{0:T(1024)S(1)} %pad_clamp_fusion.6), kind=kCustom, calls=%fused_computation.3 | custom fusion | bytes 1639424 | tf_op jit(solution)/shard_map/gather | solution.py:72
  67.2 4.7 %collective-permute-start.2 = (bf16[256,1600]{0,1:T(8,128)(2,1)}, bf16[256,1600]{0,1:T(8,128)(2,1)}, u32[]{:S(2)}, u32[]{:S(2)}) collective-permute-start(bf16[256,1600]{0,1:T(8,128)(2,1)} %copy.60), channel_id=1, source_target_pairs={{0,3},{1,2},{2,1},{3,0},{4,7},{5,6},{6,5},{7,4},{8,11},{9,10},{10,... | collective-permute-start | bytes 2457608 | tf_op jit(solution)/shard_map/ppermute | solution.py:74
  71.9 2.1 %collective-permute-start.1 = (bf16[256,1600]{0,1:T(8,128)(2,1)}, bf16[256,1600]{0,1:T(8,128)(2,1)}, u32[]{:S(2)}, u32[]{:S(2)}) collective-permute-start(bf16[256,1600]{0,1:T(8,128)(2,1)} %copy.60), channel_id=1, source_target_pairs={{0,2},{1,3},{2,0},{3,1},{4,6},{5,7},{6,4},{7,5},{8,10},{9,11},{10,... | collective-permute-start | bytes 2457608 | tf_op jit(solution)/shard_map/ppermute | solution.py:74
  74.1 2.1 %collective-permute-start = (bf16[256,1600]{0,1:T(8,128)(2,1)}, bf16[256,1600]{0,1:T(8,128)(2,1)}, u32[]{:S(2)}, u32[]{:S(2)}) collective-permute-start(bf16[256,1600]{0,1:T(8,128)(2,1)} %copy.60), channel_id=1, source_target_pairs={{0,1},{1,0},{2,3},{3,2},{4,5},{5,4},{6,7},{7,6},{8,9},{9,8},{10,11... | collective-permute-start | bytes 2457608 | tf_op jit(solution)/shard_map/ppermute | solution.py:74
  77.5 6.4 %all-to-all-start.1 = ((bf16[32,16,1250]{2,1,0:T(8,128)(2,1)}), bf16[32,16,1250]{2,1,0:T(8,128)(2,1)}, u32[]{:S(2)}, u32[]{:S(2)}) async-start(bf16[32,16,1250]{2,1,0:T(8,128)(2,1)} %broadcast_in_dim.285), calls=%async_computation.1 | async-start | bytes 2621440 | tf_op jit(solution)/shard_map/all_to_all | solution.py:68
  86.7 4.6 %collective-permute-done.2 = bf16[256,1600]{0,1:T(8,128)(2,1)} collective-permute-done((bf16[256,1600]{0,1:T(8,128)(2,1)}, bf16[256,1600]{0,1:T(8,128)(2,1)}, u32[]{:S(2)}, u32[]{:S(2)}) %collective-permute-start.2) | collective-permute-done | bytes 819232 | tf_op jit(solution)/shard_map/ppermute | solution.py:74
  92.8 15.9 %collective-permute-done.1 = bf16[256,1600]{0,1:T(8,128)(2,1)} collective-permute-done((bf16[256,1600]{0,1:T(8,128)(2,1)}, bf16[256,1600]{0,1:T(8,128)(2,1)}, u32[]{:S(2)}, u32[]{:S(2)}) %collective-permute-start.1) | collective-permute-done | bytes 819232 | tf_op jit(solution)/shard_map/ppermute | solution.py:74
  110.2 2.2 %copy.61 = bf16[256,1600]{1,0:T(8,128)(2,1)} copy(bf16[256,1600]{0,1:T(8,128)(2,1)} %collective-permute-done) | data formatting | bytes 1638400 | tf_op jit(solution)/shard_map/ppermute | solution.py:74
  117.9 4.5 %reshape_reshape.4 = bf16[1600,400]{1,0:T(8,128)(2,1)} reshape(bf16[32,16,1250]{2,1,0:T(8,128)(2,1)} %all-to-all-done.1) | data formatting | bytes 2560000 | tf_op jit(solution)/shard_map/reshape;reshape | solution.py:116
  122.5 2.6 %convolution_convert_fusion.4 = bf16[256,300]{0,1:T(8,128)(2,1)S(1)} fusion(f32[256,1600]{1,0:T(8,128)} %copy-done.5, f32[1600]{0:T(1024)S(1)} %copy-done.27, f32[256]{0:T(256)S(1)} %copy-done.37, f32[256]{0:T(256)S(1)} %copy-done.31, bf16[1600,400]{1,0:T(8,128)(2,1)} %reshape_reshape.4), kind=kOutput, calls=%fused_computation.33 | convolution fusion | flops 247475200 | bytes 3094784 | tf_op jit(solution)/shard_map/dot_general | solution.py:130
  136.8 4.1 %gather_fusion.8 = bf16[1280,200]{1,0:T(8,128)(2,1)S(1)} fusion(bf16[1280,200]{1,0:T(8,128)(2,1)S(1)} %copy.66, s32[2048]{0:T(1024)S(1)} %copy-done.19), kind=kCustom, calls=%fused_computation.8 | custom fusion | bytes 1029120 | tf_op jit(solution)/shard_map/gather | solution.py:141
  143.5 2.4 %collective-permute-start.3 = (f32[4,32,320]{2,1,0:T(8,128)S(1)}, f32[4,32,320]{2,1,0:T(8,128)}, u32[]{:S(2)}, u32[]{:S(2)}) collective-permute-start(f32[4,32,320]{2,1,0:T(8,128)S(1)} %fusion.25), channel_id=1, source_target_pairs={{1,0},{2,1},{3,2},{4,3},{5,4},{6,5},{7,6},{8,7},{9,8},{10,9},{11,1... | collective-permute-start | bytes 491528 | tf_op jit(solution)/shard_map/ppermute | solution.py:168
  146.9 3.4 %collective-permute-start.4 = (f32[4,32,320]{2,1,0:T(8,128)}, f32[4,32,320]{2,1,0:T(8,128)S(1)}, u32[]{:S(2)}, u32[]{:S(2)}) collective-permute-start(f32[4,32,320]{2,1,0:T(8,128)} %get-tuple-element.67), channel_id=1, source_target_pairs={{0,1},{1,2},{2,3},{3,4},{4,5},{5,6},{6,7},{7,8},{8,9},{9,10},{10,1... | collective-permute-start | bytes 491528 | tf_op jit(solution)/shard_map/ppermute | solution.py:167
  159.3 16.6 %all-to-all-start.2 = ((f32[16,128,100]{1,2,0:T(8,128)}), f32[16,128,100]{1,2,0:T(8,128)S(1)}, u32[]{:S(2)}, u32[]{:S(2)}) async-start(f32[16,128,100]{1,2,0:T(8,128)} %convolution_bitcast_fusion), calls=%async_computation.2 | async-start | bytes 1703936 | tf_op jit(solution)/shard_map/all_to_all | solution.py:188
  187.4 14.1 %all-to-all-done.2 = f32[16,128,100]{1,2,0:T(8,128)S(1)} async-done(((f32[16,128,100]{1,2,0:T(8,128)}), f32[16,128,100]{1,2,0:T(8,128)S(1)}, u32[]{:S(2)}, u32[]{:S(2)}) %all-to-all-start.2) | async-done | bytes 819232 | tf_op jit(solution)/shard_map/all_to_all | solution.py:188
  (256 shorter events, 68.1 us)
Async XLA Ops:
  6.4 13.8 %copy-start.29 = (bf16[1600]{0:T(1024)(128)(2,1)S(1)}, bf16[1600]{0:T(1024)(128)(2,1)}, u32[]{:S(2)}) copy-start(bf16[1600]{0:T(1024)(128)(2,1)} %param.11) | copy-start | bytes 9604
  6.4 15.0 %copy-start.20 = (bf16[50,2,100]{2,1,0:T(2,128)(2,1)S(1)}, bf16[50,2,100]{2,1,0:T(2,128)(2,1)}, u32[]{:S(2)}) copy-start(bf16[50,2,100]{2,1,0:T(2,128)(2,1)} %param.13) | copy-start | bytes 60004
  6.4 15.1 %copy-start.24 = (s32[128,32]{0,1:T(8,128)S(1)}, s32[128,32]{0,1:T(8,128)}, u32[]{:S(2)}) copy-start(s32[128,32]{0,1:T(8,128)} %param.17) | copy-start | bytes 49156
  6.4 55.7 %all-to-all-start = ((bf16[32,16,1600]{2,1,0:T(8,128)(2,1)}), bf16[32,16,1600]{2,1,0:T(8,128)(2,1)}, u32[]{:S(2)}, u32[]{:S(2)}) async-start(bf16[32,16,1600]{2,1,0:T(8,128)(2,1)} %broadcast_select_fusion), calls=%async_computation | async-start | bytes 3407872 | tf_op jit(solution)/shard_map/all_to_all | solution.py:65
  41.7 4.5 %copy-start.25 = (bf16[100,50]{0,1:T(8,128)(2,1)S(1)}, bf16[100,50]{0,1:T(8,128)(2,1)}, u32[]{:S(2)}) copy-start(bf16[100,50]{0,1:T(8,128)(2,1)} %param.14) | copy-start | bytes 30004
  41.7 4.5 %copy-start.26 = (bf16[50,100]{1,0:T(8,128)(2,1)S(1)}, bf16[50,100]{1,0:T(8,128)(2,1)}, u32[]{:S(2)}) copy-start(bf16[50,100]{1,0:T(8,128)(2,1)} %param.12) | copy-start | bytes 30004
  46.4 19.5 %copy-start.30 = (f32[256]{0:T(256)}, f32[256]{0:T(256)S(1)}, u32[]{:S(2)}) copy-start(f32[256]{0:T(256)S(1)} %broadcast_multiply_fusion.4) | copy-start | bytes 3076
  67.2 24.1 %collective-permute-start.2 = (bf16[256,1600]{0,1:T(8,128)(2,1)}, bf16[256,1600]{0,1:T(8,128)(2,1)}, u32[]{:S(2)}, u32[]{:S(2)}) collective-permute-start(bf16[256,1600]{0,1:T(8,128)(2,1)} %copy.60), channel_id=1, source_target_pairs={{0,3},{1,2},{2,1},{3,0},{4,7},{5,6},{6,5},{7,4},{8,11},{9,10},{10,... | collective-permute-start | bytes 2457608 | tf_op jit(solution)/shard_map/ppermute | solution.py:74
  71.9 36.8 %collective-permute-start.1 = (bf16[256,1600]{0,1:T(8,128)(2,1)}, bf16[256,1600]{0,1:T(8,128)(2,1)}, u32[]{:S(2)}, u32[]{:S(2)}) collective-permute-start(bf16[256,1600]{0,1:T(8,128)(2,1)} %copy.60), channel_id=1, source_target_pairs={{0,2},{1,3},{2,0},{3,1},{4,6},{5,7},{6,4},{7,5},{8,10},{9,11},{10,... | collective-permute-start | bytes 2457608 | tf_op jit(solution)/shard_map/ppermute | solution.py:74
  74.1 36.2 %collective-permute-start = (bf16[256,1600]{0,1:T(8,128)(2,1)}, bf16[256,1600]{0,1:T(8,128)(2,1)}, u32[]{:S(2)}, u32[]{:S(2)}) collective-permute-start(bf16[256,1600]{0,1:T(8,128)(2,1)} %copy.60), channel_id=1, source_target_pairs={{0,1},{1,0},{2,3},{3,2},{4,5},{5,4},{6,7},{7,6},{8,9},{9,8},{10,11... | collective-permute-start | bytes 2457608 | tf_op jit(solution)/shard_map/ppermute | solution.py:74
  76.3 7.7 %copy-start.12 = (bf16[256,1600]{1,0:T(8,128)(2,1)S(1)}, bf16[256,1600]{1,0:T(8,128)(2,1)}, u32[]{:S(2)}) copy-start(bf16[256,1600]{1,0:T(8,128)(2,1)} %gather_fusion.4) | copy-start | bytes 2457604
  77.5 40.4 %all-to-all-start.1 = ((bf16[32,16,1250]{2,1,0:T(8,128)(2,1)}), bf16[32,16,1250]{2,1,0:T(8,128)(2,1)}, u32[]{:S(2)}, u32[]{:S(2)}) async-start(bf16[32,16,1250]{2,1,0:T(8,128)(2,1)} %broadcast_in_dim.285), calls=%async_computation.1 | async-start | bytes 2621440 | tf_op jit(solution)/shard_map/all_to_all | solution.py:68
  117.5 9.7 %copy-start.4 = (f32[256,1600]{1,0:T(8,128)}, f32[256,1600]{1,0:T(8,128)S(1)}, u32[]{:S(2)}) copy-start(f32[256,1600]{1,0:T(8,128)S(1)} %get-tuple-element.42) | copy-start | bytes 4915204
  117.9 4.6 %copy-start.27 = (f32[1600]{0:T(1024)S(1)}, f32[1600]{0:T(1024)}, u32[]{:S(2)}) copy-start(f32[1600]{0:T(1024)} %convert_element_type.167) | copy-start | bytes 19204
  117.9 4.6 %copy-start.31 = (f32[256]{0:T(256)S(1)}, f32[256]{0:T(256)}, u32[]{:S(2)}) copy-start(f32[256]{0:T(256)} %copy-done.30) | copy-start | bytes 3076
  117.9 4.6 %copy-start.37 = (f32[256]{0:T(256)S(1)}, f32[256]{0:T(256)}, u32[]{:S(2)}) copy-start(f32[256]{0:T(256)} %add_rsqrt_fusion.4) | copy-start | bytes 3076
  130.2 4.5 %copy-start.14 = (bf16[1280,200]{0,1:T(8,128)(2,1)S(1)}, bf16[1280,200]{0,1:T(8,128)(2,1)}, u32[]{:S(2)}) copy-start(bf16[1280,200]{0,1:T(8,128)(2,1)} %slice_dynamic-update-slice_fusion.4) | copy-start | bytes 1536004
  131.0 5.8 %copy-start.19 = (s32[2048]{0:T(1024)S(1)}, s32[2048]{0:T(1024)}, u32[]{:S(2)}) copy-start(s32[2048]{0:T(1024)} %pad_clamp_fusion) | copy-start | bytes 24580
  141.2 4.7 %copy-start.32 = (pred[100]{0:T(512)(128)(4,1)S(1)}, pred[100]{0:T(512)(128)(4,1)}, u32[]{:S(2)}) copy-start(pred[100]{0:T(512)(128)(4,1)} %get-tuple-element.74) | copy-start | bytes 304
  142.8 7.5 %copy-start.18 = (s32[4,32]{0,1:T(8,128)S(1)}, s32[4,32]{0,1:T(8,128)}, u32[]{:S(2)}) copy-start(s32[4,32]{0,1:T(8,128)} %get-tuple-element.32) | copy-start | bytes 1540
  143.5 10.7 %collective-permute-start.3 = (f32[4,32,320]{2,1,0:T(8,128)S(1)}, f32[4,32,320]{2,1,0:T(8,128)}, u32[]{:S(2)}, u32[]{:S(2)}) collective-permute-start(f32[4,32,320]{2,1,0:T(8,128)S(1)} %fusion.25), channel_id=1, source_target_pairs={{1,0},{2,1},{3,2},{4,3},{5,4},{6,5},{7,6},{8,7},{9,8},{10,9},{11,1... | collective-permute-start | bytes 491528 | tf_op jit(solution)/shard_map/ppermute | solution.py:168
  146.9 7.3 %collective-permute-start.4 = (f32[4,32,320]{2,1,0:T(8,128)}, f32[4,32,320]{2,1,0:T(8,128)S(1)}, u32[]{:S(2)}, u32[]{:S(2)}) collective-permute-start(f32[4,32,320]{2,1,0:T(8,128)} %get-tuple-element.67), channel_id=1, source_target_pairs={{0,1},{1,2},{2,3},{3,4},{4,5},{5,6},{6,7},{7,8},{8,9},{9,10},{10,1... | collective-permute-start | bytes 491528 | tf_op jit(solution)/shard_map/ppermute | solution.py:167
  159.3 25.1 %copy-start.23 = (s32[1024]{0:T(1024)S(1)}, s32[1024]{0:T(1024)}, u32[]{:S(2)}) copy-start(s32[1024]{0:T(1024)} %pad_clamp_fusion.1) | copy-start | bytes 12292
  159.3 42.3 %all-to-all-start.2 = ((f32[16,128,100]{1,2,0:T(8,128)}), f32[16,128,100]{1,2,0:T(8,128)S(1)}, u32[]{:S(2)}, u32[]{:S(2)}) async-start(f32[16,128,100]{1,2,0:T(8,128)} %convolution_bitcast_fusion), calls=%async_computation.2 | async-start | bytes 1703936 | tf_op jit(solution)/shard_map/all_to_all | solution.py:188
  (24 other events, 54.9 us)

commit v5 on v4

--- a/solution.py
+++ b/solution.py
@@ -6,7 +6,7 @@
 HEADS = 25
 HEAD_DIM = 64
 REM_DEV = 32
-TOKEN_SPLIT = 4
+TOKEN_SPLIT = 8
 HIGH = lax.Precision.HIGHEST
 
 
@@ -58,9 +58,15 @@
     own_part = col_index % split
     store_rows = group_store.reshape(slot_count * group_len, full_width)
     tok_ids = jnp.arange(part, dtype=jnp.int32)
-    send_rows = send_slot[:, :, None] * group_len + own_part * part + tok_ids
-    payload = store_rows[send_rows.reshape(-1)].reshape(row_count, capacity * part, full_width)
-    live_rows = jnp.repeat(send_live, part, axis=1)
+    row_split = max(1, 16 // (capacity * part))
+    if full_width % row_split:
+        row_split = 1
+    seg = full_width // row_split
+    seg_ids = jnp.arange(row_split, dtype=jnp.int32)
+    store_segs = group_store.reshape(slot_count * group_len * row_split, seg)
+    send_rows = (send_slot[:, :, None] * group_len + own_part * part + tok_ids)[..., None] * row_split + seg_ids
+    payload = store_segs[send_rows.reshape(-1)].reshape(row_count, capacity * part * row_split, seg)
+    live_rows = jnp.repeat(send_live, part * row_split, axis=1)
     sent = jnp.where(live_rows[:, :, None], payload, jnp.zeros_like(payload))
     received = lax.all_to_all(sent, "row", split_axis=0, concat_axis=0, tiled=True)
     extra, received = lax.optimization_barrier((extra, received))
@@ -68,8 +74,9 @@
     extra_all = lax.all_to_all(
         jnp.broadcast_to(extra_tiles[None], (row_count,) + extra_tiles.shape), "row", 0, 0, tiled=True
     ).reshape((row_count,) + extra.shape)
-    flat = received.reshape(row_count * capacity * part, full_width)
-    compact = flat[(compact_index[:, None] * part + tok_ids).reshape(-1)]
+    flat = received.reshape(row_count * capacity * part * row_split, seg)
+    compact_rows = (compact_index[:, None] * part + tok_ids)[..., None] * row_split + seg_ids
+    compact = flat[compact_rows.reshape(-1)].reshape(REM_DEV * part, full_width)
     pieces = [compact] + [
         lax.ppermute(compact, "col", [(c, c ^ m) for c in range(col_count)]) for m in range(1, split)
     ]

time: 204 us -> 238 us (1.17)
  local copies, waits for them, and re-layouts: 72 us -> 98.3 us
  waiting for transfers between devices: 48 us -> 30.3 us
  starting transfers between devices: 51.4 us -> 66.9 us
  other arithmetic: 19.1 us -> 26.5 us
    reshape x0 -> x10, local copies, waits for them, and re-layouts: none -> 14.9 us  [the longest x8 9.68 us: per_device(): jnp.broadcast_to(pos_tok[None], (groups_in, tok_len, full_width))]
    ppermute x3 -> x7, starting transfers between devices: 8.95 us -> 23.3 us  [fetch_groups(): lax.ppermute(compact, 'col', [(c, c ^ m) for c in range(col_count)])]
    all_to_all x1, waiting for transfers between devices: 13.4 us -> 0.01 us  [fetch_groups(): lax.all_to_all(sent, 'row', split_axis=0, concat_axis=0, tiled=True)]
    unnamed x94 -> x138, local copies, waits for them, and re-layouts: 18.8 us -> 24.4 us
    ppermute x3 -> x0, local copies, waits for them, and re-layouts: 5.22 us -> none  [fetch_groups(): lax.ppermute(compact, 'col', [(c, c ^ m) for c in range(col_count)])]
    reduce_sum x4 -> x9, other arithmetic: 5.4 us -> 9.41 us  [layer_norm(): center = shifted - jnp.mean(shifted, axis=-1, keepdims=True)]
    gather x5 -> x9, local copies, waits for them, and re-layouts: 11.3 us -> 15.2 us  [per_device(): pos_place = positions[place].astype(jnp.float32)]
    all_to_all x1, starting transfers between devices: 6.45 us -> 9.64 us  [fetch_groups(): lax.all_to_all(jnp.broadcast_to(extra_tiles[None], (row_count,) + extra_t...]
  transfers between devices with their start and end apart: 8 -> 12, of which waited for: 4 -> 4; matrix products, arithmetic and copies ran while one was open for 28% -> 31% of each run, Pallas kernels for 0% -> 0%
where the time goes in v5:
time: 238 us; the launch traced here: 236 us
  local copies, waits for them, and re-layouts  98.3 us (41%)
  starting transfers between devices  66.9 us (28%)
  waiting for transfers between devices  30.3 us (13%)
  other arithmetic  26.5 us (11%)
  matrix products  12.3 us (5%)
    unnamed x138, local copies, waits for them, and re-layouts  24.4 us
    ppermute x7, starting transfers between devices, fetch_groups(): lax.ppermute(compact, 'col', [(c, c ^ m) for c in range(col_count)])  23.3 us
    ppermute x7, waiting for transfers between devices, fetch_groups(): lax.ppermute(compact, 'col', [(c, c ^ m) for c in range(col_count)])  19.1 us
    gather x9, local copies, waits for them, and re-layouts, per_device(): pos_place = positions[place].astype(jnp.float32)  15.2 us
    all_to_all x1, starting transfers between devices, per_device(): lax.all_to_all(projected, 'col', 0, 0, tiled=True)  15.2 us
    all_to_all x1, starting transfers between devices, fetch_groups(): lax.all_to_all(sent, 'row', split_axis=0, concat_axis=0, tiled=True)  13.6 us
    all_to_all x1, waiting for transfers between devices, per_device(): lax.all_to_all(projected, 'col', 0, 0, tiled=True)  11.2 us
    reshape x8, local copies, waits for them, and re-layouts, per_device(): jnp.broadcast_to(pos_tok[None], (groups_in, tok_len, full_width))  9.68 us
  transfers between devices with their start and end apart: 12, of which 4 were waited for; matrix products, arithmetic and copies ran while one was open for 31% of the time, Pallas kernels for 0%

profile of v5, /device:TPU:9, one launch (start us, length us, event | category | flops | bytes accessed | tf_op | source)
XLA Modules:
  0.0 236.4 jit_solution(4550494146022141258)
XLA Ops:
  5.6 3.1 %reshape.1086 = bf16[1024,800]{1,0:T(8,128)(2,1)S(1)} reshape(bf16[16,32,1600]{2,1,0:T(8,128)(2,1)} %param.9) | data formatting | bytes 3276800 | tf_op jit(solution)/shard_map/reshape | solution.py:66
  12.0 13.6 %all-to-all-start = ((bf16[32,16,800]{2,1,0:T(8,128)(2,1)}), bf16[32,16,800]{2,1,0:T(8,128)(2,1)}, u32[]{:S(2)}, u32[]{:S(2)}) async-start(bf16[32,16,800]{2,1,0:T(8,128)(2,1)} %broadcast_select_fusion), calls=%async_computation | async-start | bytes 1835008 | tf_op jit(solution)/shard_map/all_to_all | solution.py:71
  34.5 2.3 gather_fusion.1
  58.1 2.3 gather_fusion
  65.8 3.5 %gather_fusion.3 = bf16[256,800]{1,0:T(8,128)(2,1)} fusion(bf16[512,800]{1,0:T(8,128)(2,1)} %bitcast.11, s32[1024]{0:T(1024)S(1)} %pad_clamp_fusion.10), kind=kCustom, calls=%fused_computation.3 | custom fusion | bytes 820224 | tf_op jit(solution)/shard_map/gather | solution.py:79
  74.8 3.1 %collective-permute-start = (bf16[128,1600]{1,0:T(8,128)(2,1)}, bf16[128,1600]{1,0:T(8,128)(2,1)}, u32[]{:S(2)}, u32[]{:S(2)}) collective-permute-start(bf16[128,1600]{1,0:T(8,128)(2,1)} %reshape.1089), channel_id=1, source_target_pairs={{0,1},{1,0},{2,3},{3,2},{4,5},{5,4},{6,7},{7,6},{8,9},{9,8},{10,11... | collective-permute-start | bytes 1228808 | tf_op jit(solution)/shard_map/ppermute | solution.py:81
  77.9 3.1 %collective-permute-start.1 = (bf16[128,1600]{1,0:T(8,128)(2,1)}, bf16[128,1600]{1,0:T(8,128)(2,1)}, u32[]{:S(2)}, u32[]{:S(2)}) collective-permute-start(bf16[128,1600]{1,0:T(8,128)(2,1)} %reshape.1089), channel_id=1, source_target_pairs={{0,2},{1,3},{2,0},{3,1},{4,6},{5,7},{6,4},{7,5},{8,10},{9,11},{10,... | collective-permute-start | bytes 1228808 | tf_op jit(solution)/shard_map/ppermute | solution.py:81
  81.0 2.3 collective-permute-start.2
  83.4 4.7 %collective-permute-start.3 = (bf16[128,1600]{1,0:T(8,128)(2,1)}, bf16[128,1600]{1,0:T(8,128)(2,1)}, u32[]{:S(2)}, u32[]{:S(2)}) collective-permute-start(bf16[128,1600]{1,0:T(8,128)(2,1)} %reshape.1089), channel_id=1, source_target_pairs={{0,4},{1,5},{2,6},{3,7},{4,0},{5,1},{6,2},{7,3},{8,12},{9,13},{10,... | collective-permute-start | bytes 1228808 | tf_op jit(solution)/shard_map/ppermute | solution.py:81
  88.1 2.5 %collective-permute-start.4 = (bf16[128,1600]{1,0:T(8,128)(2,1)}, bf16[128,1600]{1,0:T(8,128)(2,1)}, u32[]{:S(2)}, u32[]{:S(2)}) collective-permute-start(bf16[128,1600]{1,0:T(8,128)(2,1)} %reshape.1089), channel_id=1, source_target_pairs={{0,5},{1,4},{2,7},{3,6},{4,1},{5,0},{6,3},{7,2},{8,13},{9,12},{10,... | collective-permute-start | bytes 1228808 | tf_op jit(solution)/shard_map/ppermute | solution.py:81
  92.0 9.6 %all-to-all-start.1 = ((bf16[32,16,1250]{2,1,0:T(8,128)(2,1)}), bf16[32,16,1250]{2,1,0:T(8,128)(2,1)S(1)}, u32[]{:S(2)}, u32[]{:S(2)}) async-start(bf16[32,16,1250]{2,1,0:T(8,128)(2,1)} %broadcast_in_dim.176), calls=%async_computation.1 | async-start | bytes 2621440 | tf_op jit(solution)/shard_map/all_to_all | solution.py:74
  101.7 2.4 %add_subtract_fusion.8 = f32[128,1600]{1,0:T(8,128)} fusion(f32[128,1600]{1,0:T(8,128)} %reshape.1090, bf16[128,1600]{1,0:T(8,128)(2,1)} %reshape.1089, bf16[128,1600]{1,0:T(8,128)(2,1)S(1)} %copy-done.4), kind=kLoop, calls=%fused_computation.61 | loop fusion | flops 819200 | bytes 2457600 | tf_op jit(solution)/shard_map/sub | solution.py:135
  104.1 4.5 %collective-permute-start.5 = (bf16[128,1600]{1,0:T(8,128)(2,1)S(1)}, bf16[128,1600]{1,0:T(8,128)(2,1)S(1)}, u32[]{:S(2)}, u32[]{:S(2)}) collective-permute-start(bf16[128,1600]{1,0:T(8,128)(2,1)S(1)} %copy-done.28), channel_id=1, source_target_pairs={{0,6},{1,7},{2,4},{3,5},{4,2},{5,3},{6,0},{7,1},{8,14},{9,15},{10,... | collective-permute-start | bytes 1228808 | tf_op jit(solution)/shard_map/ppermute | solution.py:81
  110.0 3.0 %collective-permute-start.6 = (bf16[128,1600]{1,0:T(8,128)(2,1)S(1)}, bf16[128,1600]{1,0:T(8,128)(2,1)S(1)}, u32[]{:S(2)}, u32[]{:S(2)}) collective-permute-start(bf16[128,1600]{1,0:T(8,128)(2,1)S(1)} %copy-done.28), channel_id=1, source_target_pairs={{0,7},{1,6},{2,5},{3,4},{4,3},{5,2},{6,1},{7,0},{8,15},{9,14},{10,... | collective-permute-start | bytes 1228808 | tf_op jit(solution)/shard_map/ppermute | solution.py:81
  117.5 3.9 %collective-permute-done.4 = bf16[128,1600]{1,0:T(8,128)(2,1)} collective-permute-done((bf16[128,1600]{1,0:T(8,128)(2,1)}, bf16[128,1600]{1,0:T(8,128)(2,1)}, u32[]{:S(2)}, u32[]{:S(2)}) %collective-permute-start.4) | collective-permute-done | bytes 409632 | tf_op jit(solution)/shard_map/ppermute | solution.py:81
  122.6 7.9 %collective-permute-done.5 = bf16[128,1600]{1,0:T(8,128)(2,1)S(1)} collective-permute-done((bf16[128,1600]{1,0:T(8,128)(2,1)S(1)}, bf16[128,1600]{1,0:T(8,128)(2,1)S(1)}, u32[]{:S(2)}, u32[]{:S(2)}) %collective-permute-start.5) | collective-permute-done | bytes 409632 | tf_op jit(solution)/shard_map/ppermute | solution.py:81
  132.2 7.4 %collective-permute-done.6 = bf16[128,1600]{1,0:T(8,128)(2,1)S(1)} collective-permute-done((bf16[128,1600]{1,0:T(8,128)(2,1)S(1)}, bf16[128,1600]{1,0:T(8,128)(2,1)S(1)}, u32[]{:S(2)}, u32[]{:S(2)}) %collective-permute-start.6) | collective-permute-done | bytes 409632 | tf_op jit(solution)/shard_map/ppermute | solution.py:81
  140.8 2.9 %reshape_reshape.4 = bf16[1600,400]{1,0:T(8,128)(2,1)} reshape(bf16[32,16,1250]{2,1,0:T(8,128)(2,1)S(1)} %all-to-all-done.1) | data formatting | bytes 2560000 | tf_op jit(solution)/shard_map/reshape;reshape | solution.py:123
  143.7 2.1 convolution_convert_fusion
  164.4 4.8 %gather_fusion.12 = bf16[1280,200]{1,0:T(8,128)(2,1)} fusion(bf16[1280,200]{1,0:T(8,128)(2,1)S(1)} %copy.54, s32[2048]{0:T(1024)} %pad_clamp_fusion), kind=kCustom, calls=%fused_computation.12 | custom fusion | bytes 1029120 | tf_op jit(solution)/shard_map/gather | solution.py:148
  169.2 2.2 reshape.1242
  180.5 3.1 %collective-permute-start.7 = (f32[4,32,320]{2,1,0:T(8,128)S(1)}, f32[4,32,320]{2,1,0:T(8,128)}, u32[]{:S(2)}, u32[]{:S(2)}) collective-permute-start(f32[4,32,320]{2,1,0:T(8,128)S(1)} %fusion.32), channel_id=1, source_target_pairs={{1,0},{2,1},{3,2},{4,3},{5,4},{6,5},{7,6},{8,7},{9,8},{10,9},{11,1... | collective-permute-start | bytes 491528 | tf_op jit(solution)/shard_map/ppermute | solution.py:175
  192.3 15.2 %all-to-all-start.2 = ((f32[16,128,100]{1,2,0:T(8,128)}), f32[16,128,100]{1,2,0:T(8,128)}, u32[]{:S(2)}, u32[]{:S(2)}) async-start(f32[16,128,100]{1,2,0:T(8,128)} %convolution_bitcast_fusion), calls=%async_computation.2 | async-start | bytes 1703936 | tf_op jit(solution)/shard_map/all_to_all | solution.py:195
  223.2 11.2 %all-to-all-done.2 = f32[16,128,100]{1,2,0:T(8,128)} async-done(((f32[16,128,100]{1,2,0:T(8,128)}), f32[16,128,100]{1,2,0:T(8,128)}, u32[]{:S(2)}, u32[]{:S(2)}) %all-to-all-start.2) | async-done | bytes 819232 | tf_op jit(solution)/shard_map/all_to_all | solution.py:195
  (365 shorter events, 113.5 us)
Async XLA Ops:
  10.9 16.0 %copy-start = (bf16[320,1600]{1,0:T(8,128)(2,1)S(1)}, bf16[320,1600]{1,0:T(8,128)(2,1)}, u32[]{:S(2)}) copy-start(bf16[320,1600]{1,0:T(8,128)(2,1)} %param.10) | copy-start | bytes 3072004
  12.0 16.1 %copy-start.44 = (s32[128,32]{0,1:T(8,128)S(1)}, s32[128,32]{0,1:T(8,128)}, u32[]{:S(2)}) copy-start(s32[128,32]{0,1:T(8,128)} %param.17) | copy-start | bytes 49156
  12.0 53.8 %all-to-all-start = ((bf16[32,16,800]{2,1,0:T(8,128)(2,1)}), bf16[32,16,800]{2,1,0:T(8,128)(2,1)}, u32[]{:S(2)}, u32[]{:S(2)}) async-start(bf16[32,16,800]{2,1,0:T(8,128)(2,1)} %broadcast_select_fusion), calls=%async_computation | async-start | bytes 1835008 | tf_op jit(solution)/shard_map/all_to_all | solution.py:71
  74.8 29.3 %collective-permute-start = (bf16[128,1600]{1,0:T(8,128)(2,1)}, bf16[128,1600]{1,0:T(8,128)(2,1)}, u32[]{:S(2)}, u32[]{:S(2)}) collective-permute-start(bf16[128,1600]{1,0:T(8,128)(2,1)} %reshape.1089), channel_id=1, source_target_pairs={{0,1},{1,0},{2,3},{3,2},{4,5},{5,4},{6,7},{7,6},{8,9},{9,8},{10,11... | collective-permute-start | bytes 1228808 | tf_op jit(solution)/shard_map/ppermute | solution.py:81
  77.9 32.0 %collective-permute-start.1 = (bf16[128,1600]{1,0:T(8,128)(2,1)}, bf16[128,1600]{1,0:T(8,128)(2,1)}, u32[]{:S(2)}, u32[]{:S(2)}) collective-permute-start(bf16[128,1600]{1,0:T(8,128)(2,1)} %reshape.1089), channel_id=1, source_target_pairs={{0,2},{1,3},{2,0},{3,1},{4,6},{5,7},{6,4},{7,5},{8,10},{9,11},{10,... | collective-permute-start | bytes 1228808 | tf_op jit(solution)/shard_map/ppermute | solution.py:81
  81.0 33.2 %collective-permute-start.2 = (bf16[128,1600]{1,0:T(8,128)(2,1)}, bf16[128,1600]{1,0:T(8,128)(2,1)}, u32[]{:S(2)}, u32[]{:S(2)}) collective-permute-start(bf16[128,1600]{1,0:T(8,128)(2,1)} %reshape.1089), channel_id=1, source_target_pairs={{0,3},{1,2},{2,1},{3,0},{4,7},{5,6},{6,5},{7,4},{8,11},{9,10},{10,... | collective-permute-start | bytes 1228808 | tf_op jit(solution)/shard_map/ppermute | solution.py:81
  83.4 32.5 %collective-permute-start.3 = (bf16[128,1600]{1,0:T(8,128)(2,1)}, bf16[128,1600]{1,0:T(8,128)(2,1)}, u32[]{:S(2)}, u32[]{:S(2)}) collective-permute-start(bf16[128,1600]{1,0:T(8,128)(2,1)} %reshape.1089), channel_id=1, source_target_pairs={{0,4},{1,5},{2,6},{3,7},{4,0},{5,1},{6,2},{7,3},{8,12},{9,13},{10,... | collective-permute-start | bytes 1228808 | tf_op jit(solution)/shard_map/ppermute | solution.py:81
  88.1 33.3 %collective-permute-start.4 = (bf16[128,1600]{1,0:T(8,128)(2,1)}, bf16[128,1600]{1,0:T(8,128)(2,1)}, u32[]{:S(2)}, u32[]{:S(2)}) collective-permute-start(bf16[128,1600]{1,0:T(8,128)(2,1)} %reshape.1089), channel_id=1, source_target_pairs={{0,5},{1,4},{2,7},{3,6},{4,1},{5,0},{6,3},{7,2},{8,13},{9,12},{10,... | collective-permute-start | bytes 1228808 | tf_op jit(solution)/shard_map/ppermute | solution.py:81
  92.0 9.7 %copy-start.4 = (bf16[128,1600]{1,0:T(8,128)(2,1)S(1)}, bf16[128,1600]{1,0:T(8,128)(2,1)}, u32[]{:S(2)}) copy-start(bf16[128,1600]{1,0:T(8,128)(2,1)} %copy-done.3) | copy-start | bytes 1228804
  92.0 48.7 %all-to-all-start.1 = ((bf16[32,16,1250]{2,1,0:T(8,128)(2,1)}), bf16[32,16,1250]{2,1,0:T(8,128)(2,1)S(1)}, u32[]{:S(2)}, u32[]{:S(2)}) async-start(bf16[32,16,1250]{2,1,0:T(8,128)(2,1)} %broadcast_in_dim.176), calls=%async_computation.1 | async-start | bytes 2621440 | tf_op jit(solution)/shard_map/all_to_all | solution.py:74
  104.1 8.8 %copy-start.35 = (bf16[128,1600]{1,0:T(8,128)(2,1)S(1)}, bf16[128,1600]{1,0:T(8,128)(2,1)}, u32[]{:S(2)}) copy-start(bf16[128,1600]{1,0:T(8,128)(2,1)} %gather_fusion.6) | copy-start | bytes 1228804
  104.1 26.3 %collective-permute-start.5 = (bf16[128,1600]{1,0:T(8,128)(2,1)S(1)}, bf16[128,1600]{1,0:T(8,128)(2,1)S(1)}, u32[]{:S(2)}, u32[]{:S(2)}) collective-permute-start(bf16[128,1600]{1,0:T(8,128)(2,1)S(1)} %copy-done.28), channel_id=1, source_target_pairs={{0,6},{1,7},{2,4},{3,5},{4,2},{5,3},{6,0},{7,1},{8,14},{9,15},{10,... | collective-permute-start | bytes 1228808 | tf_op jit(solution)/shard_map/ppermute | solution.py:81
  109.9 20.8 %copy-start.5 = (f32[128,1600]{1,0:T(8,128)}, f32[128,1600]{1,0:T(8,128)S(1)}, u32[]{:S(2)}) copy-start(f32[128,1600]{1,0:T(8,128)S(1)} %get-tuple-element.50) | copy-start | bytes 2457604
  110.0 29.6 %collective-permute-start.6 = (bf16[128,1600]{1,0:T(8,128)(2,1)S(1)}, bf16[128,1600]{1,0:T(8,128)(2,1)S(1)}, u32[]{:S(2)}, u32[]{:S(2)}) collective-permute-start(bf16[128,1600]{1,0:T(8,128)(2,1)S(1)} %copy-done.28), channel_id=1, source_target_pairs={{0,7},{1,6},{2,5},{3,4},{4,3},{5,2},{6,1},{7,0},{8,15},{9,14},{10,... | collective-permute-start | bytes 1228808 | tf_op jit(solution)/shard_map/ppermute | solution.py:81
  114.2 16.8 %copy-start.7 = (f32[128,1600]{1,0:T(8,128)}, f32[128,1600]{1,0:T(8,128)S(1)}, u32[]{:S(2)}) copy-start(f32[128,1600]{1,0:T(8,128)S(1)} %get-tuple-element.48) | copy-start | bytes 2457604
  115.8 15.4 %copy-start.9 = (f32[128,1600]{1,0:T(8,128)}, f32[128,1600]{1,0:T(8,128)S(1)}, u32[]{:S(2)}) copy-start(f32[128,1600]{1,0:T(8,128)S(1)} %get-tuple-element.46) | copy-start | bytes 2457604
  117.5 14.0 %copy-start.11 = (f32[128,1600]{1,0:T(8,128)}, f32[128,1600]{1,0:T(8,128)S(1)}, u32[]{:S(2)}) copy-start(f32[128,1600]{1,0:T(8,128)S(1)} %get-tuple-element.44) | copy-start | bytes 2457604
  117.5 13.0 %copy-start.20 = (f32[128,1600]{1,0:T(8,128)S(1)}, f32[128,1600]{1,0:T(8,128)}, u32[]{:S(2)}) copy-start(f32[128,1600]{1,0:T(8,128)} %reshape.1096) | copy-start | bytes 2457604
  117.5 13.0 %copy-start.31 = (bf16[128,1600]{1,0:T(8,128)(2,1)S(1)}, bf16[128,1600]{1,0:T(8,128)(2,1)}, u32[]{:S(2)}) copy-start(bf16[128,1600]{1,0:T(8,128)(2,1)} %gather_fusion.10) | copy-start | bytes 1228804
  122.6 9.1 %copy-start.13 = (f32[128,1600]{1,0:T(8,128)}, f32[128,1600]{1,0:T(8,128)S(1)}, u32[]{:S(2)}) copy-start(f32[128,1600]{1,0:T(8,128)S(1)} %get-tuple-element.42) | copy-start | bytes 2457604
  178.4 9.3 %collective-permute-start.8 = (f32[4,32,320]{2,1,0:T(8,128)}, f32[4,32,320]{2,1,0:T(8,128)}, u32[]{:S(2)}, u32[]{:S(2)}) collective-permute-start(f32[4,32,320]{2,1,0:T(8,128)} %get-tuple-element.81), channel_id=1, source_target_pairs={{0,1},{1,2},{2,3},{3,4},{4,5},{5,6},{6,7},{7,8},{8,9},{9,10},{10,1... | collective-permute-start | bytes 491528 | tf_op jit(solution)/shard_map/ppermute | solution.py:174
  180.5 7.2 %collective-permute-start.7 = (f32[4,32,320]{2,1,0:T(8,128)S(1)}, f32[4,32,320]{2,1,0:T(8,128)}, u32[]{:S(2)}, u32[]{:S(2)}) collective-permute-start(f32[4,32,320]{2,1,0:T(8,128)S(1)} %fusion.32), channel_id=1, source_target_pairs={{1,0},{2,1},{3,2},{4,3},{5,4},{6,5},{7,6},{8,7},{9,8},{10,9},{11,1... | collective-permute-start | bytes 491528 | tf_op jit(solution)/shard_map/ppermute | solution.py:175
  192.3 27.9 %copy-start.43 = (s32[1024]{0:T(1024)S(1)}, s32[1024]{0:T(1024)}, u32[]{:S(2)}) copy-start(s32[1024]{0:T(1024)} %pad_clamp_fusion.1) | copy-start | bytes 12292
  192.3 42.1 %all-to-all-start.2 = ((f32[16,128,100]{1,2,0:T(8,128)}), f32[16,128,100]{1,2,0:T(8,128)}, u32[]{:S(2)}, u32[]{:S(2)}) async-start(f32[16,128,100]{1,2,0:T(8,128)} %convolution_bitcast_fusion), calls=%async_computation.2 | async-start | bytes 1703936 | tf_op jit(solution)/shard_map/all_to_all | solution.py:195
  (44 other events, 135.7 us)

commit v6 on v4

--- a/solution.py
+++ b/solution.py
@@ -185,7 +185,8 @@
         attended, out_rows, (((1,), (1,)), ((), ())), preferred_element_type=jnp.float32
     )
     projected = projected.reshape(query_count, col_count, narrow).transpose(1, 0, 2)
-    own_out = jnp.sum(lax.all_to_all(projected, "col", 0, 0, tiled=True), axis=0)
+    parts = lax.all_to_all(projected.astype(jnp.bfloat16), "col", 0, 0, tiled=True)
+    own_out = jnp.sum(parts.astype(jnp.float32), axis=0)
     hidden_out = (picked_shift.reshape(query_count, narrow) + own_out).astype(jnp.bfloat16)
     return (joined_cache, hidden_out.reshape(req_here, sel_count, narrow))
 

time: 204 us -> 194 us (0.951)
  waiting for transfers between devices: 48 us -> 43.3 us
  local copies, waits for them, and re-layouts: 72 us -> 67.6 us
    all_to_all x1, waiting for transfers between devices: 14.1 us -> 9.25 us  [per_device(): lax.all_to_all(projected.astype(jnp.bfloat16), 'col', 0, 0, tiled=True)]
    unnamed x94, local copies, waits for them, and re-layouts: 18.8 us -> 16.2 us
  transfers between devices with their start and end apart: 8 -> 8, of which waited for: 4 -> 4; matrix products, arithmetic and copies ran while one was open for 28% -> 27% of each run, Pallas kernels for 0% -> 0%
where the time goes in v6:
time: 194 us; the launch traced here: 193 us
  local copies, waits for them, and re-layouts  67.6 us (35%)
  starting transfers between devices  51.2 us (26%)
  waiting for transfers between devices  43.3 us (22%)
  other arithmetic  19.2 us (10%)
  matrix products  9.89 us (5%)
    ppermute x3, waiting for transfers between devices, fetch_groups(): lax.ppermute(compact, 'col', [(c, c ^ m) for c in range(col_count)])  20.6 us
    all_to_all x1, starting transfers between devices, per_device(): lax.all_to_all(projected.astype(jnp.bfloat16), 'col', 0, 0, tiled=True)  16.5 us
    unnamed x94, local copies, waits for them, and re-layouts  16.2 us
    all_to_all x1, starting transfers between devices, fetch_groups(): lax.all_to_all(sent, 'row', split_axis=0, concat_axis=0, tiled=True)  13.6 us
    all_to_all x1, waiting for transfers between devices, fetch_groups(): lax.all_to_all(sent, 'row', split_axis=0, concat_axis=0, tiled=True)  13.5 us
    gather x5, local copies, waits for them, and re-layouts, per_device(): pos_place = positions[place].astype(jnp.float32)  11.3 us
    all_to_all x1, waiting for transfers between devices, per_device(): lax.all_to_all(projected.astype(jnp.bfloat16), 'col', 0, 0, tiled=True)  9.25 us
    ppermute x3, starting transfers between devices, fetch_groups(): lax.ppermute(compact, 'col', [(c, c ^ m) for c in range(col_count)])  8.92 us
  transfers between devices with their start and end apart: 8, of which 4 were waited for; matrix products, arithmetic and copies ran while one was open for 27% of the time, Pallas kernels for 0%

profile of v6, /device:TPU:9, one launch (start us, length us, event | category | flops | bytes accessed | tf_op | source)
XLA Modules:
  0.0 192.9 jit_solution(4046450467813080984)
XLA Ops:
  2.6 2.3 %gather_fusion.2 = bf16[512,1600]{1,0:T(8,128)(2,1)S(1)} fusion(bf16[512,1600]{1,0:T(8,128)(2,1)S(1)} %bitcast.75, s32[1024]{0:T(1024)S(1)} %pad_clamp_fusion.7), kind=kCustom, calls=%fused_computation.2 | custom fusion | bytes 3278848 | tf_op jit(solution)/shard_map/gather | solution.py:62
  6.4 13.6 %all-to-all-start = ((bf16[32,16,1600]{2,1,0:T(8,128)(2,1)}), bf16[32,16,1600]{2,1,0:T(8,128)(2,1)}, u32[]{:S(2)}, u32[]{:S(2)}) async-start(bf16[32,16,1600]{2,1,0:T(8,128)(2,1)} %broadcast_select_fusion), calls=%async_computation | async-start | bytes 3407872 | tf_op jit(solution)/shard_map/all_to_all | solution.py:65
  28.1 2.3 %gather_fusion = bf16[256,1600]{1,0:T(8,128)(2,1)} fusion(bf16[512,1600]{1,0:T(8,128)(2,1)S(1)} %bitcast.74, s32[1024]{0:T(1024)S(1)} %pad_clamp_fusion.9), kind=kCustom, calls=%fused_computation | custom fusion | bytes 1639424 | tf_op jit(solution)/shard_map/gather | solution.py:77
  30.3 2.2 %gather_fusion.1 = bf16[256,1600]{1,0:T(8,128)(2,1)} fusion(bf16[320,1600]{1,0:T(8,128)(2,1)S(1)} %copy-done.1, s32[1024]{0:T(1024)S(1)} %pad_clamp_fusion.8), kind=kCustom, calls=%fused_computation.1 | custom fusion | bytes 1639424 | tf_op jit(solution)/shard_map/gather | solution.py:125
  32.6 2.3 %gather_fusion.4 = bf16[256,1600]{1,0:T(8,128)(2,1)} fusion(bf16[320,1600]{1,0:T(8,128)(2,1)S(1)} %copy-done.1, s32[1024]{0:T(1024)S(1)} %pad_clamp_fusion.5), kind=kCustom, calls=%fused_computation.4 | custom fusion | bytes 1639424 | tf_op jit(solution)/shard_map/gather | solution.py:125
  34.9 2.3 %gather_fusion.7 = bf16[256,1600]{1,0:T(8,128)(2,1)} fusion(bf16[320,1600]{1,0:T(8,128)(2,1)S(1)} %copy-done.1, s32[1024]{0:T(1024)S(1)} %pad_clamp_fusion.2), kind=kCustom, calls=%fused_computation.7 | custom fusion | bytes 1639424 | tf_op jit(solution)/shard_map/gather | solution.py:125
  37.2 2.3 %gather_fusion.6 = bf16[256,1600]{1,0:T(8,128)(2,1)} fusion(bf16[320,1600]{1,0:T(8,128)(2,1)S(1)} %copy-done.1, s32[1024]{0:T(1024)S(1)} %pad_clamp_fusion.3), kind=kCustom, calls=%fused_computation.6 | custom fusion | bytes 1639424 | tf_op jit(solution)/shard_map/gather | solution.py:125
  39.4 2.2 %gather_fusion.5 = bf16[256,1600]{1,0:T(8,128)(2,1)} fusion(bf16[320,1600]{1,0:T(8,128)(2,1)S(1)} %copy-done.1, s32[1024]{0:T(1024)S(1)} %pad_clamp_fusion.4), kind=kCustom, calls=%fused_computation.5 | custom fusion | bytes 1639424 | tf_op jit(solution)/shard_map/gather | solution.py:125
  48.6 13.5 %all-to-all-done = bf16[32,16,1600]{2,1,0:T(8,128)(2,1)} async-done(((bf16[32,16,1600]{2,1,0:T(8,128)(2,1)}), bf16[32,16,1600]{2,1,0:T(8,128)(2,1)}, u32[]{:S(2)}, u32[]{:S(2)}) %all-to-all-start) | async-done | bytes 1638432 | tf_op jit(solution)/shard_map/all_to_all | solution.py:65
  62.1 3.8 %gather_fusion.3 = bf16[256,1600]{1,0:T(8,128)(2,1)S(1)} fusion(bf16[512,1600]{1,0:T(8,128)(2,1)} %bitcast.11, s32[1024]{0:T(1024)S(1)} %pad_clamp_fusion.6), kind=kCustom, calls=%fused_computation.3 | custom fusion | bytes 1639424 | tf_op jit(solution)/shard_map/gather | solution.py:72
  67.2 4.7 %collective-permute-start.2 = (bf16[256,1600]{0,1:T(8,128)(2,1)}, bf16[256,1600]{0,1:T(8,128)(2,1)}, u32[]{:S(2)}, u32[]{:S(2)}) collective-permute-start(bf16[256,1600]{0,1:T(8,128)(2,1)} %copy.60), channel_id=1, source_target_pairs={{0,3},{1,2},{2,1},{3,0},{4,7},{5,6},{6,5},{7,4},{8,11},{9,10},{10,... | collective-permute-start | bytes 2457608 | tf_op jit(solution)/shard_map/ppermute | solution.py:74
  71.9 2.2 %collective-permute-start.1 = (bf16[256,1600]{0,1:T(8,128)(2,1)}, bf16[256,1600]{0,1:T(8,128)(2,1)}, u32[]{:S(2)}, u32[]{:S(2)}) collective-permute-start(bf16[256,1600]{0,1:T(8,128)(2,1)} %copy.60), channel_id=1, source_target_pairs={{0,2},{1,3},{2,0},{3,1},{4,6},{5,7},{6,4},{7,5},{8,10},{9,11},{10,... | collective-permute-start | bytes 2457608 | tf_op jit(solution)/shard_map/ppermute | solution.py:74
  77.5 6.4 %all-to-all-start.1 = ((bf16[32,16,1250]{2,1,0:T(8,128)(2,1)}), bf16[32,16,1250]{2,1,0:T(8,128)(2,1)}, u32[]{:S(2)}, u32[]{:S(2)}) async-start(bf16[32,16,1250]{2,1,0:T(8,128)(2,1)} %broadcast_in_dim.285), calls=%async_computation.1 | async-start | bytes 2621440 | tf_op jit(solution)/shard_map/all_to_all | solution.py:68
  86.6 4.6 %collective-permute-done.2 = bf16[256,1600]{0,1:T(8,128)(2,1)} collective-permute-done((bf16[256,1600]{0,1:T(8,128)(2,1)}, bf16[256,1600]{0,1:T(8,128)(2,1)}, u32[]{:S(2)}, u32[]{:S(2)}) %collective-permute-start.2) | collective-permute-done | bytes 819232 | tf_op jit(solution)/shard_map/ppermute | solution.py:74
  92.8 15.9 %collective-permute-done.1 = bf16[256,1600]{0,1:T(8,128)(2,1)} collective-permute-done((bf16[256,1600]{0,1:T(8,128)(2,1)}, bf16[256,1600]{0,1:T(8,128)(2,1)}, u32[]{:S(2)}, u32[]{:S(2)}) %collective-permute-start.1) | collective-permute-done | bytes 819232 | tf_op jit(solution)/shard_map/ppermute | solution.py:74
  110.2 2.2 %copy.61 = bf16[256,1600]{1,0:T(8,128)(2,1)} copy(bf16[256,1600]{0,1:T(8,128)(2,1)} %collective-permute-done) | data formatting | bytes 1638400 | tf_op jit(solution)/shard_map/ppermute | solution.py:74
  117.9 4.5 %reshape_reshape.4 = bf16[1600,400]{1,0:T(8,128)(2,1)} reshape(bf16[32,16,1250]{2,1,0:T(8,128)(2,1)} %all-to-all-done.1) | data formatting | bytes 2560000 | tf_op jit(solution)/shard_map/reshape;reshape | solution.py:116
  122.5 2.6 %convolution_convert_fusion.5 = bf16[256,300]{0,1:T(8,128)(2,1)S(1)} fusion(f32[256,1600]{1,0:T(8,128)} %copy-done.5, f32[1600]{0:T(1024)S(1)} %copy-done.27, f32[256]{0:T(256)S(1)} %copy-done.37, f32[256]{0:T(256)S(1)} %copy-done.31, bf16[1600,400]{1,0:T(8,128)(2,1)} %reshape_reshape.4), kind=kOutput, calls=%fused_computation.34 | convolution fusion | flops 247475200 | bytes 3094784 | tf_op jit(solution)/shard_map/dot_general | solution.py:130
  136.8 4.1 %gather_fusion.8 = bf16[1280,200]{1,0:T(8,128)(2,1)S(1)} fusion(bf16[1280,200]{1,0:T(8,128)(2,1)S(1)} %copy.66, s32[2048]{0:T(1024)S(1)} %copy-done.19), kind=kCustom, calls=%fused_computation.8 | custom fusion | bytes 1029120 | tf_op jit(solution)/shard_map/gather | solution.py:141
  143.5 2.4 %collective-permute-start.3 = (f32[4,32,320]{2,1,0:T(8,128)S(1)}, f32[4,32,320]{2,1,0:T(8,128)}, u32[]{:S(2)}, u32[]{:S(2)}) collective-permute-start(f32[4,32,320]{2,1,0:T(8,128)S(1)} %fusion.26), channel_id=1, source_target_pairs={{1,0},{2,1},{3,2},{4,3},{5,4},{6,5},{7,6},{8,7},{9,8},{10,9},{11,1... | collective-permute-start | bytes 491528 | tf_op jit(solution)/shard_map/ppermute | solution.py:168
  146.8 3.4 %collective-permute-start.4 = (f32[4,32,320]{2,1,0:T(8,128)}, f32[4,32,320]{2,1,0:T(8,128)S(1)}, u32[]{:S(2)}, u32[]{:S(2)}) collective-permute-start(f32[4,32,320]{2,1,0:T(8,128)} %get-tuple-element.67), channel_id=1, source_target_pairs={{0,1},{1,2},{2,3},{3,4},{4,5},{5,6},{6,7},{7,8},{8,9},{9,10},{10,1... | collective-permute-start | bytes 491528 | tf_op jit(solution)/shard_map/ppermute | solution.py:167
  150.9 2.1 %slice.93 = bf16[1600,100]{1,0:T(8,128)(2,1)} slice(bf16[1600,400]{1,0:T(8,128)(2,1)} %reshape_reshape.4), slice={[0:1600], [300:400]} | slice | bytes 640000 | tf_op jit(solution)/shard_map/slice | solution.py:118
  159.1 16.5 %all-to-all-start.2 = ((bf16[16,128,100]{1,2,0:T(8,128)(2,1)}), bf16[16,128,100]{1,2,0:T(8,128)(2,1)S(1)}, u32[]{:S(2)}, u32[]{:S(2)}) async-start(bf16[16,128,100]{1,2,0:T(8,128)(2,1)} %fusion), calls=%async_computation.2 | async-start | bytes 851968 | tf_op jit(solution)/shard_map/all_to_all | solution.py:188
  182.8 9.3 %all-to-all-done.2 = bf16[16,128,100]{1,2,0:T(8,128)(2,1)S(1)} async-done(((bf16[16,128,100]{1,2,0:T(8,128)(2,1)}), bf16[16,128,100]{1,2,0:T(8,128)(2,1)S(1)}, u32[]{:S(2)}, u32[]{:S(2)}) %all-to-all-start.2) | async-done | bytes 409632 | tf_op jit(solution)/shard_map/all_to_all | solution.py:188
  (256 shorter events, 63.5 us)
Async XLA Ops:
  6.4 13.8 %copy-start.29 = (bf16[1600]{0:T(1024)(128)(2,1)S(1)}, bf16[1600]{0:T(1024)(128)(2,1)}, u32[]{:S(2)}) copy-start(bf16[1600]{0:T(1024)(128)(2,1)} %param.11) | copy-start | bytes 9604
  6.4 15.0 %copy-start.20 = (bf16[50,2,100]{2,1,0:T(2,128)(2,1)S(1)}, bf16[50,2,100]{2,1,0:T(2,128)(2,1)}, u32[]{:S(2)}) copy-start(bf16[50,2,100]{2,1,0:T(2,128)(2,1)} %param.13) | copy-start | bytes 60004
  6.4 15.1 %copy-start.24 = (s32[128,32]{0,1:T(8,128)S(1)}, s32[128,32]{0,1:T(8,128)}, u32[]{:S(2)}) copy-start(s32[128,32]{0,1:T(8,128)} %param.17) | copy-start | bytes 49156
  6.4 55.7 %all-to-all-start = ((bf16[32,16,1600]{2,1,0:T(8,128)(2,1)}), bf16[32,16,1600]{2,1,0:T(8,128)(2,1)}, u32[]{:S(2)}, u32[]{:S(2)}) async-start(bf16[32,16,1600]{2,1,0:T(8,128)(2,1)} %broadcast_select_fusion), calls=%async_computation | async-start | bytes 3407872 | tf_op jit(solution)/shard_map/all_to_all | solution.py:65
  41.7 4.5 %copy-start.25 = (bf16[100,50]{0,1:T(8,128)(2,1)S(1)}, bf16[100,50]{0,1:T(8,128)(2,1)}, u32[]{:S(2)}) copy-start(bf16[100,50]{0,1:T(8,128)(2,1)} %param.14) | copy-start | bytes 30004
  41.7 4.5 %copy-start.26 = (bf16[50,100]{1,0:T(8,128)(2,1)S(1)}, bf16[50,100]{1,0:T(8,128)(2,1)}, u32[]{:S(2)}) copy-start(bf16[50,100]{1,0:T(8,128)(2,1)} %param.12) | copy-start | bytes 30004
  46.4 19.5 %copy-start.30 = (f32[256]{0:T(256)}, f32[256]{0:T(256)S(1)}, u32[]{:S(2)}) copy-start(f32[256]{0:T(256)S(1)} %broadcast_multiply_fusion.4) | copy-start | bytes 3076
  67.2 24.1 %collective-permute-start.2 = (bf16[256,1600]{0,1:T(8,128)(2,1)}, bf16[256,1600]{0,1:T(8,128)(2,1)}, u32[]{:S(2)}, u32[]{:S(2)}) collective-permute-start(bf16[256,1600]{0,1:T(8,128)(2,1)} %copy.60), channel_id=1, source_target_pairs={{0,3},{1,2},{2,1},{3,0},{4,7},{5,6},{6,5},{7,4},{8,11},{9,10},{10,... | collective-permute-start | bytes 2457608 | tf_op jit(solution)/shard_map/ppermute | solution.py:74
  71.9 36.8 %collective-permute-start.1 = (bf16[256,1600]{0,1:T(8,128)(2,1)}, bf16[256,1600]{0,1:T(8,128)(2,1)}, u32[]{:S(2)}, u32[]{:S(2)}) collective-permute-start(bf16[256,1600]{0,1:T(8,128)(2,1)} %copy.60), channel_id=1, source_target_pairs={{0,2},{1,3},{2,0},{3,1},{4,6},{5,7},{6,4},{7,5},{8,10},{9,11},{10,... | collective-permute-start | bytes 2457608 | tf_op jit(solution)/shard_map/ppermute | solution.py:74
  74.0 36.2 %collective-permute-start = (bf16[256,1600]{0,1:T(8,128)(2,1)}, bf16[256,1600]{0,1:T(8,128)(2,1)}, u32[]{:S(2)}, u32[]{:S(2)}) collective-permute-start(bf16[256,1600]{0,1:T(8,128)(2,1)} %copy.60), channel_id=1, source_target_pairs={{0,1},{1,0},{2,3},{3,2},{4,5},{5,4},{6,7},{7,6},{8,9},{9,8},{10,11... | collective-permute-start | bytes 2457608 | tf_op jit(solution)/shard_map/ppermute | solution.py:74
  76.3 7.7 %copy-start.12 = (bf16[256,1600]{1,0:T(8,128)(2,1)S(1)}, bf16[256,1600]{1,0:T(8,128)(2,1)}, u32[]{:S(2)}) copy-start(bf16[256,1600]{1,0:T(8,128)(2,1)} %gather_fusion.4) | copy-start | bytes 2457604
  77.5 40.4 %all-to-all-start.1 = ((bf16[32,16,1250]{2,1,0:T(8,128)(2,1)}), bf16[32,16,1250]{2,1,0:T(8,128)(2,1)}, u32[]{:S(2)}, u32[]{:S(2)}) async-start(bf16[32,16,1250]{2,1,0:T(8,128)(2,1)} %broadcast_in_dim.285), calls=%async_computation.1 | async-start | bytes 2621440 | tf_op jit(solution)/shard_map/all_to_all | solution.py:68
  117.5 9.7 %copy-start.4 = (f32[256,1600]{1,0:T(8,128)}, f32[256,1600]{1,0:T(8,128)S(1)}, u32[]{:S(2)}) copy-start(f32[256,1600]{1,0:T(8,128)S(1)} %get-tuple-element.42) | copy-start | bytes 4915204
  117.9 4.6 %copy-start.27 = (f32[1600]{0:T(1024)S(1)}, f32[1600]{0:T(1024)}, u32[]{:S(2)}) copy-start(f32[1600]{0:T(1024)} %convert_element_type.176) | copy-start | bytes 19204
  117.9 4.6 %copy-start.31 = (f32[256]{0:T(256)S(1)}, f32[256]{0:T(256)}, u32[]{:S(2)}) copy-start(f32[256]{0:T(256)} %copy-done.30) | copy-start | bytes 3076
  117.9 4.6 %copy-start.37 = (f32[256]{0:T(256)S(1)}, f32[256]{0:T(256)}, u32[]{:S(2)}) copy-start(f32[256]{0:T(256)} %add_rsqrt_fusion.4) | copy-start | bytes 3076
  130.2 4.5 %copy-start.14 = (bf16[1280,200]{0,1:T(8,128)(2,1)S(1)}, bf16[1280,200]{0,1:T(8,128)(2,1)}, u32[]{:S(2)}) copy-start(bf16[1280,200]{0,1:T(8,128)(2,1)} %slice_dynamic-update-slice_fusion.4) | copy-start | bytes 1536004
  131.0 5.8 %copy-start.19 = (s32[2048]{0:T(1024)S(1)}, s32[2048]{0:T(1024)}, u32[]{:S(2)}) copy-start(s32[2048]{0:T(1024)} %pad_clamp_fusion) | copy-start | bytes 24580
  141.2 4.6 %copy-start.32 = (pred[100]{0:T(512)(128)(4,1)S(1)}, pred[100]{0:T(512)(128)(4,1)}, u32[]{:S(2)}) copy-start(pred[100]{0:T(512)(128)(4,1)} %get-tuple-element.74) | copy-start | bytes 304
  142.8 7.5 %copy-start.18 = (s32[4,32]{0,1:T(8,128)S(1)}, s32[4,32]{0,1:T(8,128)}, u32[]{:S(2)}) copy-start(s32[4,32]{0,1:T(8,128)} %get-tuple-element.32) | copy-start | bytes 1540
  143.5 10.7 %collective-permute-start.3 = (f32[4,32,320]{2,1,0:T(8,128)S(1)}, f32[4,32,320]{2,1,0:T(8,128)}, u32[]{:S(2)}, u32[]{:S(2)}) collective-permute-start(f32[4,32,320]{2,1,0:T(8,128)S(1)} %fusion.26), channel_id=1, source_target_pairs={{1,0},{2,1},{3,2},{4,3},{5,4},{6,5},{7,6},{8,7},{9,8},{10,9},{11,1... | collective-permute-start | bytes 491528 | tf_op jit(solution)/shard_map/ppermute | solution.py:168
  146.8 7.3 %collective-permute-start.4 = (f32[4,32,320]{2,1,0:T(8,128)}, f32[4,32,320]{2,1,0:T(8,128)S(1)}, u32[]{:S(2)}, u32[]{:S(2)}) collective-permute-start(f32[4,32,320]{2,1,0:T(8,128)} %get-tuple-element.67), channel_id=1, source_target_pairs={{0,1},{1,2},{2,3},{3,4},{4,5},{5,6},{6,7},{7,8},{8,9},{9,10},{10,1... | collective-permute-start | bytes 491528 | tf_op jit(solution)/shard_map/ppermute | solution.py:167
  157.9 23.0 %copy-start.23 = (s32[1024]{0:T(1024)S(1)}, s32[1024]{0:T(1024)}, u32[]{:S(2)}) copy-start(s32[1024]{0:T(1024)} %pad_clamp_fusion.1) | copy-start | bytes 12292
  159.1 33.0 %all-to-all-start.2 = ((bf16[16,128,100]{1,2,0:T(8,128)(2,1)}), bf16[16,128,100]{1,2,0:T(8,128)(2,1)S(1)}, u32[]{:S(2)}, u32[]{:S(2)}) async-start(bf16[16,128,100]{1,2,0:T(8,128)(2,1)} %fusion), calls=%async_computation.2 | async-start | bytes 851968 | tf_op jit(solution)/shard_map/all_to_all | solution.py:188
  (24 other events, 54.9 us)

commit v7 on v6

--- a/solution.py
+++ b/solution.py
@@ -7,7 +7,6 @@
 HEAD_DIM = 64
 REM_DEV = 32
 TOKEN_SPLIT = 4
-HIGH = lax.Precision.HIGHEST
 
 
 def layer_norm(shifted, ln_gain):
@@ -157,7 +156,7 @@
     masks = [feature_head == first_head + p for p in range(piece_count)]
     partial = [
         jnp.einsum(
-            "bie,bte->bit", jnp.where(m[None, None, :], query_f, 0.0), key_f, precision=HIGH
+            "bie,bte->bit", jnp.where(m[None, None, :], query_f, 0.0), key_f
         )
         for m in masks
     ]
@@ -177,7 +176,7 @@
         highest = jnp.max(scores, axis=-1, keepdims=True)
         weights = jnp.where(allowed, jnp.exp(scores - highest), 0.0)
         totals = jnp.sum(weights, axis=-1)
-        summed = jnp.einsum("bit,bte->bie", weights, value_f, precision=HIGH)
+        summed = jnp.einsum("bit,bte->bie", weights, value_f)
         attended = jnp.where(masks[p][None, None, :], summed / totals[:, :, None], attended)
     attended = attended.astype(jnp.bfloat16).reshape(query_count, narrow)
 

time: 194 us -> 193 us (level)
  no operation moved by 1% of the time
where the time goes in v7:
time: 193 us; the launch traced here: 192 us
  local copies, waits for them, and re-layouts  67.6 us (35%)
  starting transfers between devices  51.2 us (27%)
  waiting for transfers between devices  43.3 us (22%)
  other arithmetic  19.2 us (10%)
  matrix products  8.87 us (5%)
    ppermute x3, waiting for transfers between devices, fetch_groups(): lax.ppermute(compact, 'col', [(c, c ^ m) for c in range(col_count)])  20.6 us
    all_to_all x1, starting transfers between devices, per_device(): lax.all_to_all(projected.astype(jnp.bfloat16), 'col', 0, 0, tiled=True)  16.7 us
    unnamed x94, local copies, waits for them, and re-layouts  16.2 us
    all_to_all x1, starting transfers between devices, fetch_groups(): lax.all_to_all(sent, 'row', split_axis=0, concat_axis=0, tiled=True)  13.6 us
    all_to_all x1, waiting for transfers between devices, fetch_groups(): lax.all_to_all(sent, 'row', split_axis=0, concat_axis=0, tiled=True)  13.5 us
    gather x5, local copies, waits for them, and re-layouts, per_device(): pos_place = positions[place].astype(jnp.float32)  11.3 us
    all_to_all x1, waiting for transfers between devices, per_device(): lax.all_to_all(projected.astype(jnp.bfloat16), 'col', 0, 0, tiled=True)  9.22 us
    ppermute x3, starting transfers between devices, fetch_groups(): lax.ppermute(compact, 'col', [(c, c ^ m) for c in range(col_count)])  8.92 us
  transfers between devices with their start and end apart: 8, of which 4 were waited for; matrix products, arithmetic and copies ran while one was open for 27% of the time, Pallas kernels for 0%

profile of v7, /device:TPU:9, one launch (start us, length us, event | category | flops | bytes accessed | tf_op | source)
XLA Modules:
  0.0 191.9 jit_solution(16869283822039005058)
XLA Ops:
  2.6 2.3 %gather_fusion.2 = bf16[512,1600]{1,0:T(8,128)(2,1)S(1)} fusion(bf16[512,1600]{1,0:T(8,128)(2,1)S(1)} %bitcast.75, s32[1024]{0:T(1024)S(1)} %pad_clamp_fusion.7), kind=kCustom, calls=%fused_computation.2 | custom fusion | bytes 3278848 | tf_op jit(solution)/shard_map/gather | solution.py:61
  6.4 13.6 %all-to-all-start = ((bf16[32,16,1600]{2,1,0:T(8,128)(2,1)}), bf16[32,16,1600]{2,1,0:T(8,128)(2,1)}, u32[]{:S(2)}, u32[]{:S(2)}) async-start(bf16[32,16,1600]{2,1,0:T(8,128)(2,1)} %broadcast_select_fusion), calls=%async_computation | async-start | bytes 3407872 | tf_op jit(solution)/shard_map/all_to_all | solution.py:64
  28.1 2.3 %gather_fusion = bf16[256,1600]{1,0:T(8,128)(2,1)} fusion(bf16[512,1600]{1,0:T(8,128)(2,1)S(1)} %bitcast.74, s32[1024]{0:T(1024)S(1)} %pad_clamp_fusion.9), kind=kCustom, calls=%fused_computation | custom fusion | bytes 1639424 | tf_op jit(solution)/shard_map/gather | solution.py:76
  30.3 2.2 %gather_fusion.1 = bf16[256,1600]{1,0:T(8,128)(2,1)} fusion(bf16[320,1600]{1,0:T(8,128)(2,1)S(1)} %copy-done.1, s32[1024]{0:T(1024)S(1)} %pad_clamp_fusion.8), kind=kCustom, calls=%fused_computation.1 | custom fusion | bytes 1639424 | tf_op jit(solution)/shard_map/gather | solution.py:124
  32.6 2.3 %gather_fusion.4 = bf16[256,1600]{1,0:T(8,128)(2,1)} fusion(bf16[320,1600]{1,0:T(8,128)(2,1)S(1)} %copy-done.1, s32[1024]{0:T(1024)S(1)} %pad_clamp_fusion.5), kind=kCustom, calls=%fused_computation.4 | custom fusion | bytes 1639424 | tf_op jit(solution)/shard_map/gather | solution.py:124
  34.9 2.3 %gather_fusion.7 = bf16[256,1600]{1,0:T(8,128)(2,1)} fusion(bf16[320,1600]{1,0:T(8,128)(2,1)S(1)} %copy-done.1, s32[1024]{0:T(1024)S(1)} %pad_clamp_fusion.2), kind=kCustom, calls=%fused_computation.7 | custom fusion | bytes 1639424 | tf_op jit(solution)/shard_map/gather | solution.py:124
  37.2 2.3 %gather_fusion.6 = bf16[256,1600]{1,0:T(8,128)(2,1)} fusion(bf16[320,1600]{1,0:T(8,128)(2,1)S(1)} %copy-done.1, s32[1024]{0:T(1024)S(1)} %pad_clamp_fusion.3), kind=kCustom, calls=%fused_computation.6 | custom fusion | bytes 1639424 | tf_op jit(solution)/shard_map/gather | solution.py:124
  39.4 2.2 %gather_fusion.5 = bf16[256,1600]{1,0:T(8,128)(2,1)} fusion(bf16[320,1600]{1,0:T(8,128)(2,1)S(1)} %copy-done.1, s32[1024]{0:T(1024)S(1)} %pad_clamp_fusion.4), kind=kCustom, calls=%fused_computation.5 | custom fusion | bytes 1639424 | tf_op jit(solution)/shard_map/gather | solution.py:124
  48.6 13.5 %all-to-all-done = bf16[32,16,1600]{2,1,0:T(8,128)(2,1)} async-done(((bf16[32,16,1600]{2,1,0:T(8,128)(2,1)}), bf16[32,16,1600]{2,1,0:T(8,128)(2,1)}, u32[]{:S(2)}, u32[]{:S(2)}) %all-to-all-start) | async-done | bytes 1638432 | tf_op jit(solution)/shard_map/all_to_all | solution.py:64
  62.1 3.8 %gather_fusion.3 = bf16[256,1600]{1,0:T(8,128)(2,1)S(1)} fusion(bf16[512,1600]{1,0:T(8,128)(2,1)} %bitcast.11, s32[1024]{0:T(1024)S(1)} %pad_clamp_fusion.6), kind=kCustom, calls=%fused_computation.3 | custom fusion | bytes 1639424 | tf_op jit(solution)/shard_map/gather | solution.py:71
  67.2 4.7 %collective-permute-start.2 = (bf16[256,1600]{0,1:T(8,128)(2,1)}, bf16[256,1600]{0,1:T(8,128)(2,1)}, u32[]{:S(2)}, u32[]{:S(2)}) collective-permute-start(bf16[256,1600]{0,1:T(8,128)(2,1)} %copy.60), channel_id=1, source_target_pairs={{0,3},{1,2},{2,1},{3,0},{4,7},{5,6},{6,5},{7,4},{8,11},{9,10},{10,... | collective-permute-start | bytes 2457608 | tf_op jit(solution)/shard_map/ppermute | solution.py:73
  71.9 2.2 %collective-permute-start.1 = (bf16[256,1600]{0,1:T(8,128)(2,1)}, bf16[256,1600]{0,1:T(8,128)(2,1)}, u32[]{:S(2)}, u32[]{:S(2)}) collective-permute-start(bf16[256,1600]{0,1:T(8,128)(2,1)} %copy.60), channel_id=1, source_target_pairs={{0,2},{1,3},{2,0},{3,1},{4,6},{5,7},{6,4},{7,5},{8,10},{9,11},{10,... | collective-permute-start | bytes 2457608 | tf_op jit(solution)/shard_map/ppermute | solution.py:73
  77.5 6.4 %all-to-all-start.1 = ((bf16[32,16,1250]{2,1,0:T(8,128)(2,1)}), bf16[32,16,1250]{2,1,0:T(8,128)(2,1)}, u32[]{:S(2)}, u32[]{:S(2)}) async-start(bf16[32,16,1250]{2,1,0:T(8,128)(2,1)} %broadcast_in_dim.285), calls=%async_computation.1 | async-start | bytes 2621440 | tf_op jit(solution)/shard_map/all_to_all | solution.py:67
  86.6 4.6 %collective-permute-done.2 = bf16[256,1600]{0,1:T(8,128)(2,1)} collective-permute-done((bf16[256,1600]{0,1:T(8,128)(2,1)}, bf16[256,1600]{0,1:T(8,128)(2,1)}, u32[]{:S(2)}, u32[]{:S(2)}) %collective-permute-start.2) | collective-permute-done | bytes 819232 | tf_op jit(solution)/shard_map/ppermute | solution.py:73
  92.8 16.0 %collective-permute-done.1 = bf16[256,1600]{0,1:T(8,128)(2,1)} collective-permute-done((bf16[256,1600]{0,1:T(8,128)(2,1)}, bf16[256,1600]{0,1:T(8,128)(2,1)}, u32[]{:S(2)}, u32[]{:S(2)}) %collective-permute-start.1) | collective-permute-done | bytes 819232 | tf_op jit(solution)/shard_map/ppermute | solution.py:73
  110.3 2.2 %copy.61 = bf16[256,1600]{1,0:T(8,128)(2,1)} copy(bf16[256,1600]{0,1:T(8,128)(2,1)} %collective-permute-done) | data formatting | bytes 1638400 | tf_op jit(solution)/shard_map/ppermute | solution.py:73
  118.0 4.5 %reshape_reshape.4 = bf16[1600,400]{1,0:T(8,128)(2,1)} reshape(bf16[32,16,1250]{2,1,0:T(8,128)(2,1)} %all-to-all-done.1) | data formatting | bytes 2560000 | tf_op jit(solution)/shard_map/reshape;reshape | solution.py:115
  122.5 2.6 %convolution_convert_fusion.5 = bf16[256,300]{0,1:T(8,128)(2,1)S(1)} fusion(f32[256,1600]{1,0:T(8,128)} %copy-done.5, f32[1600]{0:T(1024)S(1)} %copy-done.27, f32[256]{0:T(256)S(1)} %copy-done.37, f32[256]{0:T(256)S(1)} %copy-done.31, bf16[1600,400]{1,0:T(8,128)(2,1)} %reshape_reshape.4), kind=kOutput, calls=%fused_computation.34 | convolution fusion | flops 247475200 | bytes 3094784 | tf_op jit(solution)/shard_map/dot_general | solution.py:129
  136.8 4.1 %gather_fusion.8 = bf16[1280,200]{1,0:T(8,128)(2,1)S(1)} fusion(bf16[1280,200]{1,0:T(8,128)(2,1)S(1)} %copy.66, s32[2048]{0:T(1024)S(1)} %copy-done.19), kind=kCustom, calls=%fused_computation.8 | custom fusion | bytes 1029120 | tf_op jit(solution)/shard_map/gather | solution.py:140
  143.3 2.3 %collective-permute-start.3 = (f32[4,32,320]{2,1,0:T(8,128)S(1)}, f32[4,32,320]{2,1,0:T(8,128)}, u32[]{:S(2)}, u32[]{:S(2)}) collective-permute-start(f32[4,32,320]{2,1,0:T(8,128)S(1)} %fusion.26), channel_id=1, source_target_pairs={{1,0},{2,1},{3,2},{4,3},{5,4},{6,5},{7,6},{8,7},{9,8},{10,9},{11,1... | collective-permute-start | bytes 491528 | tf_op jit(solution)/shard_map/ppermute | solution.py:167
  146.5 3.2 %collective-permute-start.4 = (f32[4,32,320]{2,1,0:T(8,128)}, f32[4,32,320]{2,1,0:T(8,128)S(1)}, u32[]{:S(2)}, u32[]{:S(2)}) collective-permute-start(f32[4,32,320]{2,1,0:T(8,128)} %get-tuple-element.67), channel_id=1, source_target_pairs={{0,1},{1,2},{2,3},{3,4},{4,5},{5,6},{6,7},{7,8},{8,9},{9,10},{10,1... | collective-permute-start | bytes 491528 | tf_op jit(solution)/shard_map/ppermute | solution.py:166
  150.4 2.1 %slice.93 = bf16[1600,100]{1,0:T(8,128)(2,1)} slice(bf16[1600,400]{1,0:T(8,128)(2,1)} %reshape_reshape.4), slice={[0:1600], [300:400]} | slice | bytes 640000 | tf_op jit(solution)/shard_map/slice | solution.py:117
  157.9 16.7 %all-to-all-start.2 = ((bf16[16,128,100]{1,2,0:T(8,128)(2,1)}), bf16[16,128,100]{1,2,0:T(8,128)(2,1)S(1)}, u32[]{:S(2)}, u32[]{:S(2)}) async-start(bf16[16,128,100]{1,2,0:T(8,128)(2,1)} %fusion), calls=%async_computation.2 | async-start | bytes 851968 | tf_op jit(solution)/shard_map/all_to_all | solution.py:187
  181.8 9.2 %all-to-all-done.2 = bf16[16,128,100]{1,2,0:T(8,128)(2,1)S(1)} async-done(((bf16[16,128,100]{1,2,0:T(8,128)(2,1)}), bf16[16,128,100]{1,2,0:T(8,128)(2,1)S(1)}, u32[]{:S(2)}, u32[]{:S(2)}) %all-to-all-start.2) | async-done | bytes 409632 | tf_op jit(solution)/shard_map/all_to_all | solution.py:187
  (256 shorter events, 62.5 us)
Async XLA Ops:
  6.4 13.8 %copy-start.29 = (bf16[1600]{0:T(1024)(128)(2,1)S(1)}, bf16[1600]{0:T(1024)(128)(2,1)}, u32[]{:S(2)}) copy-start(bf16[1600]{0:T(1024)(128)(2,1)} %param.11) | copy-start | bytes 9604
  6.4 15.0 %copy-start.20 = (bf16[50,2,100]{2,1,0:T(2,128)(2,1)S(1)}, bf16[50,2,100]{2,1,0:T(2,128)(2,1)}, u32[]{:S(2)}) copy-start(bf16[50,2,100]{2,1,0:T(2,128)(2,1)} %param.13) | copy-start | bytes 60004
  6.4 15.1 %copy-start.24 = (s32[128,32]{0,1:T(8,128)S(1)}, s32[128,32]{0,1:T(8,128)}, u32[]{:S(2)}) copy-start(s32[128,32]{0,1:T(8,128)} %param.17) | copy-start | bytes 49156
  6.4 55.7 %all-to-all-start = ((bf16[32,16,1600]{2,1,0:T(8,128)(2,1)}), bf16[32,16,1600]{2,1,0:T(8,128)(2,1)}, u32[]{:S(2)}, u32[]{:S(2)}) async-start(bf16[32,16,1600]{2,1,0:T(8,128)(2,1)} %broadcast_select_fusion), calls=%async_computation | async-start | bytes 3407872 | tf_op jit(solution)/shard_map/all_to_all | solution.py:64
  41.7 4.5 %copy-start.25 = (bf16[100,50]{0,1:T(8,128)(2,1)S(1)}, bf16[100,50]{0,1:T(8,128)(2,1)}, u32[]{:S(2)}) copy-start(bf16[100,50]{0,1:T(8,128)(2,1)} %param.14) | copy-start | bytes 30004
  41.7 4.5 %copy-start.26 = (bf16[50,100]{1,0:T(8,128)(2,1)S(1)}, bf16[50,100]{1,0:T(8,128)(2,1)}, u32[]{:S(2)}) copy-start(bf16[50,100]{1,0:T(8,128)(2,1)} %param.12) | copy-start | bytes 30004
  46.4 19.5 %copy-start.30 = (f32[256]{0:T(256)}, f32[256]{0:T(256)S(1)}, u32[]{:S(2)}) copy-start(f32[256]{0:T(256)S(1)} %broadcast_multiply_fusion.4) | copy-start | bytes 3076
  67.2 24.1 %collective-permute-start.2 = (bf16[256,1600]{0,1:T(8,128)(2,1)}, bf16[256,1600]{0,1:T(8,128)(2,1)}, u32[]{:S(2)}, u32[]{:S(2)}) collective-permute-start(bf16[256,1600]{0,1:T(8,128)(2,1)} %copy.60), channel_id=1, source_target_pairs={{0,3},{1,2},{2,1},{3,0},{4,7},{5,6},{6,5},{7,4},{8,11},{9,10},{10,... | collective-permute-start | bytes 2457608 | tf_op jit(solution)/shard_map/ppermute | solution.py:73
  71.9 36.9 %collective-permute-start.1 = (bf16[256,1600]{0,1:T(8,128)(2,1)}, bf16[256,1600]{0,1:T(8,128)(2,1)}, u32[]{:S(2)}, u32[]{:S(2)}) collective-permute-start(bf16[256,1600]{0,1:T(8,128)(2,1)} %copy.60), channel_id=1, source_target_pairs={{0,2},{1,3},{2,0},{3,1},{4,6},{5,7},{6,4},{7,5},{8,10},{9,11},{10,... | collective-permute-start | bytes 2457608 | tf_op jit(solution)/shard_map/ppermute | solution.py:73
  74.1 36.2 %collective-permute-start = (bf16[256,1600]{0,1:T(8,128)(2,1)}, bf16[256,1600]{0,1:T(8,128)(2,1)}, u32[]{:S(2)}, u32[]{:S(2)}) collective-permute-start(bf16[256,1600]{0,1:T(8,128)(2,1)} %copy.60), channel_id=1, source_target_pairs={{0,1},{1,0},{2,3},{3,2},{4,5},{5,4},{6,7},{7,6},{8,9},{9,8},{10,11... | collective-permute-start | bytes 2457608 | tf_op jit(solution)/shard_map/ppermute | solution.py:73
  76.3 7.7 %copy-start.12 = (bf16[256,1600]{1,0:T(8,128)(2,1)S(1)}, bf16[256,1600]{1,0:T(8,128)(2,1)}, u32[]{:S(2)}) copy-start(bf16[256,1600]{1,0:T(8,128)(2,1)} %gather_fusion.4) | copy-start | bytes 2457604
  77.5 40.5 %all-to-all-start.1 = ((bf16[32,16,1250]{2,1,0:T(8,128)(2,1)}), bf16[32,16,1250]{2,1,0:T(8,128)(2,1)}, u32[]{:S(2)}, u32[]{:S(2)}) async-start(bf16[32,16,1250]{2,1,0:T(8,128)(2,1)} %broadcast_in_dim.285), calls=%async_computation.1 | async-start | bytes 2621440 | tf_op jit(solution)/shard_map/all_to_all | solution.py:67
  117.6 9.7 %copy-start.4 = (f32[256,1600]{1,0:T(8,128)}, f32[256,1600]{1,0:T(8,128)S(1)}, u32[]{:S(2)}) copy-start(f32[256,1600]{1,0:T(8,128)S(1)} %get-tuple-element.42) | copy-start | bytes 4915204
  117.9 4.6 %copy-start.27 = (f32[1600]{0:T(1024)S(1)}, f32[1600]{0:T(1024)}, u32[]{:S(2)}) copy-start(f32[1600]{0:T(1024)} %convert_element_type.176) | copy-start | bytes 19204
  117.9 4.6 %copy-start.31 = (f32[256]{0:T(256)S(1)}, f32[256]{0:T(256)}, u32[]{:S(2)}) copy-start(f32[256]{0:T(256)} %copy-done.30) | copy-start | bytes 3076
  117.9 4.6 %copy-start.37 = (f32[256]{0:T(256)S(1)}, f32[256]{0:T(256)}, u32[]{:S(2)}) copy-start(f32[256]{0:T(256)} %add_rsqrt_fusion.4) | copy-start | bytes 3076
  130.3 4.5 %copy-start.14 = (bf16[1280,200]{0,1:T(8,128)(2,1)S(1)}, bf16[1280,200]{0,1:T(8,128)(2,1)}, u32[]{:S(2)}) copy-start(bf16[1280,200]{0,1:T(8,128)(2,1)} %slice_dynamic-update-slice_fusion.4) | copy-start | bytes 1536004
  131.0 5.8 %copy-start.19 = (s32[2048]{0:T(1024)S(1)}, s32[2048]{0:T(1024)}, u32[]{:S(2)}) copy-start(s32[2048]{0:T(1024)} %pad_clamp_fusion) | copy-start | bytes 24580
  141.3 4.4 %copy-start.32 = (pred[100]{0:T(512)(128)(4,1)S(1)}, pred[100]{0:T(512)(128)(4,1)}, u32[]{:S(2)}) copy-start(pred[100]{0:T(512)(128)(4,1)} %get-tuple-element.74) | copy-start | bytes 304
  142.8 6.9 %copy-start.18 = (s32[4,32]{0,1:T(8,128)S(1)}, s32[4,32]{0,1:T(8,128)}, u32[]{:S(2)}) copy-start(s32[4,32]{0,1:T(8,128)} %get-tuple-element.32) | copy-start | bytes 1540
  143.3 10.3 %collective-permute-start.3 = (f32[4,32,320]{2,1,0:T(8,128)S(1)}, f32[4,32,320]{2,1,0:T(8,128)}, u32[]{:S(2)}, u32[]{:S(2)}) collective-permute-start(f32[4,32,320]{2,1,0:T(8,128)S(1)} %fusion.26), channel_id=1, source_target_pairs={{1,0},{2,1},{3,2},{4,3},{5,4},{6,5},{7,6},{8,7},{9,8},{10,9},{11,1... | collective-permute-start | bytes 491528 | tf_op jit(solution)/shard_map/ppermute | solution.py:167
  146.5 7.1 %collective-permute-start.4 = (f32[4,32,320]{2,1,0:T(8,128)}, f32[4,32,320]{2,1,0:T(8,128)S(1)}, u32[]{:S(2)}, u32[]{:S(2)}) collective-permute-start(f32[4,32,320]{2,1,0:T(8,128)} %get-tuple-element.67), channel_id=1, source_target_pairs={{0,1},{1,2},{2,3},{3,4},{4,5},{5,6},{6,7},{7,8},{8,9},{9,10},{10,1... | collective-permute-start | bytes 491528 | tf_op jit(solution)/shard_map/ppermute | solution.py:166
  156.7 23.2 %copy-start.23 = (s32[1024]{0:T(1024)S(1)}, s32[1024]{0:T(1024)}, u32[]{:S(2)}) copy-start(s32[1024]{0:T(1024)} %pad_clamp_fusion.1) | copy-start | bytes 12292
  157.9 33.2 %all-to-all-start.2 = ((bf16[16,128,100]{1,2,0:T(8,128)(2,1)}), bf16[16,128,100]{1,2,0:T(8,128)(2,1)S(1)}, u32[]{:S(2)}, u32[]{:S(2)}) async-start(bf16[16,128,100]{1,2,0:T(8,128)(2,1)} %fusion), calls=%async_computation.2 | async-start | bytes 851968 | tf_op jit(solution)/shard_map/all_to_all | solution.py:187
  (24 other events, 54.1 us)

commit v8 on v7

--- a/solution.py
+++ b/solution.py
@@ -116,7 +116,7 @@
     w_cat = allw[:, : 3 * narrow]
     out_rows = allw[:, 3 * narrow:]
 
-    out_kv, out_q, out_sh = [], [], []
+    out_norm, out_sh = [], []
     for block, ref, (tok_start, tok_len) in zip(blocks, refs, toks):
         groups_in = block.shape[0] // tok_len
         tok = tok_start + jnp.tile(jnp.arange(tok_len, dtype=jnp.int32), groups_in)
@@ -125,13 +125,13 @@
         pos_tok = lax.dynamic_slice_in_dim(positions, tok_start, tok_len, 0).astype(jnp.float32)
         pos_tok = jnp.broadcast_to(pos_tok[None], (groups_in, tok_len, full_width)).reshape(block.shape)
         shifted = block.astype(jnp.float32) + pos_place - pos_tok
-        normed = layer_norm(shifted, ln_gain).astype(jnp.bfloat16)
-        both = jnp.dot(normed, w_cat, preferred_element_type=jnp.float32).astype(jnp.bfloat16)
-        out_kv.append(both[:, : 2 * narrow])
-        out_q.append(both[:, 2 * narrow:])
+        out_norm.append(layer_norm(shifted, ln_gain).astype(jnp.bfloat16))
         out_sh.append(lax.dynamic_slice_in_dim(shifted, first_feature, narrow, 1))
-    kv_rows = jnp.concatenate(out_kv)
-    q_rows = jnp.concatenate(out_q)
+    both = jnp.dot(
+        jnp.concatenate(out_norm), w_cat, preferred_element_type=jnp.float32
+    ).astype(jnp.bfloat16)
+    kv_rows = both[:, : 2 * narrow]
+    q_rows = both[:, 2 * narrow:]
     sh_rows = jnp.concatenate(out_sh)
 
     my_lengths = lax.dynamic_index_in_dim(lengths, row_index, 0, keepdims=False)

time: 193 us -> 189 us (0.979)
  local copies, waits for them, and re-layouts: 67.6 us -> 61.8 us
  other arithmetic: 19.2 us -> 24.4 us
  waiting for transfers between devices: 43.3 us -> 40.5 us
    unnamed x94 -> x62, local copies, waits for them, and re-layouts: 16.2 us -> 6.72 us
    ppermute x3, waiting for transfers between devices: 20.6 us -> 15.4 us  [fetch_groups(): lax.ppermute(compact, 'col', [(c, c ^ m) for c in range(col_count)])]
    unnamed x0 -> x4, other arithmetic: none -> 4.9 us
    slice x0 -> x5, local copies, waits for them, and re-layouts: none -> 3.07 us  [the longest x2 2.15 us: per_device(): kv_rows = both[:, :2 * narrow]]
    reduce_sum x4, other arithmetic: 5.4 us -> 7.95 us  [layer_norm(): center = shifted - jnp.mean(shifted, axis=-1, keepdims=True)]
    concatenate x4 -> x0, local copies, waits for them, and re-layouts: 2.05 us -> none  [the longest x2 1.8 us: per_device(): q_rows = jnp.concatenate(out_q)]
    all_to_all x1, waiting for transfers between devices: 13.5 us -> 15.5 us  [fetch_groups(): lax.all_to_all(sent, 'row', split_axis=0, concat_axis=0, tiled=True)]
    dot_general x5 -> x1, matrix products: 5.64 us -> 4.41 us  [per_device(): jnp.dot(jnp.concatenate(out_norm), w_cat, preferred_element_type=jnp.floa...]
  transfers between devices with their start and end apart: 8 -> 8, of which waited for: 4 -> 4; matrix products, arithmetic and copies ran while one was open for 27% -> 32% of each run, Pallas kernels for 0% -> 0%
where the time goes in v8:
time: 189 us; the launch traced here: 187 us
  local copies, waits for them, and re-layouts  61.8 us (33%)
  starting transfers between devices  51.5 us (27%)
  waiting for transfers between devices  40.5 us (21%)
  other arithmetic  24.4 us (13%)
  matrix products  7.62 us (4%)
    all_to_all x1, starting transfers between devices, per_device(): lax.all_to_all(projected.astype(jnp.bfloat16), 'col', 0, 0, tiled=True)  15.9 us
    all_to_all x1, waiting for transfers between devices, fetch_groups(): lax.all_to_all(sent, 'row', split_axis=0, concat_axis=0, tiled=True)  15.5 us
    ppermute x3, waiting for transfers between devices, fetch_groups(): lax.ppermute(compact, 'col', [(c, c ^ m) for c in range(col_count)])  15.4 us
    all_to_all x1, starting transfers between devices, fetch_groups(): lax.all_to_all(sent, 'row', split_axis=0, concat_axis=0, tiled=True)  13.4 us
    gather x5, local copies, waits for them, and re-layouts, per_device(): pos_place = positions[place].astype(jnp.float32)  11.4 us
    all_to_all x1, waiting for transfers between devices, per_device(): lax.all_to_all(projected.astype(jnp.bfloat16), 'col', 0, 0, tiled=True)  9.6 us
    ppermute x3, starting transfers between devices, fetch_groups(): lax.ppermute(compact, 'col', [(c, c ^ m) for c in range(col_count)])  8.78 us
    reduce_sum x4, other arithmetic, layer_norm(): center = shifted - jnp.mean(shifted, axis=-1, keepdims=True)  7.95 us
  transfers between devices with their start and end apart: 8, of which 4 were waited for; matrix products, arithmetic and copies ran while one was open for 32% of the time, Pallas kernels for 0%

profile of v8, /device:TPU:9, one launch (start us, length us, event | category | flops | bytes accessed | tf_op | source)
XLA Modules:
  0.0 187.5 jit_solution(13323150422167105693)
XLA Ops:
  2.6 2.3 %gather_fusion.2 = bf16[512,1600]{1,0:T(8,128)(2,1)S(1)} fusion(bf16[512,1600]{1,0:T(8,128)(2,1)S(1)} %bitcast.76, s32[1024]{0:T(1024)S(1)} %pad_clamp_fusion.7), kind=kCustom, calls=%fused_computation.2 | custom fusion | bytes 3278848 | tf_op jit(solution)/shard_map/gather | solution.py:61
  6.5 13.4 %all-to-all-start = ((bf16[32,16,1600]{2,1,0:T(8,128)(2,1)}), bf16[32,16,1600]{2,1,0:T(8,128)(2,1)}, u32[]{:S(2)}, u32[]{:S(2)}) async-start(bf16[32,16,1600]{2,1,0:T(8,128)(2,1)} %broadcast_select_fusion), calls=%async_computation | async-start | bytes 3407872 | tf_op jit(solution)/shard_map/all_to_all | solution.py:64
  22.1 2.3 %gather_fusion = bf16[256,1600]{1,0:T(8,128)(2,1)} fusion(bf16[512,1600]{1,0:T(8,128)(2,1)S(1)} %bitcast.75, s32[1024]{0:T(1024)S(1)} %pad_clamp_fusion.9), kind=kCustom, calls=%fused_computation | custom fusion | bytes 1639424 | tf_op jit(solution)/shard_map/gather | solution.py:76
  25.7 2.2 %gather_fusion.1 = bf16[256,1600]{1,0:T(8,128)(2,1)} fusion(bf16[320,1600]{1,0:T(8,128)(2,1)S(1)} %copy-done.1, s32[1024]{0:T(1024)S(1)} %pad_clamp_fusion.8), kind=kCustom, calls=%fused_computation.1 | custom fusion | bytes 1639424 | tf_op jit(solution)/shard_map/gather | solution.py:124
  27.9 2.2 %gather_fusion.4 = bf16[256,1600]{1,0:T(8,128)(2,1)} fusion(bf16[320,1600]{1,0:T(8,128)(2,1)S(1)} %copy-done.1, s32[1024]{0:T(1024)S(1)} %pad_clamp_fusion.5), kind=kCustom, calls=%fused_computation.4 | custom fusion | bytes 1639424 | tf_op jit(solution)/shard_map/gather | solution.py:124
  30.5 2.2 %gather_fusion.5 = bf16[256,1600]{1,0:T(8,128)(2,1)} fusion(bf16[320,1600]{1,0:T(8,128)(2,1)S(1)} %copy-done.1, s32[1024]{0:T(1024)S(1)} %pad_clamp_fusion.4), kind=kCustom, calls=%fused_computation.5 | custom fusion | bytes 1639424 | tf_op jit(solution)/shard_map/gather | solution.py:124
  32.7 2.3 %gather_fusion.7 = bf16[256,1600]{1,0:T(8,128)(2,1)} fusion(bf16[320,1600]{1,0:T(8,128)(2,1)S(1)} %copy-done.1, s32[1024]{0:T(1024)S(1)} %pad_clamp_fusion.2), kind=kCustom, calls=%fused_computation.7 | custom fusion | bytes 1639424 | tf_op jit(solution)/shard_map/gather | solution.py:124
  38.6 2.3 %gather_fusion.6 = bf16[256,1600]{1,0:T(8,128)(2,1)} fusion(bf16[320,1600]{1,0:T(8,128)(2,1)S(1)} %copy-done.1, s32[1024]{0:T(1024)S(1)} %pad_clamp_fusion.3), kind=kCustom, calls=%fused_computation.6 | custom fusion | bytes 1639424 | tf_op jit(solution)/shard_map/gather | solution.py:124
  46.5 15.5 %all-to-all-done = bf16[32,16,1600]{2,1,0:T(8,128)(2,1)} async-done(((bf16[32,16,1600]{2,1,0:T(8,128)(2,1)}), bf16[32,16,1600]{2,1,0:T(8,128)(2,1)}, u32[]{:S(2)}, u32[]{:S(2)}) %all-to-all-start) | async-done | bytes 1638432 | tf_op jit(solution)/shard_map/all_to_all | solution.py:64
  62.0 3.8 %gather_fusion.3 = bf16[256,1600]{1,0:T(8,128)(2,1)S(1)} fusion(bf16[512,1600]{1,0:T(8,128)(2,1)} %bitcast.11, s32[1024]{0:T(1024)S(1)} %pad_clamp_fusion.6), kind=kCustom, calls=%fused_computation.3 | custom fusion | bytes 1639424 | tf_op jit(solution)/shard_map/gather | solution.py:71
  67.1 3.6 %collective-permute-start = (bf16[256,1600]{0,1:T(8,128)(2,1)}, bf16[256,1600]{0,1:T(8,128)(2,1)}, u32[]{:S(2)}, u32[]{:S(2)}) collective-permute-start(bf16[256,1600]{0,1:T(8,128)(2,1)} %copy.60), channel_id=1, source_target_pairs={{0,1},{1,0},{2,3},{3,2},{4,5},{5,4},{6,7},{7,6},{8,9},{9,8},{10,11... | collective-permute-start | bytes 2457608 | tf_op jit(solution)/shard_map/ppermute | solution.py:73
  70.7 3.0 %collective-permute-start.2 = (bf16[256,1600]{0,1:T(8,128)(2,1)}, bf16[256,1600]{0,1:T(8,128)(2,1)}, u32[]{:S(2)}, u32[]{:S(2)}) collective-permute-start(bf16[256,1600]{0,1:T(8,128)(2,1)} %copy.60), channel_id=1, source_target_pairs={{0,3},{1,2},{2,1},{3,0},{4,7},{5,6},{6,5},{7,4},{8,11},{9,10},{10,... | collective-permute-start | bytes 2457608 | tf_op jit(solution)/shard_map/ppermute | solution.py:73
  80.5 6.3 %all-to-all-start.1 = ((bf16[32,16,1250]{2,1,0:T(8,128)(2,1)}), bf16[32,16,1250]{2,1,0:T(8,128)(2,1)}, u32[]{:S(2)}, u32[]{:S(2)}) async-start(bf16[32,16,1250]{2,1,0:T(8,128)(2,1)} %broadcast_in_dim.293), calls=%async_computation.1 | async-start | bytes 2621440 | tf_op jit(solution)/shard_map/all_to_all | solution.py:67
  90.6 3.1 %collective-permute-done.2 = bf16[256,1600]{0,1:T(8,128)(2,1)} collective-permute-done((bf16[256,1600]{0,1:T(8,128)(2,1)}, bf16[256,1600]{0,1:T(8,128)(2,1)}, u32[]{:S(2)}, u32[]{:S(2)}) %collective-permute-start.2) | collective-permute-done | bytes 819232 | tf_op jit(solution)/shard_map/ppermute | solution.py:73
  93.7 2.2 %copy.65 = bf16[256,1600]{1,0:T(8,128)(2,1)} copy(bf16[256,1600]{0,1:T(8,128)(2,1)} %collective-permute-done.2) | data formatting | bytes 1638400 | tf_op jit(solution)/shard_map/ppermute | solution.py:73
  97.7 12.3 %collective-permute-done.1 = bf16[256,1600]{0,1:T(8,128)(2,1)} collective-permute-done((bf16[256,1600]{0,1:T(8,128)(2,1)}, bf16[256,1600]{0,1:T(8,128)(2,1)}, u32[]{:S(2)}, u32[]{:S(2)}) %collective-permute-start.1) | collective-permute-done | bytes 819232 | tf_op jit(solution)/shard_map/ppermute | solution.py:73
  112.2 2.6 %fusion.64 = (f32[256]{0:T(256)S(1)}, f32[256,1600]{1,0:T(8,128)S(1)}, f32[256]{0:T(256)S(1)}, f32[256,1600]{1,0:T(8,128)S(1)}) fusion(f32[8,1600]{1,0:T(8,128)S(1)} %get-tuple-element.51, bf16[256,1600]{1,0:T(8,128)(2,1)} %gather_fusion.7, bf16[256,1600]{1,0:T(8,128)(2,1)} %copy.65, f32[8,1600]{1,0:T(8,128)S(1)} %copy-done.10, ...), kind=kLoop, calls=%fused_computation.219 | loop fusion | flops 4095488 | bytes 6658048 | tf_op jit(solution)/shard_map/reduce_sum | solution.py:13
  119.4 3.3 %reshape_reshape.4 = bf16[1600,400]{1,0:T(8,128)(2,1)S(1)} reshape(bf16[32,16,1250]{2,1,0:T(8,128)(2,1)} %all-to-all-done.1) | data formatting | bytes 2560000 | tf_op jit(solution)/shard_map/reshape;reshape | solution.py:115
  122.8 4.4 %convolution_convert_fusion = bf16[1280,300]{0,1:T(8,128)(2,1)S(1)} fusion(bf16[1280,1600]{1,0:T(8,128)(2,1)} %fusion.10, bf16[1600,400]{1,0:T(8,128)(2,1)S(1)} %reshape_reshape.4), kind=kOutput, calls=%fused_computation.12 | convolution fusion | flops 1229184000 | bytes 6092800 | tf_op jit(solution)/shard_map/dot_general | solution.py:130
  129.6 4.1 %gather_fusion.8 = bf16[1280,200]{1,0:T(8,128)(2,1)S(1)} fusion(bf16[1280,200]{1,0:T(8,128)(2,1)S(1)} %copy.66, s32[2048]{0:T(1024)S(1)} %pad_clamp_fusion), kind=kCustom, calls=%fused_computation.8 | custom fusion | bytes 1029120 | tf_op jit(solution)/shard_map/gather | solution.py:140
  137.9 3.9 %collective-permute-start.3 = (f32[4,32,320]{2,1,0:T(8,128)S(1)}, f32[4,32,320]{2,1,0:T(8,128)S(1)}, u32[]{:S(2)}, u32[]{:S(2)}) collective-permute-start(f32[4,32,320]{2,1,0:T(8,128)S(1)} %fusion.12), channel_id=1, source_target_pairs={{1,0},{2,1},{3,2},{4,3},{5,4},{6,5},{7,6},{8,7},{9,8},{10,9},{11,1... | collective-permute-start | bytes 491528 | tf_op jit(solution)/shard_map/ppermute | solution.py:167
  142.6 3.2 %collective-permute-start.4 = (f32[4,32,320]{2,1,0:T(8,128)}, f32[4,32,320]{2,1,0:T(8,128)}, u32[]{:S(2)}, u32[]{:S(2)}) collective-permute-start(f32[4,32,320]{2,1,0:T(8,128)} %get-tuple-element.67), channel_id=1, source_target_pairs={{0,1},{1,2},{2,3},{3,4},{4,5},{5,6},{6,7},{7,8},{8,9},{9,10},{10,1... | collective-permute-start | bytes 491528 | tf_op jit(solution)/shard_map/ppermute | solution.py:166
  153.9 15.9 %all-to-all-start.2 = ((bf16[16,128,100]{1,2,0:T(8,128)(2,1)}), bf16[16,128,100]{1,2,0:T(8,128)(2,1)S(1)}, u32[]{:S(2)}, u32[]{:S(2)}) async-start(bf16[16,128,100]{1,2,0:T(8,128)(2,1)} %fusion.1), calls=%async_computation.2 | async-start | bytes 851968 | tf_op jit(solution)/shard_map/all_to_all | solution.py:187
  177.1 9.6 %all-to-all-done.2 = bf16[16,128,100]{1,2,0:T(8,128)(2,1)S(1)} async-done(((bf16[16,128,100]{1,2,0:T(8,128)(2,1)}), bf16[16,128,100]{1,2,0:T(8,128)(2,1)S(1)}, u32[]{:S(2)}, u32[]{:S(2)}) %all-to-all-start.2) | async-done | bytes 409632 | tf_op jit(solution)/shard_map/all_to_all | solution.py:187
  (226 shorter events, 59.7 us)
Async XLA Ops:
  6.5 55.6 %all-to-all-start = ((bf16[32,16,1600]{2,1,0:T(8,128)(2,1)}), bf16[32,16,1600]{2,1,0:T(8,128)(2,1)}, u32[]{:S(2)}, u32[]{:S(2)}) async-start(bf16[32,16,1600]{2,1,0:T(8,128)(2,1)} %broadcast_select_fusion), calls=%async_computation | async-start | bytes 3407872 | tf_op jit(solution)/shard_map/all_to_all | solution.py:64
  22.1 3.6 %copy-start.1 = (bf16[320,1600]{1,0:T(8,128)(2,1)S(1)}, bf16[320,1600]{1,0:T(8,128)(2,1)}, u32[]{:S(2)}) copy-start(bf16[320,1600]{1,0:T(8,128)(2,1)} %param.10) | copy-start | bytes 3072004
  32.7 3.3 %copy-start.17 = (s32[128,32]{0,1:T(8,128)S(1)}, s32[128,32]{0,1:T(8,128)}, u32[]{:S(2)}) copy-start(s32[128,32]{0,1:T(8,128)} %param.17) | copy-start | bytes 49156
  41.2 2.9 %copy-start.18 = (bf16[100,50]{0,1:T(8,128)(2,1)S(1)}, bf16[100,50]{0,1:T(8,128)(2,1)}, u32[]{:S(2)}) copy-start(bf16[100,50]{0,1:T(8,128)(2,1)} %param.14) | copy-start | bytes 30004
  43.2 94.5 %copy-start.26 = (pred[100]{0:T(512)(128)(4,1)}, pred[100]{0:T(512)(128)(4,1)S(1)}, u32[]{:S(2)}) copy-start(pred[100]{0:T(512)(128)(4,1)S(1)} %broadcast_compare_fusion.1) | copy-start | bytes 304
  44.0 93.5 %copy-start.23 = (pred[100]{0:T(512)(128)(4,1)}, pred[100]{0:T(512)(128)(4,1)S(1)}, u32[]{:S(2)}) copy-start(pred[100]{0:T(512)(128)(4,1)S(1)} %get-tuple-element.73) | copy-start | bytes 304
  44.0 91.8 %copy-start.15 = (s32[1024]{0:T(1024)}, s32[1024]{0:T(1024)S(1)}, u32[]{:S(2)}) copy-start(s32[1024]{0:T(1024)S(1)} %pad_clamp_fusion.1) | copy-start | bytes 12292
  65.8 10.0 %copy-start.7 = (bf16[256,1600]{1,0:T(8,128)(2,1)}, bf16[256,1600]{1,0:T(8,128)(2,1)S(1)}, u32[]{:S(2)}) copy-start(bf16[256,1600]{1,0:T(8,128)(2,1)S(1)} %gather_fusion.3) | copy-start | bytes 2457604
  67.1 21.3 %collective-permute-start = (bf16[256,1600]{0,1:T(8,128)(2,1)}, bf16[256,1600]{0,1:T(8,128)(2,1)}, u32[]{:S(2)}, u32[]{:S(2)}) collective-permute-start(bf16[256,1600]{0,1:T(8,128)(2,1)} %copy.60), channel_id=1, source_target_pairs={{0,1},{1,0},{2,3},{3,2},{4,5},{5,4},{6,7},{7,6},{8,9},{9,8},{10,11... | collective-permute-start | bytes 2457608 | tf_op jit(solution)/shard_map/ppermute | solution.py:73
  70.7 23.0 %collective-permute-start.2 = (bf16[256,1600]{0,1:T(8,128)(2,1)}, bf16[256,1600]{0,1:T(8,128)(2,1)}, u32[]{:S(2)}, u32[]{:S(2)}) collective-permute-start(bf16[256,1600]{0,1:T(8,128)(2,1)} %copy.60), channel_id=1, source_target_pairs={{0,3},{1,2},{2,1},{3,0},{4,7},{5,6},{6,5},{7,4},{8,11},{9,10},{10,... | collective-permute-start | bytes 2457608 | tf_op jit(solution)/shard_map/ppermute | solution.py:73
  73.7 36.3 %collective-permute-start.1 = (bf16[256,1600]{0,1:T(8,128)(2,1)}, bf16[256,1600]{0,1:T(8,128)(2,1)}, u32[]{:S(2)}, u32[]{:S(2)}) collective-permute-start(bf16[256,1600]{0,1:T(8,128)(2,1)} %copy.60), channel_id=1, source_target_pairs={{0,2},{1,3},{2,0},{3,1},{4,6},{5,7},{6,4},{7,5},{8,10},{9,11},{10,... | collective-permute-start | bytes 2457608 | tf_op jit(solution)/shard_map/ppermute | solution.py:73
  77.7 9.5 %copy-start.2 = (f32[256,1600]{1,0:T(8,128)}, f32[256,1600]{1,0:T(8,128)S(1)}, u32[]{:S(2)}) copy-start(f32[256,1600]{1,0:T(8,128)S(1)} %get-tuple-element.44) | copy-start | bytes 4915204
  80.5 38.9 %all-to-all-start.1 = ((bf16[32,16,1250]{2,1,0:T(8,128)(2,1)}), bf16[32,16,1250]{2,1,0:T(8,128)(2,1)}, u32[]{:S(2)}, u32[]{:S(2)}) async-start(bf16[32,16,1250]{2,1,0:T(8,128)(2,1)} %broadcast_in_dim.293), calls=%async_computation.1 | async-start | bytes 2621440 | tf_op jit(solution)/shard_map/all_to_all | solution.py:67
  88.4 7.5 %copy-start.11 = (f32[8,1600]{1,0:T(8,128)S(1)}, f32[8,1600]{1,0:T(8,128)}, u32[]{:S(2)}) copy-start(f32[8,1600]{1,0:T(8,128)} %get-tuple-element.53) | copy-start | bytes 153604
  97.7 18.1 %copy-start.3 = (f32[256,1600]{1,0:T(8,128)}, f32[256,1600]{1,0:T(8,128)S(1)}, u32[]{:S(2)}) copy-start(f32[256,1600]{1,0:T(8,128)S(1)} %get-tuple-element.42) | copy-start | bytes 4915204
  97.7 14.5 %copy-start.10 = (f32[8,1600]{1,0:T(8,128)S(1)}, f32[8,1600]{1,0:T(8,128)}, u32[]{:S(2)}) copy-start(f32[8,1600]{1,0:T(8,128)} %get-tuple-element.52) | copy-start | bytes 153604
  114.7 3.5 %copy-start.5 = (f32[256,1600]{1,0:T(8,128)}, f32[256,1600]{1,0:T(8,128)S(1)}, u32[]{:S(2)}) copy-start(f32[256,1600]{1,0:T(8,128)S(1)} %get-tuple-element.36) | copy-start | bytes 4915204
  122.8 4.4 %copy-start.8 = (bf16[1600,400]{1,0:T(8,128)(2,1)}, bf16[1600,400]{1,0:T(8,128)(2,1)S(1)}, u32[]{:S(2)}) copy-start(bf16[1600,400]{1,0:T(8,128)(2,1)S(1)} %reshape_reshape.4) | copy-start | bytes 3840004
  135.7 6.0 %copy-start.21 = (pred[100]{0:T(512)(128)(4,1)S(1)}, pred[100]{0:T(512)(128)(4,1)}, u32[]{:S(2)}) copy-start(pred[100]{0:T(512)(128)(4,1)} %get-tuple-element.74) | copy-start | bytes 304
  135.7 10.0 %copy-start.12 = (s32[4,32]{0,1:T(8,128)S(1)}, s32[4,32]{0,1:T(8,128)}, u32[]{:S(2)}) copy-start(s32[4,32]{0,1:T(8,128)} %get-tuple-element.32) | copy-start | bytes 1540
  137.9 11.8 %collective-permute-start.3 = (f32[4,32,320]{2,1,0:T(8,128)S(1)}, f32[4,32,320]{2,1,0:T(8,128)S(1)}, u32[]{:S(2)}, u32[]{:S(2)}) collective-permute-start(f32[4,32,320]{2,1,0:T(8,128)S(1)} %fusion.12), channel_id=1, source_target_pairs={{1,0},{2,1},{3,2},{4,3},{5,4},{6,5},{7,6},{8,7},{9,8},{10,9},{11,1... | collective-permute-start | bytes 491528 | tf_op jit(solution)/shard_map/ppermute | solution.py:167
  142.6 7.1 %collective-permute-start.4 = (f32[4,32,320]{2,1,0:T(8,128)}, f32[4,32,320]{2,1,0:T(8,128)}, u32[]{:S(2)}, u32[]{:S(2)}) collective-permute-start(f32[4,32,320]{2,1,0:T(8,128)} %get-tuple-element.67), channel_id=1, source_target_pairs={{0,1},{1,2},{2,3},{3,4},{4,5},{5,6},{6,7},{7,8},{8,9},{9,10},{10,1... | collective-permute-start | bytes 491528 | tf_op jit(solution)/shard_map/ppermute | solution.py:166
  152.8 22.4 %copy-start.16 = (s32[1024]{0:T(1024)S(1)}, s32[1024]{0:T(1024)}, u32[]{:S(2)}) copy-start(s32[1024]{0:T(1024)} %copy-done.15) | copy-start | bytes 12292
  153.9 32.8 %all-to-all-start.2 = ((bf16[16,128,100]{1,2,0:T(8,128)(2,1)}), bf16[16,128,100]{1,2,0:T(8,128)(2,1)S(1)}, u32[]{:S(2)}, u32[]{:S(2)}) async-start(bf16[16,128,100]{1,2,0:T(8,128)(2,1)} %fusion.1), calls=%async_computation.2 | async-start | bytes 851968 | tf_op jit(solution)/shard_map/all_to_all | solution.py:187
  (13 other events, 27.8 us)

commit v9 on v8

--- a/solution.py
+++ b/solution.py
@@ -127,23 +127,23 @@
         shifted = block.astype(jnp.float32) + pos_place - pos_tok
         out_norm.append(layer_norm(shifted, ln_gain).astype(jnp.bfloat16))
         out_sh.append(lax.dynamic_slice_in_dim(shifted, first_feature, narrow, 1))
-    both = jnp.dot(
-        jnp.concatenate(out_norm), w_cat, preferred_element_type=jnp.float32
-    ).astype(jnp.bfloat16)
-    kv_rows = both[:, : 2 * narrow]
-    q_rows = both[:, 2 * narrow:]
+    normed_rows = jnp.concatenate(out_norm)
     sh_rows = jnp.concatenate(out_sh)
 
     my_lengths = lax.dynamic_index_in_dim(lengths, row_index, 0, keepdims=False)
     my_picked = lax.dynamic_slice_in_dim(selected, row_index * req_here, req_here, 0)
     token_place = jnp.arange(token_span, dtype=jnp.int32)
-    keyval = kv_rows[row_of].reshape(req_here, token_span, 2, narrow)
+    keyval = jnp.dot(
+        normed_rows[row_of], w_cat[:, : 2 * narrow], preferred_element_type=jnp.float32
+    ).astype(jnp.bfloat16).reshape(req_here, token_span, 2, narrow)
     alive = token_place[None, :] < (my_lengths * group_len)[:, None]
     joined_cache = jnp.where(alive[:, :, None, None], keyval, jnp.zeros_like(keyval))
 
     req_ids = jnp.arange(req_here, dtype=jnp.int32)[:, None]
     picked_row = row_of.reshape(req_here, token_span)[req_ids, my_picked]
-    queries = q_rows[picked_row]
+    queries = jnp.dot(
+        normed_rows[picked_row], w_cat[:, 2 * narrow:], preferred_element_type=jnp.float32
+    ).astype(jnp.bfloat16)
     picked_shift = sh_rows[picked_row]
 
     feature_head = (first_feature + jnp.arange(narrow, dtype=jnp.int32)) // HEAD_DIM

time: 189 us -> 210 us (1.11)
  local copies, waits for them, and re-layouts: 61.8 us -> 76.8 us
  other arithmetic: 24.4 us -> 28.6 us
  matrix products: 7.62 us -> 11.3 us
    gather x2, local copies, waits for them, and re-layouts: 5.73 us -> 16.9 us  [the longest x1 12.1 us: per_device(): normed_rows[row_of]]
    all_to_all x1, waiting for transfers between devices: 9.6 us -> 5.92 us  [per_device(): lax.all_to_all(projected.astype(jnp.bfloat16), 'col', 0, 0, tiled=True)]
    ppermute x3, waiting for transfers between devices: 15.4 us -> 18.6 us  [fetch_groups(): lax.ppermute(compact, 'col', [(c, c ^ m) for c in range(col_count)])]
    unnamed x62 -> x56, local copies, waits for them, and re-layouts: 6.72 us -> 9.99 us
    slice x5 -> x0, local copies, waits for them, and re-layouts: 3.07 us -> none  [the longest x2 2.15 us: per_device(): kv_rows = both[:, :2 * narrow]]
    dot_general x1 -> x2, matrix products: 4.41 us -> 6.32 us  [the longest x1 4.82 us: per_device(): jnp.dot(normed_rows[row_of], w_cat[:, :2 * narrow], preferred_element_typ...]
  transfers between devices with their start and end apart: 8 -> 8, of which waited for: 4 -> 4; matrix products, arithmetic and copies ran while one was open for 32% -> 40% of each run, Pallas kernels for 0% -> 0%
where the time goes in v9:
time: 210 us; the launch traced here: 209 us
  local copies, waits for them, and re-layouts  76.8 us (37%)
  starting transfers between devices  51.2 us (24%)
  waiting for transfers between devices  39.7 us (19%)
  other arithmetic  28.6 us (14%)
  matrix products  11.3 us (5%)
    ppermute x3, waiting for transfers between devices, fetch_groups(): lax.ppermute(compact, 'col', [(c, c ^ m) for c in range(col_count)])  18.6 us
    all_to_all x1, starting transfers between devices, per_device(): lax.all_to_all(projected.astype(jnp.bfloat16), 'col', 0, 0, tiled=True)  17.4 us
    all_to_all x1, waiting for transfers between devices, fetch_groups(): lax.all_to_all(sent, 'row', split_axis=0, concat_axis=0, tiled=True)  15.2 us
    all_to_all x1, starting transfers between devices, fetch_groups(): lax.all_to_all(sent, 'row', split_axis=0, concat_axis=0, tiled=True)  13.6 us
    gather x1, local copies, waits for them, and re-layouts, per_device(): normed_rows[row_of]  12.1 us
    gather x5, local copies, waits for them, and re-layouts, per_device(): pos_place = positions[place].astype(jnp.float32)  11.4 us
    unnamed x56, local copies, waits for them, and re-layouts  9.99 us
    reduce_sum x4, other arithmetic, layer_norm(): center = shifted - jnp.mean(shifted, axis=-1, keepdims=True)  9.84 us
  transfers between devices with their start and end apart: 8, of which 4 were waited for; matrix products, arithmetic and copies ran while one was open for 40% of the time, Pallas kernels for 0%

profile of v9, /device:TPU:9, one launch (start us, length us, event | category | flops | bytes accessed | tf_op | source)
XLA Modules:
  0.0 208.9 jit_solution(16254376620224328992)
XLA Ops:
  2.6 2.3 %gather_fusion.2 = bf16[512,1600]{1,0:T(8,128)(2,1)S(1)} fusion(bf16[512,1600]{1,0:T(8,128)(2,1)S(1)} %bitcast.82, s32[1024]{0:T(1024)S(1)} %pad_clamp_fusion.7), kind=kCustom, calls=%fused_computation.2 | custom fusion | bytes 3278848 | tf_op jit(solution)/shard_map/gather | solution.py:61
  6.4 13.6 %all-to-all-start = ((bf16[32,16,1600]{2,1,0:T(8,128)(2,1)}), bf16[32,16,1600]{2,1,0:T(8,128)(2,1)}, u32[]{:S(2)}, u32[]{:S(2)}) async-start(bf16[32,16,1600]{2,1,0:T(8,128)(2,1)} %broadcast_select_fusion), calls=%async_computation | async-start | bytes 3407872 | tf_op jit(solution)/shard_map/all_to_all | solution.py:64
  26.9 2.2 %gather_fusion = bf16[256,1600]{1,0:T(8,128)(2,1)} fusion(bf16[512,1600]{1,0:T(8,128)(2,1)S(1)} %bitcast.81, s32[1024]{0:T(1024)S(1)} %pad_clamp_fusion.9), kind=kCustom, calls=%fused_computation | custom fusion | bytes 1639424 | tf_op jit(solution)/shard_map/gather | solution.py:76
  29.2 2.3 %gather_fusion.1 = bf16[256,1600]{1,0:T(8,128)(2,1)} fusion(bf16[320,1600]{1,0:T(8,128)(2,1)S(1)} %copy-done.1, s32[1024]{0:T(1024)S(1)} %pad_clamp_fusion.8), kind=kCustom, calls=%fused_computation.1 | custom fusion | bytes 1639424 | tf_op jit(solution)/shard_map/gather | solution.py:124
  31.5 2.3 %gather_fusion.4 = bf16[256,1600]{1,0:T(8,128)(2,1)} fusion(bf16[320,1600]{1,0:T(8,128)(2,1)S(1)} %copy-done.1, s32[1024]{0:T(1024)S(1)} %pad_clamp_fusion.5), kind=kCustom, calls=%fused_computation.4 | custom fusion | bytes 1639424 | tf_op jit(solution)/shard_map/gather | solution.py:124
  33.8 2.3 %gather_fusion.7 = bf16[256,1600]{1,0:T(8,128)(2,1)} fusion(bf16[320,1600]{1,0:T(8,128)(2,1)S(1)} %copy-done.1, s32[1024]{0:T(1024)S(1)} %pad_clamp_fusion.2), kind=kCustom, calls=%fused_computation.7 | custom fusion | bytes 1639424 | tf_op jit(solution)/shard_map/gather | solution.py:124
  36.0 2.3 %gather_fusion.6 = bf16[256,1600]{1,0:T(8,128)(2,1)} fusion(bf16[320,1600]{1,0:T(8,128)(2,1)S(1)} %copy-done.1, s32[1024]{0:T(1024)S(1)} %pad_clamp_fusion.3), kind=kCustom, calls=%fused_computation.6 | custom fusion | bytes 1639424 | tf_op jit(solution)/shard_map/gather | solution.py:124
  38.3 2.3 %gather_fusion.5 = bf16[256,1600]{1,0:T(8,128)(2,1)} fusion(bf16[320,1600]{1,0:T(8,128)(2,1)S(1)} %copy-done.1, s32[1024]{0:T(1024)S(1)} %pad_clamp_fusion.4), kind=kCustom, calls=%fused_computation.5 | custom fusion | bytes 1639424 | tf_op jit(solution)/shard_map/gather | solution.py:124
  46.9 15.2 %all-to-all-done = bf16[32,16,1600]{2,1,0:T(8,128)(2,1)} async-done(((bf16[32,16,1600]{2,1,0:T(8,128)(2,1)}), bf16[32,16,1600]{2,1,0:T(8,128)(2,1)}, u32[]{:S(2)}, u32[]{:S(2)}) %all-to-all-start) | async-done | bytes 1638432 | tf_op jit(solution)/shard_map/all_to_all | solution.py:64
  62.1 3.8 %gather_fusion.3 = bf16[256,1600]{1,0:T(8,128)(2,1)S(1)} fusion(bf16[512,1600]{1,0:T(8,128)(2,1)} %bitcast.11, s32[1024]{0:T(1024)S(1)} %pad_clamp_fusion.6), kind=kCustom, calls=%fused_computation.3 | custom fusion | bytes 1639424 | tf_op jit(solution)/shard_map/gather | solution.py:71
  67.2 4.7 %collective-permute-start.2 = (bf16[256,1600]{0,1:T(8,128)(2,1)}, bf16[256,1600]{0,1:T(8,128)(2,1)}, u32[]{:S(2)}, u32[]{:S(2)}) collective-permute-start(bf16[256,1600]{0,1:T(8,128)(2,1)} %copy.66), channel_id=1, source_target_pairs={{0,3},{1,2},{2,1},{3,0},{4,7},{5,6},{6,5},{7,4},{8,11},{9,10},{10,... | collective-permute-start | bytes 2457608 | tf_op jit(solution)/shard_map/ppermute | solution.py:73
  79.9 6.4 %all-to-all-start.1 = ((bf16[32,16,1250]{2,1,0:T(8,128)(2,1)}), bf16[32,16,1250]{2,1,0:T(8,128)(2,1)}, u32[]{:S(2)}, u32[]{:S(2)}) async-start(bf16[32,16,1250]{2,1,0:T(8,128)(2,1)} %broadcast_in_dim.294), calls=%async_computation.1 | async-start | bytes 2621440 | tf_op jit(solution)/shard_map/all_to_all | solution.py:67
  87.9 3.4 %collective-permute-done.2 = bf16[256,1600]{0,1:T(8,128)(2,1)} collective-permute-done((bf16[256,1600]{0,1:T(8,128)(2,1)}, bf16[256,1600]{0,1:T(8,128)(2,1)}, u32[]{:S(2)}, u32[]{:S(2)}) %collective-permute-start.2) | collective-permute-done | bytes 819232 | tf_op jit(solution)/shard_map/ppermute | solution.py:73
  93.5 15.2 %collective-permute-done.1 = bf16[256,1600]{0,1:T(8,128)(2,1)} collective-permute-done((bf16[256,1600]{0,1:T(8,128)(2,1)}, bf16[256,1600]{0,1:T(8,128)(2,1)}, u32[]{:S(2)}, u32[]{:S(2)}) %collective-permute-start.1) | collective-permute-done | bytes 819232 | tf_op jit(solution)/shard_map/ppermute | solution.py:73
  111.0 4.3 %fusion.68 = (f32[256]{0:T(256)S(1)}, f32[256,1600]{1,0:T(8,128)}, f32[256]{0:T(256)S(1)}, f32[256,1600]{1,0:T(8,128)}) fusion(f32[8,1600]{1,0:T(8,128)S(1)} %get-tuple-element.53, bf16[256,1600]{1,0:T(8,128)(2,1)} %gather_fusion.7, bf16[256,1600]{1,0:T(8,128)(2,1)} %copy.71, f32[8,1600]{1,0:T(8,128)S(1)} %get-tuple-element.54, ...), kind=kLoop, calls=%fused_computation.222 | loop fusion | flops 4095488 | bytes 6658048 | tf_op jit(solution)/shard_map/reduce_sum | solution.py:13
  125.8 4.8 %gather_fusion.11 = bf16[128,1600]{1,0:T(8,128)(2,1)} fusion(bf16[1280,1600]{1,0:T(8,128)(2,1)} %fusion.10, s32[1024]{0:T(1024)S(1)} %pad_clamp_fusion.1), kind=kCustom, calls=%fused_computation.11 | custom fusion | bytes 819712 | tf_op jit(solution)/shard_map/gather | solution.py:145
  130.7 12.1 %gather_fusion.8 = bf16[1280,1600]{1,0:T(8,128)(2,1)} fusion(bf16[1280,1600]{1,0:T(8,128)(2,1)} %fusion.10, s32[2048]{0:T(1024)S(1)} %pad_clamp_fusion), kind=kCustom, calls=%fused_computation.8 | custom fusion | bytes 8197120 | tf_op jit(solution)/shard_map/gather | solution.py:137
  142.7 4.3 %reshape_reshape.4 = bf16[1600,400]{1,0:T(8,128)(2,1)} reshape(bf16[32,16,1250]{2,1,0:T(8,128)(2,1)} %all-to-all-done.1) | data formatting | bytes 2560000 | tf_op jit(solution)/shard_map/reshape;reshape | solution.py:115
  147.1 4.8 %convolution_convert_fusion = bf16[1280,200]{0,1:T(8,128)(2,1)} fusion(bf16[1280,1600]{1,0:T(8,128)(2,1)} %gather_fusion.8, bf16[1600,400]{1,0:T(8,128)(2,1)} %reshape_reshape.4), kind=kOutput, calls=%fused_computation.12 | convolution fusion | flops 819456000 | bytes 5591040 | tf_op jit(solution)/shard_map/dot_general | solution.py:136
  153.4 2.7 %reshape.895 = bf16[4,320,2,100]{1,0,3,2:T(4,128)(2,1)} reshape(bf16[1280,200]{0,1:T(8,128)(2,1)} %convolution_convert_fusion) | data formatting | bytes 1024000 | tf_op jit(solution)/shard_map/reshape | solution.py:138
  158.5 2.4 %collective-permute-start.3 = (f32[4,32,320]{2,1,0:T(8,128)}, f32[4,32,320]{2,1,0:T(8,128)}, u32[]{:S(2)}, u32[]{:S(2)}) collective-permute-start(f32[4,32,320]{2,1,0:T(8,128)} %fusion.13), channel_id=1, source_target_pairs={{1,0},{2,1},{3,2},{4,3},{5,4},{6,5},{7,6},{8,7},{9,8},{10,9},{11,1... | collective-permute-start | bytes 491528 | tf_op jit(solution)/shard_map/ppermute | solution.py:167
  162.7 2.5 %collective-permute-start.4 = (f32[4,32,320]{2,1,0:T(8,128)}, f32[4,32,320]{2,1,0:T(8,128)}, u32[]{:S(2)}, u32[]{:S(2)}) collective-permute-start(f32[4,32,320]{2,1,0:T(8,128)} %get-tuple-element.69), channel_id=1, source_target_pairs={{0,1},{1,2},{2,3},{3,4},{4,5},{5,6},{6,7},{7,8},{8,9},{9,10},{10,1... | collective-permute-start | bytes 491528 | tf_op jit(solution)/shard_map/ppermute | solution.py:166
  173.2 17.4 %all-to-all-start.2 = ((bf16[16,128,100]{1,2,0:T(8,128)(2,1)}), bf16[16,128,100]{1,2,0:T(8,128)(2,1)}, u32[]{:S(2)}, u32[]{:S(2)}) async-start(bf16[16,128,100]{1,2,0:T(8,128)(2,1)} %fusion), calls=%async_computation.2 | async-start | bytes 851968 | tf_op jit(solution)/shard_map/all_to_all | solution.py:187
  201.2 5.9 %all-to-all-done.2 = bf16[16,128,100]{1,2,0:T(8,128)(2,1)} async-done(((bf16[16,128,100]{1,2,0:T(8,128)(2,1)}), bf16[16,128,100]{1,2,0:T(8,128)(2,1)}, u32[]{:S(2)}, u32[]{:S(2)}) %all-to-all-start.2) | async-done | bytes 409632 | tf_op jit(solution)/shard_map/all_to_all | solution.py:187
  (215 shorter events, 68.0 us)
Async XLA Ops:
  6.4 13.8 %copy-start.20 = (bf16[1600]{0:T(1024)(128)(2,1)S(1)}, bf16[1600]{0:T(1024)(128)(2,1)}, u32[]{:S(2)}) copy-start(bf16[1600]{0:T(1024)(128)(2,1)} %param.11) | copy-start | bytes 9604
  6.4 14.4 %copy-start.15 = (bf16[50,2,100]{2,1,0:T(2,128)(2,1)S(1)}, bf16[50,2,100]{2,1,0:T(2,128)(2,1)}, u32[]{:S(2)}) copy-start(bf16[50,2,100]{2,1,0:T(2,128)(2,1)} %param.13) | copy-start | bytes 60004
  6.4 14.5 %copy-start.16 = (s32[128,32]{0,1:T(8,128)S(1)}, s32[128,32]{0,1:T(8,128)}, u32[]{:S(2)}) copy-start(s32[128,32]{0,1:T(8,128)} %param.17) | copy-start | bytes 49156
  6.4 55.7 %all-to-all-start = ((bf16[32,16,1600]{2,1,0:T(8,128)(2,1)}), bf16[32,16,1600]{2,1,0:T(8,128)(2,1)}, u32[]{:S(2)}, u32[]{:S(2)}) async-start(bf16[32,16,1600]{2,1,0:T(8,128)(2,1)} %broadcast_select_fusion), calls=%async_computation | async-start | bytes 3407872 | tf_op jit(solution)/shard_map/all_to_all | solution.py:64
  40.6 3.4 %copy-start.17 = (bf16[100,50]{0,1:T(8,128)(2,1)S(1)}, bf16[100,50]{0,1:T(8,128)(2,1)}, u32[]{:S(2)}) copy-start(bf16[100,50]{0,1:T(8,128)(2,1)} %param.14) | copy-start | bytes 30004
  40.6 3.4 %copy-start.18 = (bf16[50,100]{1,0:T(8,128)(2,1)S(1)}, bf16[50,100]{1,0:T(8,128)(2,1)}, u32[]{:S(2)}) copy-start(bf16[50,100]{1,0:T(8,128)(2,1)} %param.12) | copy-start | bytes 30004
  42.4 3.3 %copy-start.3 = (f32[256,1600]{1,0:T(8,128)}, f32[256,1600]{1,0:T(8,128)S(1)}, u32[]{:S(2)}) copy-start(f32[256,1600]{1,0:T(8,128)S(1)} %get-tuple-element.52) | copy-start | bytes 4915204
  65.9 11.0 %copy-start.9 = (bf16[256,1600]{1,0:T(8,128)(2,1)}, bf16[256,1600]{1,0:T(8,128)(2,1)S(1)}, u32[]{:S(2)}) copy-start(bf16[256,1600]{1,0:T(8,128)(2,1)S(1)} %gather_fusion.3) | copy-start | bytes 2457604
  67.2 24.1 %collective-permute-start.2 = (bf16[256,1600]{0,1:T(8,128)(2,1)}, bf16[256,1600]{0,1:T(8,128)(2,1)}, u32[]{:S(2)}, u32[]{:S(2)}) collective-permute-start(bf16[256,1600]{0,1:T(8,128)(2,1)} %copy.66), channel_id=1, source_target_pairs={{0,3},{1,2},{2,1},{3,0},{4,7},{5,6},{6,5},{7,4},{8,11},{9,10},{10,... | collective-permute-start | bytes 2457608 | tf_op jit(solution)/shard_map/ppermute | solution.py:73
  71.9 36.8 %collective-permute-start.1 = (bf16[256,1600]{0,1:T(8,128)(2,1)}, bf16[256,1600]{0,1:T(8,128)(2,1)}, u32[]{:S(2)}, u32[]{:S(2)}) collective-permute-start(bf16[256,1600]{0,1:T(8,128)(2,1)} %copy.66), channel_id=1, source_target_pairs={{0,2},{1,3},{2,0},{3,1},{4,6},{5,7},{6,4},{7,5},{8,10},{9,11},{10,... | collective-permute-start | bytes 2457608 | tf_op jit(solution)/shard_map/ppermute | solution.py:73
  74.1 41.2 %collective-permute-start = (bf16[256,1600]{0,1:T(8,128)(2,1)}, bf16[256,1600]{0,1:T(8,128)(2,1)}, u32[]{:S(2)}, u32[]{:S(2)}) collective-permute-start(bf16[256,1600]{0,1:T(8,128)(2,1)} %copy.66), channel_id=1, source_target_pairs={{0,1},{1,0},{2,3},{3,2},{4,5},{5,4},{6,7},{7,6},{8,9},{9,8},{10,11... | collective-permute-start | bytes 2457608 | tf_op jit(solution)/shard_map/ppermute | solution.py:73
  79.9 62.9 %all-to-all-start.1 = ((bf16[32,16,1250]{2,1,0:T(8,128)(2,1)}), bf16[32,16,1250]{2,1,0:T(8,128)(2,1)}, u32[]{:S(2)}, u32[]{:S(2)}) async-start(bf16[32,16,1250]{2,1,0:T(8,128)(2,1)} %broadcast_in_dim.294), calls=%async_computation.1 | async-start | bytes 2621440 | tf_op jit(solution)/shard_map/all_to_all | solution.py:67
  119.4 2.8 %copy-start.2 = (f32[256,1600]{1,0:T(8,128)}, f32[256,1600]{1,0:T(8,128)S(1)}, u32[]{:S(2)}) copy-start(f32[256,1600]{1,0:T(8,128)S(1)} %get-tuple-element.44) | copy-start | bytes 4915204
  147.1 4.8 %copy-start.12 = (bf16[128,1600]{1,0:T(8,128)(2,1)S(1)}, bf16[128,1600]{1,0:T(8,128)(2,1)}, u32[]{:S(2)}) copy-start(bf16[128,1600]{1,0:T(8,128)(2,1)} %gather_fusion.11) | copy-start | bytes 1228804
  151.9 4.3 %copy-start.19 = (pred[4,320]{1,0:T(4,128)(4,1)S(1)}, pred[4,320]{1,0:T(4,128)(4,1)}, u32[]{:S(2)}) copy-start(pred[4,320]{1,0:T(4,128)(4,1)} %iota_compare_fusion.5) | copy-start | bytes 3844
  151.9 5.5 %copy-start.24 = (pred[100]{0:T(512)(128)(4,1)S(1)}, pred[100]{0:T(512)(128)(4,1)}, u32[]{:S(2)}) copy-start(pred[100]{0:T(512)(128)(4,1)} %broadcast_compare_fusion.1) | copy-start | bytes 304
  151.9 6.4 %copy-start.22 = (pred[100]{0:T(512)(128)(4,1)S(1)}, pred[100]{0:T(512)(128)(4,1)}, u32[]{:S(2)}) copy-start(pred[100]{0:T(512)(128)(4,1)} %get-tuple-element.75) | copy-start | bytes 304
  153.4 7.4 %copy-start.21 = (pred[100]{0:T(512)(128)(4,1)S(1)}, pred[100]{0:T(512)(128)(4,1)}, u32[]{:S(2)}) copy-start(pred[100]{0:T(512)(128)(4,1)} %get-tuple-element.76) | copy-start | bytes 304
  157.4 3.5 %copy-start.6 = (bf16[4,320,2,100]{1,3,0,2:T(8,128)(2,1)}, bf16[4,320,2,100]{1,3,0,2:T(8,128)(2,1)S(1)}, u32[]{:S(2)}) copy-start(bf16[4,320,2,100]{1,3,0,2:T(8,128)(2,1)S(1)} %copy_select_fusion) | copy-start | bytes 1536004
  158.5 4.3 %copy-start.10 = (f32[4,32,320]{2,1,0:T(8,128)}, f32[4,32,320]{2,1,0:T(8,128)S(1)}, u32[]{:S(2)}) copy-start(f32[4,32,320]{2,1,0:T(8,128)S(1)} %fusion.12) | copy-start | bytes 491524
  158.5 10.8 %collective-permute-start.3 = (f32[4,32,320]{2,1,0:T(8,128)}, f32[4,32,320]{2,1,0:T(8,128)}, u32[]{:S(2)}, u32[]{:S(2)}) collective-permute-start(f32[4,32,320]{2,1,0:T(8,128)} %fusion.13), channel_id=1, source_target_pairs={{1,0},{2,1},{3,2},{4,3},{5,4},{6,5},{7,6},{8,7},{9,8},{10,9},{11,1... | collective-permute-start | bytes 491528 | tf_op jit(solution)/shard_map/ppermute | solution.py:167
  162.7 6.5 %collective-permute-start.4 = (f32[4,32,320]{2,1,0:T(8,128)}, f32[4,32,320]{2,1,0:T(8,128)}, u32[]{:S(2)}, u32[]{:S(2)}) collective-permute-start(f32[4,32,320]{2,1,0:T(8,128)} %get-tuple-element.69), channel_id=1, source_target_pairs={{0,1},{1,2},{2,3},{3,4},{4,5},{5,6},{6,7},{7,8},{8,9},{9,10},{10,1... | collective-permute-start | bytes 491528 | tf_op jit(solution)/shard_map/ppermute | solution.py:166
  173.2 34.0 %all-to-all-start.2 = ((bf16[16,128,100]{1,2,0:T(8,128)(2,1)}), bf16[16,128,100]{1,2,0:T(8,128)(2,1)}, u32[]{:S(2)}, u32[]{:S(2)}) async-start(bf16[16,128,100]{1,2,0:T(8,128)(2,1)} %fusion), calls=%async_computation.2 | async-start | bytes 851968 | tf_op jit(solution)/shard_map/all_to_all | solution.py:187
  193.0 6.9 %copy-start.8 = (bf16[4,320,2,100]{1,3,0,2:T(8,128)(2,1)S(1)}, bf16[4,320,2,100]{1,3,0,2:T(8,128)(2,1)}, u32[]{:S(2)}) copy-start(bf16[4,320,2,100]{1,3,0,2:T(8,128)(2,1)} %copy-done.6) | copy-start | bytes 1536004
  (9 other events, 17.2 us)
